TPU v7x, 256 devices: a whole 4x4x8 slice. The times are simulated.
256 devices in a mesh: up: 32 (over y, z), down: 8 (over x, core).
Axes of the slice: x: 4, y: 4, z: 8, core: 2. Of those that a mesh axis runs over, the one named last changes fastest.
Arguments:
- amplitudes: float32 [4096, 4096], P('up', 'down'), may hold values from -6 to 6
- double_occ: int32 [4096, 4096], P('up', 'down'), may hold values from 0 to 8
- up_cols: int32 [64, 32], replicated, may hold values from 0 to 63, as said below
- up_ids: int32 [64, 32], replicated, may hold values from 0 to 31, as said below
- up_blocks: bfloat16 [32, 64, 64], replicated, may hold values from -0.125 to 0.125
- down_cols: int32 [64, 32], replicated, may hold values from 0 to 63, as said below
- down_ids: int32 [64, 32], replicated, may hold values from 0 to 31, as said below
- down_blocks: bfloat16 [32, 64, 64], replicated, may hold values from -0.125 to 0.125
Outputs:
- chebyshev: float32 [4096, 4096], P('up', 'down')
Inputs may be any that keep to these rules, and one draw needn't show every extreme that they name: `up_cols`: each row names 32 different blocks. `up_ids`: each row names every shared block exactly once. `down_cols`: each row names 32 different blocks. `down_ids`: each row names every shared block exactly once.
All inputs are finite; a program needn't handle non-finite values.
Results may differ from a plain program's by a relative error of at most 0.0031.
Values may be sent and summed in bfloat16 or wider, within the bound.
No kernel may reach another device: no remote copies, remote signals or barrier semaphores. Data moves between devices by JAX's collectives and lax.ppermute only.
A program may use at most 64 MiB of HBM per device.

v0:
```python
import math

import jax
import jax.numpy as jnp
from jax import lax
from jax.sharding import PartitionSpec as P

coupling = 0.5
center = 2.0
half_span = 2.0


def block_order(block_cols, block_ids, shared_count):
    matched = block_ids[:, :, None] == jnp.arange(shared_count, dtype=jnp.int32)[None, None, :]
    return jnp.sum(jnp.where(matched, block_cols[:, :, None], 0), axis=1)


def hop_strings(values, by_shared, shared_table):
    row_count = values.shape[0]
    shared_count = shared_table.shape[0]
    block_width = shared_table.shape[1]
    block_total = values.shape[1] // block_width
    out_blocks = by_shared.shape[0]
    pieces = values.reshape(row_count, block_total, block_width)
    flat_table = shared_table.reshape(shared_count * block_width, block_width)
    group_size = math.gcd(8, out_blocks)

    def one_group(step_index, result):
        chosen = lax.dynamic_slice_in_dim(
            by_shared, step_index * group_size, group_size, 0
        ).reshape(-1)
        taken_rows = jnp.take(pieces, chosen, axis=1).reshape(
            row_count * group_size, shared_count * block_width
        )
        block_out = jnp.dot(taken_rows, flat_table, preferred_element_type=jnp.float32)
        block_out = block_out.reshape(row_count, group_size * block_width)
        return lax.dynamic_update_slice_in_dim(
            result, block_out, step_index * group_size * block_width, 1
        )

    result = jnp.zeros((row_count, out_blocks * block_width), jnp.float32)
    return lax.fori_loop(0, out_blocks // group_size, one_group, result)


def body(amplitudes, double_occ, up_cols, up_ids, up_blocks, down_cols, down_ids, down_blocks):
    shared_count = up_blocks.shape[0]
    block_width = up_blocks.shape[1]
    local_rows, local_cols = amplitudes.shape
    up_count = lax.axis_size("up")
    up_order = block_order(up_cols, up_ids, shared_count)
    down_order = block_order(down_cols, down_ids, shared_count)
    onsite = coupling * double_occ.astype(jnp.float32) - center

    def apply_up(items):
        return hop_strings(items[0], up_order, up_blocks)[None]

    def up_part(rounded):
        sectioned = rounded.T.reshape(up_count, local_cols // up_count, local_rows)
        exchanged = apply_up(
            lax.all_to_all(sectioned, "up", split_axis=0, concat_axis=2, tiled=True)
        )
        returned = lax.all_to_all(exchanged, "up", split_axis=2, concat_axis=0, tiled=True)
        return returned.reshape(local_cols, local_rows).T

    def down_part(rounded):
        gathered = lax.all_gather(rounded, "down", axis=1, tiled=True)
        own_blocks = local_cols // block_width
        own_order = lax.dynamic_slice_in_dim(
            down_order, lax.axis_index("down") * own_blocks, own_blocks, 0
        )
        return hop_strings(gathered, own_order, down_blocks)

    def apply_scaled(current):
        rounded = current.astype(jnp.bfloat16)
        return (onsite * current + up_part(rounded) + down_part(rounded)) / half_span

    first = apply_scaled(amplitudes)
    return 2.0 * apply_scaled(first) - amplitudes


def solution(mesh):
    placed = (P("up", "down"), P("up", "down"), P(), P(), P(), P(), P(), P())
    return jax.shard_map(
        body, mesh=mesh, in_specs=placed, out_specs=P("up", "down"), check_vma=False
    )
```

profile of v0, /device:TPU:32, one launch (start us, length us, event | category | flops | bytes accessed | tf_op | source)
XLA Modules:
  0.0 286.4 jit_solution(3535279625799799941)
XLA Ops:
  6.5 1.1 copy.122
  8.4 11.4 %all-to-all-start = ((bf16[32,16,128]{2,1,0:T(8,128)(2,1)}), bf16[32,16,128]{2,1,0:T(8,128)(2,1)S(1)}, u32[]{:S(2)}, u32[]{:S(2)}) async-start(bf16[32,16,128]{2,1,0:T(8,128)(2,1)} %bitcast.89), calls=%async_computation | async-start | bytes 262144 | tf_op jit(solution)/shard_map/all_to_all | solution.py:60
  21.7 1.1 copy.121
  22.8 6.7 %all-to-all-done = bf16[32,16,128]{2,1,0:T(8,128)(2,1)S(1)} async-done(((bf16[32,16,128]{2,1,0:T(8,128)(2,1)}), bf16[32,16,128]{2,1,0:T(8,128)(2,1)S(1)}, u32[]{:S(2)}, u32[]{:S(2)}) %all-to-all-start) | async-done | bytes 131104 | tf_op jit(solution)/shard_map/all_to_all | solution.py:60
  30.6 31.8 %while.40 = (s32[]{:T(128)}, f32[16,4096]{1,0:T(8,128)}, s32[64,32]{1,0:T(8,128)S(1)}, bf16[16,64,64]{2,0,1:T(8,128)(2,1)S(1)}, bf16[2048,64]{1,0:T(8,128)(2,1)}...) while((s32[]{:T(128)}, f32[16,4096]{1,0:T(8,128)}, ...), condition=%wide.region_2.4_spmd, body=%wide.region_1.0_spmd.sunk | while | flops 33819908 | bytes 6207213 | solution.py:42
  31.6 0.9 select_bitcast_fusion.6
  35.6 0.9 select_bitcast_fusion.6
  39.5 0.9 select_bitcast_fusion.6
  43.5 0.9 select_bitcast_fusion.6
  47.5 0.9 select_bitcast_fusion.6
  51.5 0.9 select_bitcast_fusion.6
  55.5 0.9 select_bitcast_fusion.6
  59.4 0.9 select_bitcast_fusion.6
  62.5 1.5 copy.127
  64.6 19.4 %reduce = f32[4096,16]{1,0:T(8,128)} reduce(f32[4096,1,16]{2,1,0:T(1,128)S(1)} %bitcast.87, f32[]{:T(128)} %broadcast.71), dimensions={1}, to_apply=%bitcast.56.reduce_sub_computation | reduce | bytes 524292
  84.0 3.0 %reshape.183 = f32[32,1,2048]{2,1,0:T(1,128)} reshape(f32[4096,16]{1,0:T(8,128)} %reduce) | data formatting | bytes 524288
  87.0 4.3 %all-to-all-start.1 = ((f32[32,1,2048]{2,1,0:T(1,128)}), f32[32,1,2048]{2,1,0:T(1,128)S(1)}, u32[]{:S(2)}, u32[]{:S(2)}) async-start(f32[32,1,2048]{2,1,0:T(1,128)} %reshape.183), calls=%async_computation.1 | async-start | bytes 524288 | tf_op jit(solution)/shard_map/all_to_all | solution.py:62
  91.3 11.2 %all-to-all-done.1 = f32[32,1,2048]{2,1,0:T(1,128)S(1)} async-done(((f32[32,1,2048]{2,1,0:T(1,128)}), f32[32,1,2048]{2,1,0:T(1,128)S(1)}, u32[]{:S(2)}, u32[]{:S(2)}) %all-to-all-start.1) | async-done | bytes 262176 | tf_op jit(solution)/shard_map/all_to_all | solution.py:62
  102.5 1.3 reduce.1
  103.8 3.9 %reshape.184 = f32[4096,1,16]{2,1,0:T(1,128)S(1)} reshape(f32[32,2048]{1,0:T(8,128)S(1)} %reduce.1) | data formatting | bytes 524288
  107.8 2.1 copy.128
  110.1 4.3 %gather_fusion.2 = bf16[256,128,64]{1,2,0:T(8,128)(2,1)} fusion(bf16[128,64,64]{0,2,1:T(8,128)(2,1)} %bitcast.82, s32[1024]{0:T(1024)S(1)} %pad_clamp_fusion.2), kind=kCustom, calls=%fused_computation.1.clone | custom fusion | bytes 8389632 | tf_op jit(solution)/shard_map/while/body/eval_jaxpr/jit(_take)/gather | solution.py:32
  114.4 4.0 %select_bitcast_fusion.3 = bf16[128,256,64]{0,2,1:T(8,128)(2,1)} fusion(bf16[256,128,64]{1,2,0:T(8,128)(2,1)} %gather_fusion.2, pred[256]{0:T(512)(128)(4,1)S(1)} %compare_and_fusion.2), kind=kLoop, calls=%fused_computation.17 | loop fusion | flops 2097152 | bytes 8388864 | tf_op jit(solution)/shard_map/while/body/eval_jaxpr/jit(_take)/select_n | solution.py:32
  118.4 12.9 %copy.131 = bf16[128,256,64]{2,1,0:T(8,128)(2,1)} copy(bf16[128,256,64]{0,2,1:T(8,128)(2,1)} %select_bitcast_fusion.3) | data formatting | bytes 8388608 | tf_op jit(solution)/shard_map/while/body/eval_jaxpr/jit(_take)/select_n | solution.py:32
  131.3 12.3 %reshape.131 = bf16[1024,2048]{1,0:T(8,128)(2,1)} reshape(bf16[128,256,64]{2,1,0:T(8,128)(2,1)} %copy.131) | data formatting | bytes 8388608 | tf_op jit(solution)/shard_map/while/body/eval_jaxpr/reshape | solution.py:32
  143.6 3.5 %fusion.7 = f32[1024,64]{1,0:T(8,128)S(1)} fusion(bf16[1024,2048]{1,0:T(8,128)(2,1)} %reshape.131, bf16[2048,64]{1,0:T(8,128)(2,1)S(1)} %bitcast.80), kind=kOutput, calls=%fused_computation.36 | convolution fusion | flops 268435456 | bytes 4718592 | tf_op jit(solution)/shard_map/while/body/eval_jaxpr/dot_general | solution.py:35
  148.2 4.5 %all-to-all-start.2 = ((bf16[32,16,128]{2,1,0:T(8,128)(2,1)}), bf16[32,16,128]{2,1,0:T(8,128)(2,1)S(1)}, u32[]{:S(2)}, u32[]{:S(2)}) async-start(bf16[32,16,128]{2,1,0:T(8,128)(2,1)} %bitcast.16), calls=%async_computation.2 | async-start | bytes 262144 | tf_op jit(solution)/shard_map/all_to_all | solution.py:60
  153.5 8.9 %all-to-all-done.2 = bf16[32,16,128]{2,1,0:T(8,128)(2,1)S(1)} async-done(((bf16[32,16,128]{2,1,0:T(8,128)(2,1)}), bf16[32,16,128]{2,1,0:T(8,128)(2,1)S(1)}, u32[]{:S(2)}, u32[]{:S(2)}) %all-to-all-start.2) | async-done | bytes 131104 | tf_op jit(solution)/shard_map/all_to_all | solution.py:60
  163.5 31.7 %while.41 = (s32[]{:T(128)}, f32[16,4096]{1,0:T(8,128)}, s32[64,32]{1,0:T(8,128)S(1)}, bf16[16,64,64]{2,0,1:T(8,128)(2,1)S(1)}, bf16[2048,64]{1,0:T(8,128)(2,1)S...) while((s32[]{:T(128)}, f32[16,4096]{1,0:T(8,128)}, ...), condition=%wide.region_5.8_spmd, body=%wide.region_4.7_spmd.sunk | while | flops 33819908 | bytes 5158609 | solution.py:42
  164.4 0.9 select_bitcast_fusion.7
  168.4 0.9 select_bitcast_fusion.7
  172.4 0.9 select_bitcast_fusion.7
  176.3 0.9 select_bitcast_fusion.7
  180.3 0.9 select_bitcast_fusion.7
  184.3 0.9 select_bitcast_fusion.7
  188.2 0.9 select_bitcast_fusion.7
  195.2 1.5 copy.137
  196.8 19.4 %reduce.2 = f32[4096,16]{1,0:T(8,128)} reduce(f32[4096,1,16]{2,1,0:T(1,128)S(1)} %bitcast.88, f32[]{:T(128)} %broadcast.71), dimensions={1}, to_apply=%bitcast.58.reduce_sub_computation | reduce | bytes 524292
  216.2 2.4 reshape.185
  218.6 15.2 %all_to_all.60 = f32[32,1,2048]{2,1,0:T(1,128)S(1)} all-to-all(f32[32,1,2048]{2,1,0:T(1,128)S(1)} %reshape.185), channel_id=1, replica_groups=mesh['up'=32,'down'=8] {'up'}, dimensions={0} | all-to-all | bytes 524288 | tf_op jit(solution)/shard_map/all_to_all | solution.py:62
  233.8 1.3 reduce.3
  235.1 3.9 %reshape.186 = f32[4096,1,16]{2,1,0:T(1,128)S(1)} reshape(f32[32,2048]{1,0:T(8,128)S(1)} %reduce.3) | data formatting | bytes 524288
  239.1 2.1 copy.138
  241.3 4.3 %gather_fusion.3 = bf16[256,128,64]{1,2,0:T(8,128)(2,1)} fusion(bf16[128,64,64]{0,2,1:T(8,128)(2,1)} %bitcast.83, s32[1024]{0:T(1024)S(1)} %pad_clamp_fusion.2), kind=kCustom, calls=%fused_computation.3.clone | custom fusion | bytes 8389632 | tf_op jit(solution)/shard_map/while/body/eval_jaxpr/jit(_take)/gather | solution.py:32
  245.6 4.0 %select_bitcast_fusion.2 = bf16[128,256,64]{0,2,1:T(8,128)(2,1)} fusion(bf16[256,128,64]{1,2,0:T(8,128)(2,1)} %gather_fusion.3, pred[256]{0:T(512)(128)(4,1)S(1)} %compare_and_fusion.2), kind=kLoop, calls=%fused_computation.16 | loop fusion | flops 2097152 | bytes 8388864 | tf_op jit(solution)/shard_map/while/body/eval_jaxpr/jit(_take)/select_n | solution.py:32
  249.6 12.9 %copy.140 = bf16[128,256,64]{2,1,0:T(8,128)(2,1)} copy(bf16[128,256,64]{0,2,1:T(8,128)(2,1)} %select_bitcast_fusion.2) | data formatting | bytes 8388608 | tf_op jit(solution)/shard_map/while/body/eval_jaxpr/jit(_take)/select_n | solution.py:32
  262.5 12.3 %reshape.137 = bf16[1024,2048]{1,0:T(8,128)(2,1)} reshape(bf16[128,256,64]{2,1,0:T(8,128)(2,1)} %copy.140) | data formatting | bytes 8388608 | tf_op jit(solution)/shard_map/while/body/eval_jaxpr/reshape | solution.py:32
  274.8 3.5 %fusion.8 = f32[1024,64]{1,0:T(8,128)S(1)} fusion(bf16[1024,2048]{1,0:T(8,128)(2,1)} %reshape.137, bf16[2048,64]{1,0:T(8,128)(2,1)S(1)} %bitcast.81), kind=kOutput, calls=%fused_computation.37 | convolution fusion | flops 268435456 | bytes 4718592 | tf_op jit(solution)/shard_map/while/body/eval_jaxpr/dot_general | solution.py:35
  (239 shorter events, 57.8 us)
Async XLA Ops:
  6.5 137.1 %copy-start = (bf16[32,64,64]{2,1,0:T(8,128)(2,1)S(1)}, bf16[32,64,64]{2,1,0:T(8,128)(2,1)}, u32[]{:S(2)}) copy-start(bf16[32,64,64]{2,1,0:T(8,128)(2,1)} %param.23) | copy-start | bytes 786436
  6.5 103.5 %all-gather.3.cloned.1.call-start = ((), (), s32[]{:S(2)}) async-start(), calls=%async_computation.4 | async-start | bytes 1179648 | tf_op jit(solution)/shard_map/all_gather | solution.py:66
  8.4 21.2 %all-to-all-start = ((bf16[32,16,128]{2,1,0:T(8,128)(2,1)}), bf16[32,16,128]{2,1,0:T(8,128)(2,1)S(1)}, u32[]{:S(2)}, u32[]{:S(2)}) async-start(bf16[32,16,128]{2,1,0:T(8,128)(2,1)} %bitcast.89), calls=%async_computation | async-start | bytes 262144 | tf_op jit(solution)/shard_map/all_to_all | solution.py:60
  30.6 3.0 %copy-start.1 = (bf16[2048,64]{1,0:T(8,128)(2,1)S(1)}, bf16[2048,64]{1,0:T(8,128)(2,1)}, u32[]{:S(2)}) copy-start(bf16[2048,64]{1,0:T(8,128)(2,1)} %get-tuple-element.457) | copy-start | bytes 786436 | tf_op jit(solution)/shard_map/while
  34.6 3.0 %copy-start.1 = (bf16[2048,64]{1,0:T(8,128)(2,1)S(1)}, bf16[2048,64]{1,0:T(8,128)(2,1)}, u32[]{:S(2)}) copy-start(bf16[2048,64]{1,0:T(8,128)(2,1)} %get-tuple-element.457) | copy-start | bytes 786436 | tf_op jit(solution)/shard_map/while
  38.6 3.0 %copy-start.1 = (bf16[2048,64]{1,0:T(8,128)(2,1)S(1)}, bf16[2048,64]{1,0:T(8,128)(2,1)}, u32[]{:S(2)}) copy-start(bf16[2048,64]{1,0:T(8,128)(2,1)} %get-tuple-element.457) | copy-start | bytes 786436 | tf_op jit(solution)/shard_map/while
  42.5 3.0 %copy-start.1 = (bf16[2048,64]{1,0:T(8,128)(2,1)S(1)}, bf16[2048,64]{1,0:T(8,128)(2,1)}, u32[]{:S(2)}) copy-start(bf16[2048,64]{1,0:T(8,128)(2,1)} %get-tuple-element.457) | copy-start | bytes 786436 | tf_op jit(solution)/shard_map/while
  46.5 3.0 %copy-start.1 = (bf16[2048,64]{1,0:T(8,128)(2,1)S(1)}, bf16[2048,64]{1,0:T(8,128)(2,1)}, u32[]{:S(2)}) copy-start(bf16[2048,64]{1,0:T(8,128)(2,1)} %get-tuple-element.457) | copy-start | bytes 786436 | tf_op jit(solution)/shard_map/while
  50.5 3.0 %copy-start.1 = (bf16[2048,64]{1,0:T(8,128)(2,1)S(1)}, bf16[2048,64]{1,0:T(8,128)(2,1)}, u32[]{:S(2)}) copy-start(bf16[2048,64]{1,0:T(8,128)(2,1)} %get-tuple-element.457) | copy-start | bytes 786436 | tf_op jit(solution)/shard_map/while
  54.5 3.0 %copy-start.1 = (bf16[2048,64]{1,0:T(8,128)(2,1)S(1)}, bf16[2048,64]{1,0:T(8,128)(2,1)}, u32[]{:S(2)}) copy-start(bf16[2048,64]{1,0:T(8,128)(2,1)} %get-tuple-element.457) | copy-start | bytes 786436 | tf_op jit(solution)/shard_map/while
  58.5 3.0 %copy-start.1 = (bf16[2048,64]{1,0:T(8,128)(2,1)S(1)}, bf16[2048,64]{1,0:T(8,128)(2,1)}, u32[]{:S(2)}) copy-start(bf16[2048,64]{1,0:T(8,128)(2,1)} %get-tuple-element.457) | copy-start | bytes 786436 | tf_op jit(solution)/shard_map/while
  87.0 15.5 %all-to-all-start.1 = ((f32[32,1,2048]{2,1,0:T(1,128)}), f32[32,1,2048]{2,1,0:T(1,128)S(1)}, u32[]{:S(2)}, u32[]{:S(2)}) async-start(f32[32,1,2048]{2,1,0:T(1,128)} %reshape.183), calls=%async_computation.1 | async-start | bytes 524288 | tf_op jit(solution)/shard_map/all_to_all | solution.py:62
  110.0 37.4 %copy-start.3 = (f32[32,1,16,128]{3,2,0,1:T(8,128)}, f32[32,1,16,128]{3,2,0,1:T(8,128)S(1)}, u32[]{:S(2)}) copy-start(f32[32,1,16,128]{3,2,0,1:T(8,128)S(1)} %copy.129) | copy-start | bytes 786436
  143.6 19.9 %copy-start.2 = (bf16[2048,64]{1,0:T(8,128)(2,1)S(1)}, bf16[2048,64]{1,0:T(8,128)(2,1)}, u32[]{:S(2)}) copy-start(bf16[2048,64]{1,0:T(8,128)(2,1)} %get-tuple-element.501) | copy-start | bytes 786436
  147.4 15.0 %copy-start.5 = (f32[128,512]{0,1:T(8,128)}, f32[128,512]{0,1:T(8,128)S(1)}, u32[]{:S(2)}) copy-start(f32[128,512]{0,1:T(8,128)S(1)} %copy.133) | copy-start | bytes 786436
  148.2 14.2 %all-to-all-start.2 = ((bf16[32,16,128]{2,1,0:T(8,128)(2,1)}), bf16[32,16,128]{2,1,0:T(8,128)(2,1)S(1)}, u32[]{:S(2)}, u32[]{:S(2)}) async-start(bf16[32,16,128]{2,1,0:T(8,128)(2,1)} %bitcast.16), calls=%async_computation.2 | async-start | bytes 262144 | tf_op jit(solution)/shard_map/all_to_all | solution.py:60
  152.7 88.6 %all-gather.5.cloned.1.call-start = ((), (), s32[]{:S(2)}) async-start(), calls=%async_computation.5 | async-start | bytes 1179648 | tf_op jit(solution)/shard_map/all_gather | solution.py:66
  274.8 3.8 %copy-start.4 = (f32[32,1,16,128]{3,2,0,1:T(8,128)S(1)}, f32[32,1,16,128]{3,2,0,1:T(8,128)}, u32[]{:S(2)}) copy-start(f32[32,1,16,128]{3,2,0,1:T(8,128)} %copy-done.3) | copy-start | bytes 786436
  274.8 3.8 %copy-start.6 = (f32[128,512]{0,1:T(8,128)S(1)}, f32[128,512]{0,1:T(8,128)}, u32[]{:S(2)}) copy-start(f32[128,512]{0,1:T(8,128)} %copy-done.5) | copy-start | bytes 786436
Sparse Core Ops, SparseCore 0:
  9.2 28.3 all-gather.2
  155.4 26.7 all-gather.4
where the time goes:
time: 288 us; the launch traced here: 286 us
  local copies, waits for them, and re-layouts  130 us (45%)
  other arithmetic  67.7 us (24%)
  waiting for transfers between devices  27.4 us (10%)
  starting transfers between devices  20.4 us (7%)
  blocking collectives  15.2 us (5%)
  between operations  13.7 us (5%)
  matrix products  11.6 us (4%)
    unnamed x2, other arithmetic  38.8 us
    reshape x18, local copies, waits for them, and re-layouts, one_group(): jnp.take(pieces, chosen, axis=1)  37.4 us
    select_n x18, local copies, waits for them, and re-layouts, one_group(): jnp.take(pieces, chosen, axis=1)  30.1 us
    select_n x35, other arithmetic, one_group(): jnp.take(pieces, chosen, axis=1)  22.9 us
    gather x18, local copies, waits for them, and re-layouts, one_group(): jnp.take(pieces, chosen, axis=1)  22.1 us
    unnamed x19, local copies, waits for them, and re-layouts  16.1 us
    all_to_all x2, starting transfers between devices, up_part(): lax.all_to_all(sectioned, 'up', split_axis=0, concat_axis=2, tiled=True)  15.9 us
    all_to_all x2, waiting for transfers between devices, up_part(): lax.all_to_all(sectioned, 'up', split_axis=0, concat_axis=2, tiled=True)  15.6 us
  transfers between devices with their start and end apart: 5, of which 3 were waited for; matrix products, arithmetic and copies ran while one was open for 46% of the time, Pallas kernels for 0%

commit v1 on v0

v1 whole, which is shorter than its diff:
```python
import jax
import jax.numpy as jnp
from jax import lax
from jax.experimental import pallas as pl
from jax.experimental.pallas import tpu as pltpu
from jax.sharding import PartitionSpec as P

coupling = 0.5
center = 2.0
half_span = 2.0

LANES = 128


def block_order(block_cols, block_ids, shared_count):
    matched = block_ids[:, :, None] == jnp.arange(shared_count, dtype=jnp.int32)[None, None, :]
    return jnp.sum(jnp.where(matched, block_cols[:, :, None], 0), axis=1)


def doubled_table(shared_table):
    shared_count, block_width, _ = shared_table.shape
    wide = jnp.broadcast_to(shared_table[:, None], (shared_count, 2, block_width, block_width))
    return wide.reshape(shared_count * 2 * block_width, block_width)


def _stage_row(idx_ref, base, src_ref, stage_ref, row0, rows, shared_count, half_of_lane):
    for s in range(shared_count):
        c = idx_ref[base + s]
        piece = src_ref[lax.shift_right_logical(c, 1)]
        keep = half_of_lane == (c & 1)
        stage_ref[row0:row0 + rows, s * LANES:(s + 1) * LANES] = jnp.where(
            keep, piece, jnp.zeros_like(piece)
        )


def up_kernel(idx_ref, x_ref, w_ref, o_ref, stage_ref):
    pairs, n, _ = x_ref.shape
    block_width = w_ref.shape[1]
    shared_count = w_ref.shape[0] // LANES
    rows_per_chunk = stage_ref.shape[0] // n
    half_of_lane = jnp.where(
        lax.broadcasted_iota(jnp.int32, (n, LANES), 1) >= block_width, 1, 0
    )

    def chunk(g, carry):
        for rr in range(rows_per_chunk):
            r = g * rows_per_chunk + rr
            _stage_row(idx_ref, r * shared_count, x_ref, stage_ref, rr * n, n,
                       shared_count, half_of_lane)
        res = jnp.dot(stage_ref[...], w_ref[...], preferred_element_type=jnp.float32)
        for rr in range(0, rows_per_chunk, 2):
            i = (g * rows_per_chunk + rr) // 2
            o_ref[i, :, 0:block_width] = res[rr * n:(rr + 1) * n]
            o_ref[i, :, block_width:2 * block_width] = res[(rr + 1) * n:(rr + 2) * n]
        return carry

    lax.fori_loop(0, 2 * pairs // rows_per_chunk, chunk, 0)


def down_kernel(idx_ref, g_ref, w_ref, o_ref, stage_ref):
    _, rows, _ = g_ref.shape
    block_width = w_ref.shape[1]
    shared_count = w_ref.shape[0] // LANES
    own_blocks = o_ref.shape[1] // block_width
    half_of_lane = jnp.where(
        lax.broadcasted_iota(jnp.int32, (rows, LANES), 1) >= block_width, 1, 0
    )
    for r in range(own_blocks):
        _stage_row(idx_ref, r * shared_count, g_ref, stage_ref, 0, rows,
                   shared_count, half_of_lane)
        o_ref[:, r * block_width:(r + 1) * block_width] = jnp.dot(
            stage_ref[...], w_ref[...], preferred_element_type=jnp.float32
        )


def up_hop(idx, x, w):
    pairs, n, _ = x.shape
    rows_per_chunk = 8
    return pl.pallas_call(
        up_kernel,
        out_shape=jax.ShapeDtypeStruct((pairs, n, LANES), jnp.float32),
        in_specs=[
            pl.BlockSpec(memory_space=pltpu.SMEM),
            pl.BlockSpec(memory_space=pltpu.VMEM),
            pl.BlockSpec(memory_space=pltpu.VMEM),
        ],
        out_specs=pl.BlockSpec(memory_space=pltpu.VMEM),
        scratch_shapes=[pltpu.VMEM((rows_per_chunk * n, w.shape[0]), jnp.bfloat16)],
    )(idx, x, w)


def down_hop(idx, g, w, own_cols):
    _, rows, _ = g.shape
    return pl.pallas_call(
        down_kernel,
        out_shape=jax.ShapeDtypeStruct((rows, own_cols), jnp.float32),
        in_specs=[
            pl.BlockSpec(memory_space=pltpu.SMEM),
            pl.BlockSpec(memory_space=pltpu.VMEM),
            pl.BlockSpec(memory_space=pltpu.VMEM),
        ],
        out_specs=pl.BlockSpec(memory_space=pltpu.VMEM),
        scratch_shapes=[pltpu.VMEM((rows, w.shape[0]), jnp.bfloat16)],
    )(idx, g, w)


def body(amplitudes, double_occ, up_cols, up_ids, up_blocks, down_cols, down_ids, down_blocks):
    shared_count = up_blocks.shape[0]
    block_width = up_blocks.shape[1]
    local_rows, local_cols = amplitudes.shape
    up_count = lax.axis_size("up")
    own_blocks = local_cols // block_width
    up_idx = block_order(up_cols, up_ids, shared_count).reshape(-1)
    down_order = block_order(down_cols, down_ids, shared_count)
    down_idx = lax.dynamic_slice_in_dim(
        down_order, lax.axis_index("down") * own_blocks, own_blocks, 0
    ).reshape(-1)
    up_table = doubled_table(up_blocks)
    down_table = doubled_table(down_blocks)
    onsite = coupling * double_occ.astype(jnp.float32) - center

    def up_part(rounded):
        sectioned = rounded.T.reshape(up_count, local_cols // up_count, local_rows)
        received = lax.all_to_all(sectioned, "up", 0, 0, tiled=True)
        hopped = up_hop(up_idx, received, up_table)
        returned = lax.all_to_all(hopped, "up", 0, 0, tiled=True)
        return returned.reshape(local_cols, local_rows).T

    def down_part(rounded):
        paired = rounded.reshape(local_rows, local_cols // LANES, LANES).transpose(1, 0, 2)
        gathered = lax.all_gather(paired, "down", axis=0, tiled=True)
        return down_hop(down_idx, gathered, down_table, local_cols)

    def apply_scaled(current):
        rounded = current.astype(jnp.bfloat16)
        return (onsite * current + up_part(rounded) + down_part(rounded)) / half_span

    first = apply_scaled(amplitudes)
    return 2.0 * apply_scaled(first) - amplitudes


def solution(mesh):
    placed = (P("up", "down"), P("up", "down"), P(), P(), P(), P(), P(), P())
    return jax.shard_map(
        body, mesh=mesh, in_specs=placed, out_specs=P("up", "down"), check_vma=False
    )
```

time: 288 us -> 120 us (0.42)
  local copies, waits for them, and re-layouts: 130 us -> 8.84 us
  other arithmetic: 67.7 us -> 3.08 us
  Pallas kernels: 0 us -> 29.1 us
  blocking collectives: 15.2 us -> 29.8 us
  matrix products: 11.6 us -> 0 us
  waiting for transfers between devices: 27.4 us -> 19.3 us
  starting transfers between devices: 20.4 us -> 15.8 us
    reshape x55 -> x4, local copies, waits for them, and re-layouts: 40.6 us -> 1.58 us  [the longest x1 0.67 us: body(): up_idx = block_order(up_cols, up_ids, shared_count).reshape(-1)]
    unnamed x2 -> x0, other arithmetic: 38.8 us -> none
    select_n x18 -> x0, local copies, waits for them, and re-layouts: 30.1 us -> none  [one_group(): jnp.take(pieces, chosen, axis=1)]
    pallas_call x0 -> x4, Pallas kernels: none -> 29.1 us  [the longest x2 17.6 us: up_hop(): pl.pallas_call(up_kernel, out_shape=jax.ShapeDtypeStruct((pairs, n, LANES...]
    select_n x35 -> x0, other arithmetic: 22.9 us -> none  [one_group(): jnp.take(pieces, chosen, axis=1)]
    gather x18 -> x0, local copies, waits for them, and re-layouts: 22.1 us -> none  [one_group(): jnp.take(pieces, chosen, axis=1)]
    all_to_all x1 -> x2, blocking collectives: 15.2 us -> 29.8 us  [the longest x1 15.6 us: up_part(): returned = lax.all_to_all(hopped, 'up', 0, 0, tiled=True)]
    unnamed x19 -> x21, local copies, waits for them, and re-layouts: 16.1 us -> 1.81 us
  transfers between devices with their start and end apart: 5 -> 4, of which waited for: 3 -> 2; matrix products, arithmetic and copies ran while one was open for 46% -> 3% of each run, Pallas kernels for 0% -> 15%
where the time goes in v1:
time: 120 us; the launch traced here: 119 us
  blocking collectives  29.8 us (25%)
  Pallas kernels  29.1 us (24%)
  waiting for transfers between devices  19.3 us (16%)
  starting transfers between devices  15.8 us (13%)
  between operations  13.5 us (11%)
  local copies, waits for them, and re-layouts  8.84 us (7%)
  other arithmetic  3.08 us (3%)
    pallas_call x2, Pallas kernels, up_hop(): pl.pallas_call(up_kernel, out_shape=jax.ShapeDtypeStruct((pairs, n, LANES...  17.6 us
    all_to_all x1, blocking collectives, up_part(): returned = lax.all_to_all(hopped, 'up', 0, 0, tiled=True)  15.6 us
    all_to_all x1, blocking collectives, up_part(): received = lax.all_to_all(sectioned, 'up', 0, 0, tiled=True)  14.1 us
    pallas_call x2, Pallas kernels, down_hop(): pl.pallas_call(down_kernel, out_shape=jax.ShapeDtypeStruct((rows, own_col...  11.6 us
    all_to_all x1, starting transfers between devices, up_part(): received = lax.all_to_all(sectioned, 'up', 0, 0, tiled=True)  11.4 us
    all_to_all x1, waiting for transfers between devices, up_part(): returned = lax.all_to_all(hopped, 'up', 0, 0, tiled=True)  10.3 us
    all_to_all x1, waiting for transfers between devices, up_part(): received = lax.all_to_all(sectioned, 'up', 0, 0, tiled=True)  8.91 us
    all_to_all x1, starting transfers between devices, up_part(): returned = lax.all_to_all(hopped, 'up', 0, 0, tiled=True)  4.41 us
  transfers between devices with their start and end apart: 4, of which 2 were waited for; matrix products, arithmetic and copies ran while one was open for 3% of the time, Pallas kernels for 15%

profile of v1, /device:TPU:32, one launch (start us, length us, event | category | flops | bytes accessed | tf_op | source)
XLA Modules:
  0.0 119.4 jit_solution(14812809131475754021)
XLA Ops:
  6.5 0.0 copy-start.3
  6.5 0.0 all-gather.3.cloned.1.call-start
  6.5 1.8 %copy.48 = bf16[128,512]{0,1:T(8,128)(2,1)} copy(f32[128,512]{1,0:T(8,128)} %param.8) | data formatting | bytes 393216 | tf_op args[0]
  8.3 1.7 %copy.51 = bf16[4,128,128]{2,1,0:T(8,128)(2,1)} copy(bf16[4,128,128]{1,2,0:T(8,128)(2,1)} %bitcast.6) | data formatting | bytes 262144 | tf_op jit(solution)/shard_map/transpose | solution.py:130
  10.0 0.0 all-gather.3.cloned.1.call-update
  10.0 0.0 copy-start.6
  10.0 0.0 copy-start.7
  10.0 11.4 %all-to-all-start = ((bf16[32,16,128]{2,1,0:T(8,128)(2,1)}), bf16[32,16,128]{2,1,0:T(8,128)(2,1)S(1)}, u32[]{:S(2)}, u32[]{:S(2)}) async-start(bf16[32,16,128]{2,1,0:T(8,128)(2,1)} %bitcast.1), calls=%async_computation | async-start | bytes 262144 | tf_op jit(solution)/shard_map/all_to_all | solution.py:124
  21.4 0.0 copy-done.6
  21.4 0.0 copy-done.7
  21.4 0.1 select_reduce_fusion.1
  21.5 0.1 copy.47
  21.6 0.7 reshape.36.idx_ref
  22.3 8.9 %all-to-all-done.x_ref = bf16[32,16,128]{2,1,0:T(8,128)(2,1)S(1)} async-done(((bf16[32,16,128]{2,1,0:T(8,128)(2,1)}), bf16[32,16,128]{2,1,0:T(8,128)(2,1)S(1)}, u32[]{:S(2)}, u32[]{:S(2)}) %all-to-all-start) | async-done | bytes 131104 | tf_op jit(solution)/shard_map/all_to_all | solution.py:124
  31.2 0.0 copy-done.3
  31.2 1.3 %broadcast_in_dim.38 = bf16[32,2,64,64]{3,2,1,0:T(8,128)(2,1)} broadcast(bf16[32,64,64]{2,1,0:T(8,128)(2,1)S(1)} %copy-done.3), dimensions={0,2,3} | broadcast | bytes 786432 | tf_op jit(solution)/shard_map/broadcast_in_dim | solution.py:22
  32.5 0.0 copy-done.5
  32.5 8.8 %shard_map.82 = f32[32,16,128]{2,1,0:T(8,128)} custom-call(s32[2048]{0:T(1024)} %reshape.36.idx_ref, bf16[32,16,128]{2,1,0:T(8,128)(2,1)} %copy-done.5, bf16[4096,64]{1,0:T(8,128)(2,1)} %bitcast.31), custom_call_target="tpu_custom_call" | custom-call | tf_op jit(solution)/shard_map/pallas_call | solution.py:79
  41.3 4.4 %all-to-all-start.1 = ((f32[32,16,128]{2,1,0:T(8,128)}), f32[32,16,128]{2,1,0:T(8,128)S(1)}, u32[]{:S(2)}, u32[]{:S(2)}) async-start(f32[32,16,128]{2,1,0:T(8,128)} %shard_map.82), calls=%async_computation.1 | async-start | bytes 524288 | tf_op jit(solution)/shard_map/all_to_all | solution.py:126
  45.7 0.0 all-gather.5.cloned.1.call-start
  45.7 0.0 copy-done.8
  45.8 0.0 copy-done.9
  45.8 0.1 select_reduce_fusion
  45.9 0.1 constant_dynamic-slice_fusion
  45.9 0.1 copy.50
  46.0 0.7 reshape.40.idx_ref
  46.7 10.3 %all-to-all-done.1 = f32[32,16,128]{2,1,0:T(8,128)S(1)} async-done(((f32[32,16,128]{2,1,0:T(8,128)}), f32[32,16,128]{2,1,0:T(8,128)S(1)}, u32[]{:S(2)}, u32[]{:S(2)}) %all-to-all-start.1) | async-done | bytes 262176 | tf_op jit(solution)/shard_map/all_to_all | solution.py:126
  57.0 0.1 copy.49
  57.1 0.0 all-gather.3.cloned.1.call-done.g_ref
  57.1 0.0 copy-done.4
  57.1 1.3 %broadcast_in_dim.40 = bf16[32,2,64,64]{3,2,1,0:T(8,128)(2,1)} broadcast(bf16[32,64,64]{2,1,0:T(8,128)(2,1)S(1)} %copy-done.4), dimensions={0,2,3} | broadcast | bytes 786432 | tf_op jit(solution)/shard_map/broadcast_in_dim | solution.py:22
  58.4 5.8 %shard_map.83 = f32[128,512]{1,0:T(8,128)} custom-call(s32[256]{0:T(256)} %reshape.40.idx_ref, bf16[32,128,128]{2,1,0:T(8,128)(2,1)} %all-gather.3.cloned.1.call-done.g_ref, bf16[4096,64]{1,0:T(8,128)(2,1)} %bitcast.33), custom_call_target="tpu_custom_call" | custom-call | tf_op jit(solution)/shard_map/pallas_call | solution.py:94
  64.2 0.0 copy-done.1
  64.2 0.0 copy-done.2
  64.2 1.1 fusion.4
  65.3 0.1 copy.54
  65.4 0.8 copy.55
  66.2 0.0 all-gather.5.cloned.1.call-update
  66.2 0.1 copy.52
  66.3 14.1 %all_to_all.20.x_ref = bf16[32,16,128]{2,1,0:T(8,128)(2,1)} all-to-all(bf16[32,16,128]{2,1,0:T(8,128)(2,1)S(1)} %bitcast.38), channel_id=1, replica_groups=mesh['up'=32,'down'=8] {'up'}, dimensions={0} | all-to-all | bytes 262144 | tf_op jit(solution)/shard_map/all_to_all | solution.py:124
  80.5 8.8 %shard_map.84 = f32[32,16,128]{2,1,0:T(8,128)} custom-call(s32[2048]{0:T(1024)} %reshape.36.idx_ref, bf16[32,16,128]{2,1,0:T(8,128)(2,1)} %all_to_all.20.x_ref, bf16[4096,64]{1,0:T(8,128)(2,1)} %bitcast.32), custom_call_target="tpu_custom_call" | custom-call | tf_op jit(solution)/shard_map/pallas_call | solution.py:79
  89.2 15.6 %all_to_all.21 = f32[32,16,128]{2,1,0:T(8,128)S(1)} all-to-all(f32[32,16,128]{2,1,0:T(8,128)} %shard_map.84), channel_id=1, replica_groups=mesh['up'=32,'down'=8] {'up'}, dimensions={0} | all-to-all | bytes 524288 | tf_op jit(solution)/shard_map/all_to_all | solution.py:126
  104.8 0.1 copy.53
  105.0 0.0 copy-start
  105.0 0.0 all-gather.5.cloned.1.call-done.g_ref
  105.0 5.8 %shard_map.85 = f32[128,512]{1,0:T(8,128)} custom-call(s32[256]{0:T(256)} %reshape.40.idx_ref, bf16[32,128,128]{2,1,0:T(8,128)(2,1)} %all-gather.5.cloned.1.call-done.g_ref, bf16[4096,64]{1,0:T(8,128)(2,1)} %bitcast.34), custom_call_target="tpu_custom_call" | custom-call | tf_op jit(solution)/shard_map/pallas_call | solution.py:94
  110.8 0.0 copy-done
  110.8 1.8 %fusion.1 = f32[128,512]{1,0:T(8,128)} fusion(f32[128,512]{1,0:T(8,128)S(1)} %copy-done.1, f32[128,512]{1,0:T(8,128)} %shard_map.85, f32[512,128]{0,1:T(8,128)S(1)} %copy.53, s32[128,512]{1,0:T(8,128)S(1)} %copy-done.2, f32[128,512]{1,0:T(8,128)S(1)} %copy-done, f32[512,128]{0,1:T(8,128)S(1)} %copy.49), kind=kLoop, calls=%fused_computation.6 | loop fusion | flops 720896 | bytes 1835008 | tf_op jit(solution)/shard_map/sub | solution.py:139
  (6 shorter events, 0.0 us)
Async XLA Ops:
  6.5 24.6 %copy-start.3 = (bf16[32,64,64]{2,1,0:T(8,128)(2,1)S(1)}, bf16[32,64,64]{2,1,0:T(8,128)(2,1)}, u32[]{:S(2)}) copy-start(bf16[32,64,64]{2,1,0:T(8,128)(2,1)} %param.12) | copy-start | bytes 786436
  6.5 50.6 %all-gather.3.cloned.1.call-start = ((), (), s32[]{:S(2)}) async-start(), calls=%async_computation.4 | async-start | bytes 1179648 | tf_op jit(solution)/shard_map/all_gather | solution.py:131
  10.0 11.4 %copy-start.6 = (s32[64,32]{0,1:T(8,128)S(1)}, s32[64,32]{0,1:T(8,128)}, u32[]{:S(2)}) copy-start(s32[64,32]{0,1:T(8,128)} %param.10) | copy-start | bytes 24580
  10.0 11.4 %copy-start.7 = (s32[64,32]{0,1:T(8,128)S(1)}, s32[64,32]{0,1:T(8,128)}, u32[]{:S(2)}) copy-start(s32[64,32]{0,1:T(8,128)} %param.11) | copy-start | bytes 24580
  10.0 21.2 %all-to-all-start = ((bf16[32,16,128]{2,1,0:T(8,128)(2,1)}), bf16[32,16,128]{2,1,0:T(8,128)(2,1)S(1)}, u32[]{:S(2)}, u32[]{:S(2)}) async-start(bf16[32,16,128]{2,1,0:T(8,128)(2,1)} %bitcast.1), calls=%async_computation | async-start | bytes 262144 | tf_op jit(solution)/shard_map/all_to_all | solution.py:124
  31.2 1.3 %copy-start.5 = (bf16[32,16,128]{2,1,0:T(8,128)(2,1)}, bf16[32,16,128]{2,1,0:T(8,128)(2,1)S(1)}, u32[]{:S(2)}) copy-start(bf16[32,16,128]{2,1,0:T(8,128)(2,1)S(1)} %all-to-all-done.x_ref) | copy-start | bytes 393220
  32.5 13.3 %copy-start.8 = (s32[64,32]{0,1:T(8,128)S(1)}, s32[64,32]{0,1:T(8,128)}, u32[]{:S(2)}) copy-start(s32[64,32]{0,1:T(8,128)} %param.13) | copy-start | bytes 24580
  32.5 13.3 %copy-start.9 = (s32[64,32]{0,1:T(8,128)S(1)}, s32[64,32]{0,1:T(8,128)}, u32[]{:S(2)}) copy-start(s32[64,32]{0,1:T(8,128)} %param.14) | copy-start | bytes 24580
  41.3 15.8 %copy-start.4 = (bf16[32,64,64]{2,1,0:T(8,128)(2,1)S(1)}, bf16[32,64,64]{2,1,0:T(8,128)(2,1)}, u32[]{:S(2)}) copy-start(bf16[32,64,64]{2,1,0:T(8,128)(2,1)} %param.15) | copy-start | bytes 786436
  41.3 15.7 %all-to-all-start.1 = ((f32[32,16,128]{2,1,0:T(8,128)}), f32[32,16,128]{2,1,0:T(8,128)S(1)}, u32[]{:S(2)}, u32[]{:S(2)}) async-start(f32[32,16,128]{2,1,0:T(8,128)} %shard_map.82), calls=%async_computation.1 | async-start | bytes 524288 | tf_op jit(solution)/shard_map/all_to_all | solution.py:126
  45.7 59.3 %all-gather.5.cloned.1.call-start = ((), (), s32[]{:S(2)}) async-start(), calls=%async_computation.5 | async-start | bytes 1179648 | tf_op jit(solution)/shard_map/all_gather | solution.py:131
  58.4 5.8 %copy-start.1 = (f32[128,512]{1,0:T(8,128)S(1)}, f32[128,512]{1,0:T(8,128)}, u32[]{:S(2)}) copy-start(f32[128,512]{1,0:T(8,128)} %param.8) | copy-start | bytes 786436
  58.4 5.8 %copy-start.2 = (s32[128,512]{1,0:T(8,128)S(1)}, s32[128,512]{1,0:T(8,128)}, u32[]{:S(2)}) copy-start(s32[128,512]{1,0:T(8,128)} %param.9) | copy-start | bytes 786436
  105.0 5.8 %copy-start = (f32[128,512]{1,0:T(8,128)S(1)}, f32[128,512]{1,0:T(8,128)}, u32[]{:S(2)}) copy-start(f32[128,512]{1,0:T(8,128)} %shard_map.83) | copy-start | bytes 786436
Sparse Core Ops, SparseCore 0:
  10.1 28.3 all-gather.2
  66.3 21.5 all-gather.4

commit v2 on v1

--- a/solution.py
+++ b/solution.py
@@ -118,25 +118,38 @@
     up_table = doubled_table(up_blocks)
     down_table = doubled_table(down_blocks)
     onsite = coupling * double_occ.astype(jnp.float32) - center
+    down_count = lax.axis_size("down")
+    col_chunk = local_cols // up_count
 
-    def up_part(rounded):
-        sectioned = rounded.T.reshape(up_count, local_cols // up_count, local_rows)
-        received = lax.all_to_all(sectioned, "up", 0, 0, tiled=True)
-        hopped = up_hop(up_idx, received, up_table)
-        returned = lax.all_to_all(hopped, "up", 0, 0, tiled=True)
-        return returned.reshape(local_cols, local_rows).T
+    def to_columns(values):
+        return values.T.reshape(up_count, col_chunk, local_rows)
+
+    def to_rows(pieces):
+        return pieces.reshape(local_cols, local_rows).T
+
+    def exchange_up(pieces):
+        return lax.all_to_all(pieces, "up", 0, 0, tiled=True)
 
     def down_part(rounded):
         paired = rounded.reshape(local_rows, local_cols // LANES, LANES).transpose(1, 0, 2)
-        gathered = lax.all_gather(paired, "down", axis=0, tiled=True)
+        copies = jnp.broadcast_to(paired[None], (down_count,) + paired.shape)
+        gathered = lax.all_to_all(copies, "down", 0, 0, tiled=True)
+        gathered = gathered.reshape((-1,) + paired.shape[1:])
         return down_hop(down_idx, gathered, down_table, local_cols)
 
-    def apply_scaled(current):
-        rounded = current.astype(jnp.bfloat16)
-        return (onsite * current + up_part(rounded) + down_part(rounded)) / half_span
+    rounded0 = amplitudes.astype(jnp.bfloat16)
+    up0_cols = up_hop(up_idx, exchange_up(to_columns(rounded0)), up_table)
+    partial_rows = onsite * amplitudes + down_part(rounded0)
+    both = exchange_up(jnp.concatenate([to_columns(partial_rows), up0_cols], axis=1))
+    partial_cols = both[:, :col_chunk]
+    up0_rows = to_rows(both[:, col_chunk:])
+    first_cols = (partial_cols + up0_cols) / half_span
+    first_rows = (partial_rows + up0_rows) / half_span
 
-    first = apply_scaled(amplitudes)
-    return 2.0 * apply_scaled(first) - amplitudes
+    up1_cols = up_hop(up_idx, first_cols.astype(jnp.bfloat16), up_table)
+    down1_rows = down_part(first_rows.astype(jnp.bfloat16))
+    up1_rows = to_rows(exchange_up(up1_cols))
+    return 2.0 * ((onsite * first_rows + up1_rows + down1_rows) / half_span) - amplitudes
 
 
 def solution(mesh):

time: 120 us -> 132 us (1.10)
  waiting for transfers between devices: 19.3 us -> 39.9 us
  between operations: 13.5 us -> 0.17 us
  blocking collectives: 29.8 us -> 21.4 us
  starting transfers between devices: 15.8 us -> 24.2 us
  other arithmetic: 3.08 us -> 4.88 us
  local copies, waits for them, and re-layouts: 8.84 us -> 10.6 us
    all_to_all x2 -> x4, waiting for transfers between devices: 19.2 us -> 39.9 us  [the longest x2 20.2 us: exchange_up(): return lax.all_to_all(pieces, 'up', 0, 0, tiled=True)]
    all_to_all x2 -> x4, starting transfers between devices: 15.8 us -> 24.2 us  [the longest x2 16.2 us: exchange_up(): return lax.all_to_all(pieces, 'up', 0, 0, tiled=True)]
    all_to_all x2 -> x1, blocking collectives: 29.8 us -> 21.4 us  [exchange_up(): return lax.all_to_all(pieces, 'up', 0, 0, tiled=True)]
    broadcast_in_dim x0 -> x2, local copies, waits for them, and re-layouts: none -> 2.44 us  [down_part(): copies = jnp.broadcast_to(paired[None], (down_count,) + paired.shape)]
    transpose x2, local copies, waits for them, and re-layouts: 2.42 us -> 0.04 us  [down_part(): rounded.reshape(local_rows, local_cols // LANES, LANES).transpose(1, 0, 2)]
    transpose x0 -> x2, other arithmetic: none -> 1.98 us  [to_columns(): return values.T.reshape(up_count, col_chunk, local_rows)]
    unnamed x21 -> x26, local copies, waits for them, and re-layouts: 1.81 us -> 2.71 us
  transfers between devices with their start and end apart: 4 -> 4, of which waited for: 2 -> 4; matrix products, arithmetic and copies ran while one was open for 3% -> 3% of each run, Pallas kernels for 15% -> 7%
where the time goes in v2:
time: 132 us; the launch traced here: 130 us
  waiting for transfers between devices  39.9 us (30%)
  Pallas kernels  29.1 us (22%)
  starting transfers between devices  24.2 us (18%)
  blocking collectives  21.4 us (16%)
  local copies, waits for them, and re-layouts  10.6 us (8%)
  other arithmetic  4.88 us (4%)
    all_to_all x1, blocking collectives, exchange_up(): return lax.all_to_all(pieces, 'up', 0, 0, tiled=True)  21.4 us
    all_to_all x2, waiting for transfers between devices, exchange_up(): return lax.all_to_all(pieces, 'up', 0, 0, tiled=True)  20.2 us
    all_to_all x2, waiting for transfers between devices, down_part(): gathered = lax.all_to_all(copies, 'down', 0, 0, tiled=True)  19.7 us
    pallas_call x2, Pallas kernels, up_hop(): pl.pallas_call(up_kernel, out_shape=jax.ShapeDtypeStruct((pairs, n, LANES...  17.6 us
    all_to_all x2, starting transfers between devices, exchange_up(): return lax.all_to_all(pieces, 'up', 0, 0, tiled=True)  16.2 us
    pallas_call x2, Pallas kernels, down_hop(): pl.pallas_call(down_kernel, out_shape=jax.ShapeDtypeStruct((rows, own_col...  11.5 us
    all_to_all x2, starting transfers between devices, down_part(): gathered = lax.all_to_all(copies, 'down', 0, 0, tiled=True)  8 us
    unnamed x26, local copies, waits for them, and re-layouts  2.71 us
  transfers between devices with their start and end apart: 4, of which 4 were waited for; matrix products, arithmetic and copies ran while one was open for 3% of the time, Pallas kernels for 7%

profile of v2, /device:TPU:32, one launch (start us, length us, event | category | flops | bytes accessed | tf_op | source)
XLA Modules:
  0.0 130.2 jit_solution(12403012594636830684)
XLA Ops:
  0.0 1.0 convert_bitcast_fusion
  1.0 0.0 copy-start
  1.0 0.8 copy.40
  1.7 11.4 %all-to-all-start.1 = ((bf16[32,16,128]{2,1,0:T(8,128)(2,1)}), bf16[32,16,128]{2,1,0:T(8,128)(2,1)S(1)}, u32[]{:S(2)}, u32[]{:S(2)}) async-start(bf16[32,16,128]{2,1,0:T(8,128)(2,1)} %bitcast.6), calls=%async_computation.1 | async-start | bytes 262144 | tf_op jit(solution)/shard_map/all_to_all | solution.py:131
  13.1 0.0 copy-done
  13.2 9.7 %all-to-all-done.1.x_ref = bf16[32,16,128]{2,1,0:T(8,128)(2,1)S(1)} async-done(((bf16[32,16,128]{2,1,0:T(8,128)(2,1)}), bf16[32,16,128]{2,1,0:T(8,128)(2,1)S(1)}, u32[]{:S(2)}, u32[]{:S(2)}) %all-to-all-start.1) | async-done | bytes 131104 | tf_op jit(solution)/shard_map/all_to_all | solution.py:131
  22.9 1.2 broadcast_in_dim.28
  24.1 0.0 copy-done.8
  24.1 4.4 %all-to-all-start = ((bf16[8,4,128,128]{3,2,1,0:T(8,128)(2,1)}), bf16[8,4,128,128]{3,2,1,0:T(8,128)(2,1)S(1)}, u32[]{:S(2)}, u32[]{:S(2)}) async-start(bf16[8,4,128,128]{3,2,1,0:T(8,128)(2,1)} %broadcast_in_dim.28), calls=%async_computation | async-start | bytes 2097152 | tf_op jit(solution)/shard_map/all_to_all | solution.py:136
  28.6 0.0 copy-done.9
  28.6 0.0 copy-done.10
  28.6 0.1 select_reduce_fusion
  28.7 0.1 copy.39
  28.8 0.0 copy-start.12
  28.8 0.7 reshape.49.idx_ref
  29.4 0.0 copy-done.11
  29.5 0.0 copy-done.12
  29.5 0.1 select_reduce_fusion.1
  29.6 0.1 constant_dynamic-slice_fusion
  29.7 0.1 copy.36
  29.8 0.7 reshape.44.idx_ref
  30.4 0.0 copy-done.6
  30.4 1.3 broadcast_in_dim.53
  31.7 8.8 %shard_map.83 = f32[32,16,128]{2,1,0:T(8,128)} custom-call(s32[2048]{0:T(1024)} %reshape.49.idx_ref, bf16[32,16,128]{2,1,0:T(8,128)(2,1)} %copy-done.8, bf16[4096,64]{1,0:T(8,128)(2,1)} %bitcast.30), custom_call_target="tpu_custom_call" | custom-call | tf_op jit(solution)/shard_map/pallas_call | solution.py:79
  40.5 4.0 %all-to-all-done = bf16[8,4,128,128]{3,2,1,0:T(8,128)(2,1)S(1)} async-done(((bf16[8,4,128,128]{3,2,1,0:T(8,128)(2,1)}), bf16[8,4,128,128]{3,2,1,0:T(8,128)(2,1)S(1)}, u32[]{:S(2)}, u32[]{:S(2)}) %all-to-all-start) | async-done | bytes 1048608 | tf_op jit(solution)/shard_map/all_to_all | solution.py:136
  44.5 0.0 copy-done.7
  44.5 1.3 %broadcast_in_dim.29 = bf16[32,2,64,64]{3,2,1,0:T(8,128)(2,1)} broadcast(bf16[32,64,64]{2,1,0:T(8,128)(2,1)S(1)} %copy-done.7), dimensions={0,2,3} | broadcast | bytes 786432 | tf_op jit(solution)/shard_map/broadcast_in_dim | solution.py:22
  45.8 0.0 copy-done.1
  45.8 5.8 %shard_map.82 = f32[128,512]{1,0:T(8,128)} custom-call(s32[256]{0:T(256)} %reshape.44.idx_ref, bf16[32,128,128]{2,1,0:T(8,128)(2,1)} %bitcast.32, bf16[4096,64]{1,0:T(8,128)(2,1)} %bitcast.28), custom_call_target="tpu_custom_call" | custom-call | tf_op jit(solution)/shard_map/pallas_call | solution.py:94
  51.6 1.0 fusion.6
  52.6 0.0 copy-start.5
  52.6 0.1 copy.38
  52.8 0.8 copy-done.5
  53.6 21.4 %all_to_all.25 = f32[32,32,128]{2,1,0:T(8,128)S(1)} all-to-all(f32[32,32,128]{2,1,0:T(8,128)S(1)} %pad_maximum_fusion), channel_id=1, replica_groups=mesh['up'=32,'down'=8] {'up'}, dimensions={0} | all-to-all | bytes 1048576 | tf_op jit(solution)/shard_map/all_to_all | solution.py:131
  75.0 0.7 fusion.1
  75.7 8.8 %shard_map.84 = f32[32,16,128]{2,1,0:T(8,128)} custom-call(s32[2048]{0:T(1024)} %reshape.49.idx_ref, bf16[32,16,128]{2,1,0:T(8,128)(2,1)} %get-tuple-element.5.x_ref, bf16[4096,64]{1,0:T(8,128)(2,1)} %bitcast.31), custom_call_target="tpu_custom_call" | custom-call | tf_op jit(solution)/shard_map/pallas_call | solution.py:79
  84.5 4.8 %all-to-all-start.3 = ((f32[32,16,128]{2,1,0:T(8,128)}), f32[32,16,128]{2,1,0:T(8,128)S(1)}, u32[]{:S(2)}, u32[]{:S(2)}) async-start(f32[32,16,128]{2,1,0:T(8,128)} %shard_map.84), calls=%async_computation.3 | async-start | bytes 524288 | tf_op jit(solution)/shard_map/all_to_all | solution.py:131
  89.4 0.1 copy.41
  89.5 0.8 copy-done.3
  90.3 0.1 fusion.5
  90.5 10.5 %all-to-all-done.3 = f32[32,16,128]{2,1,0:T(8,128)S(1)} async-done(((f32[32,16,128]{2,1,0:T(8,128)}), f32[32,16,128]{2,1,0:T(8,128)S(1)}, u32[]{:S(2)}, u32[]{:S(2)}) %all-to-all-start.3) | async-done | bytes 262176 | tf_op jit(solution)/shard_map/all_to_all | solution.py:131
  101.0 1.2 broadcast_in_dim.54
  102.3 3.6 %all-to-all-start.4 = ((bf16[8,4,128,128]{3,2,1,0:T(8,128)(2,1)}), bf16[8,4,128,128]{3,2,1,0:T(8,128)(2,1)S(1)}, u32[]{:S(2)}, u32[]{:S(2)}) async-start(bf16[8,4,128,128]{3,2,1,0:T(8,128)(2,1)} %broadcast_in_dim.54), calls=%async_computation.4 | async-start | bytes 2097152 | tf_op jit(solution)/shard_map/all_to_all | solution.py:136
  105.8 0.1 copy.42
  106.0 15.7 %all-to-all-done.4 = bf16[8,4,128,128]{3,2,1,0:T(8,128)(2,1)S(1)} async-done(((bf16[8,4,128,128]{3,2,1,0:T(8,128)(2,1)}), bf16[8,4,128,128]{3,2,1,0:T(8,128)(2,1)S(1)}, u32[]{:S(2)}, u32[]{:S(2)}) %all-to-all-start.4) | async-done | bytes 1048608 | tf_op jit(solution)/shard_map/all_to_all | solution.py:136
  121.7 1.0 copy-done.2
  122.7 5.7 %shard_map.85 = f32[128,512]{1,0:T(8,128)} custom-call(s32[256]{0:T(256)} %reshape.44.idx_ref, bf16[32,128,128]{2,1,0:T(8,128)(2,1)} %bitcast.33, bf16[4096,64]{1,0:T(8,128)(2,1)} %bitcast.29), custom_call_target="tpu_custom_call" | custom-call | tf_op jit(solution)/shard_map/pallas_call | solution.py:94
  128.4 1.8 %fusion.3 = f32[128,512]{1,0:T(8,128)} fusion(f32[128,512]{1,0:T(8,128)S(1)} %copy-done, f32[128,512]{1,0:T(8,128)} %shard_map.85, f32[512,128]{0,1:T(8,128)S(1)} %copy.42, s32[128,512]{1,0:T(8,128)S(1)} %copy-done.4, f32[512,128]{0,1:T(8,128)S(1)} %copy.41, f32[128,512]{1,0:T(8,128)S(1)} %copy-done.3), kind=kLoop, calls=%fused_computation.10 | loop fusion | flops 720896 | bytes 1835008 | tf_op jit(solution)/shard_map/sub | solution.py:152
  (17 shorter events, 0.2 us)
Async XLA Ops:
  1.0 12.1 %copy-start = (f32[128,512]{1,0:T(8,128)S(1)}, f32[128,512]{1,0:T(8,128)}, u32[]{:S(2)}) copy-start(f32[128,512]{1,0:T(8,128)} %param.8) | copy-start | bytes 786436
  1.7 21.2 %all-to-all-start.1 = ((bf16[32,16,128]{2,1,0:T(8,128)(2,1)}), bf16[32,16,128]{2,1,0:T(8,128)(2,1)S(1)}, u32[]{:S(2)}, u32[]{:S(2)}) async-start(bf16[32,16,128]{2,1,0:T(8,128)(2,1)} %bitcast.6), calls=%async_computation.1 | async-start | bytes 262144 | tf_op jit(solution)/shard_map/all_to_all | solution.py:131
  22.9 1.2 copy-start.8
  24.1 4.5 %copy-start.9 = (s32[64,32]{0,1:T(8,128)S(1)}, s32[64,32]{0,1:T(8,128)}, u32[]{:S(2)}) copy-start(s32[64,32]{0,1:T(8,128)} %param.10) | copy-start | bytes 24580
  24.1 4.5 %copy-start.10 = (s32[64,32]{0,1:T(8,128)S(1)}, s32[64,32]{0,1:T(8,128)}, u32[]{:S(2)}) copy-start(s32[64,32]{0,1:T(8,128)} %param.11) | copy-start | bytes 24580
  24.1 6.3 %copy-start.6 = (bf16[32,64,64]{2,1,0:T(8,128)(2,1)S(1)}, bf16[32,64,64]{2,1,0:T(8,128)(2,1)}, u32[]{:S(2)}) copy-start(bf16[32,64,64]{2,1,0:T(8,128)(2,1)} %param.12) | copy-start | bytes 786436
  24.1 20.4 %all-to-all-start = ((bf16[8,4,128,128]{3,2,1,0:T(8,128)(2,1)}), bf16[8,4,128,128]{3,2,1,0:T(8,128)(2,1)S(1)}, u32[]{:S(2)}, u32[]{:S(2)}) async-start(bf16[8,4,128,128]{3,2,1,0:T(8,128)(2,1)} %broadcast_in_dim.28), calls=%async_computation | async-start | bytes 2097152 | tf_op jit(solution)/shard_map/all_to_all | solution.py:136
  28.8 0.7 copy-start.11
  28.8 0.7 copy-start.12
  31.7 12.8 %copy-start.7 = (bf16[32,64,64]{2,1,0:T(8,128)(2,1)S(1)}, bf16[32,64,64]{2,1,0:T(8,128)(2,1)}, u32[]{:S(2)}) copy-start(bf16[32,64,64]{2,1,0:T(8,128)(2,1)} %param.15) | copy-start | bytes 786436
  44.5 1.3 %copy-start.1 = (bf16[8,4,128,128]{3,2,1,0:T(8,128)(2,1)}, bf16[8,4,128,128]{3,2,1,0:T(8,128)(2,1)S(1)}, u32[]{:S(2)}) copy-start(bf16[8,4,128,128]{3,2,1,0:T(8,128)(2,1)S(1)} %all-to-all-done) | copy-start | bytes 3145732
  45.8 5.8 %copy-start.4 = (s32[128,512]{1,0:T(8,128)S(1)}, s32[128,512]{1,0:T(8,128)}, u32[]{:S(2)}) copy-start(s32[128,512]{1,0:T(8,128)} %param.9) | copy-start | bytes 786436
  52.6 1.0 copy-start.5
  84.5 16.5 %all-to-all-start.3 = ((f32[32,16,128]{2,1,0:T(8,128)}), f32[32,16,128]{2,1,0:T(8,128)S(1)}, u32[]{:S(2)}, u32[]{:S(2)}) async-start(f32[32,16,128]{2,1,0:T(8,128)} %shard_map.84), calls=%async_computation.3 | async-start | bytes 524288 | tf_op jit(solution)/shard_map/all_to_all | solution.py:131
  89.4 1.0 copy-start.3
  102.3 19.4 %all-to-all-start.4 = ((bf16[8,4,128,128]{3,2,1,0:T(8,128)(2,1)}), bf16[8,4,128,128]{3,2,1,0:T(8,128)(2,1)S(1)}, u32[]{:S(2)}, u32[]{:S(2)}) async-start(bf16[8,4,128,128]{3,2,1,0:T(8,128)(2,1)} %broadcast_in_dim.54), calls=%async_computation.4 | async-start | bytes 2097152 | tf_op jit(solution)/shard_map/all_to_all | solution.py:136
  121.7 1.0 copy-start.2

commit v3 on v2

--- a/solution.py
+++ b/solution.py
@@ -118,7 +118,6 @@
     up_table = doubled_table(up_blocks)
     down_table = doubled_table(down_blocks)
     onsite = coupling * double_occ.astype(jnp.float32) - center
-    down_count = lax.axis_size("down")
     col_chunk = local_cols // up_count
 
     def to_columns(values):
@@ -132,9 +131,7 @@
 
     def down_part(rounded):
         paired = rounded.reshape(local_rows, local_cols // LANES, LANES).transpose(1, 0, 2)
-        copies = jnp.broadcast_to(paired[None], (down_count,) + paired.shape)
-        gathered = lax.all_to_all(copies, "down", 0, 0, tiled=True)
-        gathered = gathered.reshape((-1,) + paired.shape[1:])
+        gathered = lax.all_gather(paired, "down", axis=0, tiled=True)
         return down_hop(down_idx, gathered, down_table, local_cols)
 
     rounded0 = amplitudes.astype(jnp.bfloat16)

time: 132 us -> 119 us (0.902)
  waiting for transfers between devices: 39.9 us -> 7.96 us
  blocking collectives: 21.4 us -> 42 us
  between operations: 0.17 us -> 13.5 us
  starting transfers between devices: 24.2 us -> 11.4 us
    all_to_all x1 -> x2, blocking collectives: 21.4 us -> 42 us  [exchange_up(): return lax.all_to_all(pieces, 'up', 0, 0, tiled=True)]
    all_to_all x2 -> x0, waiting for transfers between devices: 19.7 us -> none  [down_part(): gathered = lax.all_to_all(copies, 'down', 0, 0, tiled=True)]
    all_to_all x2 -> x1, waiting for transfers between devices: 20.2 us -> 7.9 us  [exchange_up(): return lax.all_to_all(pieces, 'up', 0, 0, tiled=True)]
    all_to_all x2 -> x0, starting transfers between devices: 8 us -> none  [down_part(): gathered = lax.all_to_all(copies, 'down', 0, 0, tiled=True)]
    all_to_all x2 -> x1, starting transfers between devices: 16.2 us -> 11.4 us  [exchange_up(): return lax.all_to_all(pieces, 'up', 0, 0, tiled=True)]
    transpose x2, local copies, waits for them, and re-layouts: 0.04 us -> 2.5 us  [down_part(): rounded.reshape(local_rows, local_cols // LANES, LANES).transpose(1, 0, 2)]
    broadcast_in_dim x2 -> x0, local copies, waits for them, and re-layouts: 2.44 us -> none  [down_part(): copies = jnp.broadcast_to(paired[None], (down_count,) + paired.shape)]
    unnamed x26 -> x23, local copies, waits for them, and re-layouts: 2.71 us -> 3.43 us
  transfers between devices with their start and end apart: 4 -> 3, of which waited for: 4 -> 1; matrix products, arithmetic and copies ran while one was open for 3% -> 3% of each run, Pallas kernels for 7% -> 15%
where the time goes in v3:
time: 119 us; the launch traced here: 118 us
  blocking collectives  42 us (35%)
  Pallas kernels  29.1 us (24%)
  between operations  13.5 us (11%)
  starting transfers between devices  11.4 us (10%)
  local copies, waits for them, and re-layouts  10.6 us (9%)
  waiting for transfers between devices  7.96 us (7%)
  other arithmetic  3.88 us (3%)
    all_to_all x2, blocking collectives, exchange_up(): return lax.all_to_all(pieces, 'up', 0, 0, tiled=True)  42 us
    pallas_call x2, Pallas kernels, up_hop(): pl.pallas_call(up_kernel, out_shape=jax.ShapeDtypeStruct((pairs, n, LANES...  17.6 us
    pallas_call x2, Pallas kernels, down_hop(): pl.pallas_call(down_kernel, out_shape=jax.ShapeDtypeStruct((rows, own_col...  11.5 us
    all_to_all x1, starting transfers between devices, exchange_up(): return lax.all_to_all(pieces, 'up', 0, 0, tiled=True)  11.4 us
    all_to_all x1, waiting for transfers between devices, exchange_up(): return lax.all_to_all(pieces, 'up', 0, 0, tiled=True)  7.9 us
    unnamed x23, local copies, waits for them, and re-layouts  3.43 us
    broadcast_in_dim x2, local copies, waits for them, and re-layouts, doubled_table(): jnp.broadcast_to(shared_table[:, None], (shared_count, 2, block_width, bl...  2.6 us
    transpose x2, local copies, waits for them, and re-layouts, down_part(): rounded.reshape(local_rows, local_cols // LANES, LANES).transpose(1, 0, 2)  2.5 us
  transfers between devices with their start and end apart: 3, of which 1 were waited for; matrix products, arithmetic and copies ran while one was open for 3% of the time, Pallas kernels for 15%

profile of v3, /device:TPU:32, one launch (start us, length us, event | category | flops | bytes accessed | tf_op | source)
XLA Modules:
  0.0 118.5 jit_solution(9792172189433725677)
XLA Ops:
  6.5 0.0 all-gather.3.cloned.1.call-start
  6.5 1.7 %copy.48 = bf16[128,512]{0,1:T(8,128)(2,1)} copy(f32[128,512]{1,0:T(8,128)} %param.8) | data formatting | bytes 393216 | tf_op args[0]
  8.2 1.7 %copy.49 = bf16[4,128,128]{2,1,0:T(8,128)(2,1)} copy(bf16[4,128,128]{1,2,0:T(8,128)(2,1)} %bitcast.1) | data formatting | bytes 262144 | tf_op jit(solution)/shard_map/transpose | solution.py:133
  10.0 0.0 all-gather.3.cloned.1.call-update
  10.0 0.0 copy-start.7
  10.0 0.0 copy-start.8
  10.0 11.4 %all-to-all-start = ((bf16[32,16,128]{2,1,0:T(8,128)(2,1)}), bf16[32,16,128]{2,1,0:T(8,128)(2,1)S(1)}, u32[]{:S(2)}, u32[]{:S(2)}) async-start(bf16[32,16,128]{2,1,0:T(8,128)(2,1)} %bitcast.6), calls=%async_computation | async-start | bytes 262144 | tf_op jit(solution)/shard_map/all_to_all | solution.py:130
  21.4 0.0 all-gather.5.cloned.1.call-start
  21.4 0.0 copy-done.7
  21.5 0.0 copy-done.8
  21.5 0.1 select_reduce_fusion
  21.6 0.1 copy.51
  21.7 0.0 copy-start.10
  21.7 0.7 reshape.40.idx_ref
  22.3 0.0 copy-done.9
  22.4 0.0 copy-done.10
  22.4 0.1 select_reduce_fusion.1
  22.5 0.1 constant_dynamic-slice_fusion
  22.6 0.1 copy.47
  22.6 0.7 reshape.36.idx_ref
  23.3 7.9 %all-to-all-done.x_ref = bf16[32,16,128]{2,1,0:T(8,128)(2,1)S(1)} async-done(((bf16[32,16,128]{2,1,0:T(8,128)(2,1)}), bf16[32,16,128]{2,1,0:T(8,128)(2,1)S(1)}, u32[]{:S(2)}, u32[]{:S(2)}) %all-to-all-start) | async-done | bytes 131104 | tf_op jit(solution)/shard_map/all_to_all | solution.py:130
  31.2 0.0 copy-done.4
  31.2 1.3 %broadcast_in_dim.40 = bf16[32,2,64,64]{3,2,1,0:T(8,128)(2,1)} broadcast(bf16[32,64,64]{2,1,0:T(8,128)(2,1)S(1)} %copy-done.4), dimensions={0,2,3} | broadcast | bytes 786432 | tf_op jit(solution)/shard_map/broadcast_in_dim | solution.py:22
  32.5 0.0 copy-done.6
  32.5 8.8 %shard_map.83 = f32[32,16,128]{2,1,0:T(8,128)} custom-call(s32[2048]{0:T(1024)} %reshape.40.idx_ref, bf16[32,16,128]{2,1,0:T(8,128)(2,1)} %copy-done.6, bf16[4096,64]{1,0:T(8,128)(2,1)} %bitcast.32), custom_call_target="tpu_custom_call" | custom-call | tf_op jit(solution)/shard_map/pallas_call | solution.py:79
  41.3 0.0 copy-done.5
  41.3 1.3 %broadcast_in_dim.38 = bf16[32,2,64,64]{3,2,1,0:T(8,128)(2,1)} broadcast(bf16[32,64,64]{2,1,0:T(8,128)(2,1)S(1)} %copy-done.5), dimensions={0,2,3} | broadcast | bytes 786432 | tf_op jit(solution)/shard_map/broadcast_in_dim | solution.py:22
  42.6 5.8 %shard_map.82 = f32[128,512]{1,0:T(8,128)} custom-call(s32[256]{0:T(256)} %reshape.36.idx_ref, bf16[32,128,128]{2,1,0:T(8,128)(2,1)} %all-gather.3.cloned.1.call-done.g_ref, bf16[4096,64]{1,0:T(8,128)(2,1)} %bitcast.30), custom_call_target="tpu_custom_call" | custom-call | tf_op jit(solution)/shard_map/pallas_call | solution.py:94
  48.4 0.0 copy-done.1
  48.4 0.0 copy-done.2
  48.4 1.0 fusion.6
  49.4 0.0 copy-start.3
  49.5 0.1 copy.50
  49.6 0.8 copy-done.3
  50.5 25.1 %all_to_all.15 = f32[32,32,128]{2,1,0:T(8,128)S(1)} all-to-all(f32[32,32,128]{2,1,0:T(8,128)S(1)} %pad_maximum_fusion), channel_id=1, replica_groups=mesh['up'=32,'down'=8] {'up'}, dimensions={0} | all-to-all | bytes 1048576 | tf_op jit(solution)/shard_map/all_to_all | solution.py:130
  75.5 0.7 fusion.1
  76.2 0.1 copy.52
  76.4 0.8 copy-done
  77.2 0.1 fusion.5
  77.3 0.1 copy.54
  77.4 0.8 copy.55
  78.2 0.0 all-gather.5.cloned.1.call-update
  78.2 8.8 %shard_map.84 = f32[32,16,128]{2,1,0:T(8,128)} custom-call(s32[2048]{0:T(1024)} %reshape.40.idx_ref, bf16[32,16,128]{2,1,0:T(8,128)(2,1)} %get-tuple-element.5.x_ref, bf16[4096,64]{1,0:T(8,128)(2,1)} %bitcast.33), custom_call_target="tpu_custom_call" | custom-call | tf_op jit(solution)/shard_map/pallas_call | solution.py:79
  87.0 16.9 %all_to_all.16 = f32[32,16,128]{2,1,0:T(8,128)S(1)} all-to-all(f32[32,16,128]{2,1,0:T(8,128)} %shard_map.84), channel_id=1, replica_groups=mesh['up'=32,'down'=8] {'up'}, dimensions={0} | all-to-all | bytes 524288 | tf_op jit(solution)/shard_map/all_to_all | solution.py:130
  103.9 0.1 copy.53
  104.1 0.0 all-gather.5.cloned.1.call-done.g_ref
  104.1 5.7 %shard_map.85 = f32[128,512]{1,0:T(8,128)} custom-call(s32[256]{0:T(256)} %reshape.36.idx_ref, bf16[32,128,128]{2,1,0:T(8,128)(2,1)} %all-gather.5.cloned.1.call-done.g_ref, bf16[4096,64]{1,0:T(8,128)(2,1)} %bitcast.31), custom_call_target="tpu_custom_call" | custom-call | tf_op jit(solution)/shard_map/pallas_call | solution.py:94
  109.8 1.8 %fusion.3 = f32[128,512]{1,0:T(8,128)} fusion(f32[128,512]{1,0:T(8,128)S(1)} %copy-done.1, f32[128,512]{1,0:T(8,128)} %shard_map.85, f32[512,128]{0,1:T(8,128)S(1)} %copy.53, s32[128,512]{1,0:T(8,128)S(1)} %copy-done.2, f32[512,128]{0,1:T(8,128)S(1)} %copy.52, f32[128,512]{1,0:T(8,128)S(1)} %copy-done), kind=kLoop, calls=%fused_computation.10 | loop fusion | flops 720896 | bytes 1835008 | tf_op jit(solution)/shard_map/sub | solution.py:149
  (9 shorter events, 0.1 us)
Async XLA Ops:
  6.5 34.8 %all-gather.3.cloned.1.call-start = ((), (), s32[]{:S(2)}) async-start(), calls=%async_computation.3 | async-start | bytes 1179648 | tf_op jit(solution)/shard_map/all_gather | solution.py:134
  8.2 22.9 %copy-start.4 = (bf16[32,64,64]{2,1,0:T(8,128)(2,1)S(1)}, bf16[32,64,64]{2,1,0:T(8,128)(2,1)}, u32[]{:S(2)}) copy-start(bf16[32,64,64]{2,1,0:T(8,128)(2,1)} %param.12) | copy-start | bytes 786436
  10.0 11.5 %copy-start.7 = (s32[64,32]{0,1:T(8,128)S(1)}, s32[64,32]{0,1:T(8,128)}, u32[]{:S(2)}) copy-start(s32[64,32]{0,1:T(8,128)} %param.10) | copy-start | bytes 24580
  10.0 11.5 %copy-start.8 = (s32[64,32]{0,1:T(8,128)S(1)}, s32[64,32]{0,1:T(8,128)}, u32[]{:S(2)}) copy-start(s32[64,32]{0,1:T(8,128)} %param.11) | copy-start | bytes 24580
  10.0 21.2 %all-to-all-start = ((bf16[32,16,128]{2,1,0:T(8,128)(2,1)}), bf16[32,16,128]{2,1,0:T(8,128)(2,1)S(1)}, u32[]{:S(2)}, u32[]{:S(2)}) async-start(bf16[32,16,128]{2,1,0:T(8,128)(2,1)} %bitcast.6), calls=%async_computation | async-start | bytes 262144 | tf_op jit(solution)/shard_map/all_to_all | solution.py:130
  21.4 82.7 %all-gather.5.cloned.1.call-start = ((), (), s32[]{:S(2)}) async-start(), calls=%async_computation.4 | async-start | bytes 1179648 | tf_op jit(solution)/shard_map/all_gather | solution.py:134
  21.6 0.7 copy-start.9
  21.7 0.7 copy-start.10
  31.2 1.3 %copy-start.6 = (bf16[32,16,128]{2,1,0:T(8,128)(2,1)}, bf16[32,16,128]{2,1,0:T(8,128)(2,1)S(1)}, u32[]{:S(2)}) copy-start(bf16[32,16,128]{2,1,0:T(8,128)(2,1)S(1)} %all-to-all-done.x_ref) | copy-start | bytes 393220
  32.5 8.8 %copy-start.5 = (bf16[32,64,64]{2,1,0:T(8,128)(2,1)S(1)}, bf16[32,64,64]{2,1,0:T(8,128)(2,1)}, u32[]{:S(2)}) copy-start(bf16[32,64,64]{2,1,0:T(8,128)(2,1)} %param.15) | copy-start | bytes 786436
  42.6 5.8 %copy-start.1 = (f32[128,512]{1,0:T(8,128)S(1)}, f32[128,512]{1,0:T(8,128)}, u32[]{:S(2)}) copy-start(f32[128,512]{1,0:T(8,128)} %param.8) | copy-start | bytes 786436
  42.6 5.8 %copy-start.2 = (s32[128,512]{1,0:T(8,128)S(1)}, s32[128,512]{1,0:T(8,128)}, u32[]{:S(2)}) copy-start(s32[128,512]{1,0:T(8,128)} %param.9) | copy-start | bytes 786436
  49.4 1.0 copy-start.3
  76.2 0.9 copy-start
Sparse Core Ops, SparseCore 0:
  10.1 28.3 all-gather.2
  78.3 20.4 all-gather.4

commit v4 on v3

--- a/solution.py
+++ b/solution.py
@@ -115,6 +115,18 @@
     down_idx = lax.dynamic_slice_in_dim(
         down_order, lax.axis_index("down") * own_blocks, own_blocks, 0
     ).reshape(-1)
+    down_count = lax.axis_size("down")
+    pairs_per_device = local_cols // LANES
+    split = pairs_per_device // 2
+    pair = down_idx >> 1
+    source, slot = pair // pairs_per_device, pair % pairs_per_device
+    in_second = slot >= split
+    new_pair = jnp.where(
+        in_second,
+        down_count * split + source * (pairs_per_device - split) + slot - split,
+        source * split + slot,
+    )
+    down_idx = new_pair * 2 + (down_idx & 1)
     up_table = doubled_table(up_blocks)
     down_table = doubled_table(down_blocks)
     onsite = coupling * double_occ.astype(jnp.float32) - center
@@ -131,8 +143,11 @@
 
     def down_part(rounded):
         paired = rounded.reshape(local_rows, local_cols // LANES, LANES).transpose(1, 0, 2)
-        gathered = lax.all_gather(paired, "down", axis=0, tiled=True)
-        return down_hop(down_idx, gathered, down_table, local_cols)
+        halves = [
+            lax.all_gather(paired[:split], "down", axis=0, tiled=True),
+            lax.all_gather(paired[split:], "down", axis=0, tiled=True),
+        ]
+        return down_hop(down_idx, jnp.concatenate(halves, axis=0), down_table, local_cols)
 
     rounded0 = amplitudes.astype(jnp.bfloat16)
     up0_cols = up_hop(up_idx, exchange_up(to_columns(rounded0)), up_table)

time: 119 us -> 144 us (1.21)
  blocking collectives: 42 us -> 80.8 us
  between operations: 13.5 us -> 0.19 us
  waiting for transfers between devices: 7.96 us -> 0.01 us
  starting transfers between devices: 11.4 us -> 16.5 us
  other arithmetic: 3.88 us -> 6.66 us
  local copies, waits for them, and re-layouts: 10.6 us -> 8.99 us
    all_gather x0 -> x4, blocking collectives: none -> 52.9 us  [the longest x2 26.6 us: down_part(): lax.all_gather(paired[split:], 'down', axis=0, tiled=True)]
    all_to_all x2 -> x1, blocking collectives: 42 us -> 27.9 us  [exchange_up(): return lax.all_to_all(pieces, 'up', 0, 0, tiled=True)]
    all_to_all x1 -> x2, waiting for transfers between devices: 7.9 us -> 0.01 us  [exchange_up(): return lax.all_to_all(pieces, 'up', 0, 0, tiled=True)]
    all_to_all x1 -> x2, starting transfers between devices: 11.4 us -> 16.5 us  [exchange_up(): return lax.all_to_all(pieces, 'up', 0, 0, tiled=True)]
    transpose x2 -> x0, local copies, waits for them, and re-layouts: 2.5 us -> none  [down_part(): rounded.reshape(local_rows, local_cols // LANES, LANES).transpose(1, 0, 2)]
    concatenate x0 -> x2, other arithmetic: none -> 2.18 us  [down_part(): jnp.concatenate(halves, axis=0)]
    unnamed x23 -> x26, local copies, waits for them, and re-layouts: 3.43 us -> 3.53 us
  transfers between devices with their start and end apart: 3 -> 2, of which waited for: 1 -> 0; matrix products, arithmetic and copies ran while one was open for 3% -> 6% of each run, Pallas kernels for 15% -> 8%
where the time goes in v4:
time: 144 us; the launch traced here: 142 us
  blocking collectives  80.8 us (56%)
  Pallas kernels  29.1 us (20%)
  starting transfers between devices  16.5 us (11%)
  local copies, waits for them, and re-layouts  8.99 us (6%)
  other arithmetic  6.66 us (5%)
    all_to_all x1, blocking collectives, exchange_up(): return lax.all_to_all(pieces, 'up', 0, 0, tiled=True)  27.9 us
    all_gather x2, blocking collectives, down_part(): lax.all_gather(paired[split:], 'down', axis=0, tiled=True)  26.6 us
    all_gather x2, blocking collectives, down_part(): lax.all_gather(paired[:split], 'down', axis=0, tiled=True)  26.4 us
    pallas_call x2, Pallas kernels, up_hop(): pl.pallas_call(up_kernel, out_shape=jax.ShapeDtypeStruct((pairs, n, LANES...  17.5 us
    all_to_all x2, starting transfers between devices, exchange_up(): return lax.all_to_all(pieces, 'up', 0, 0, tiled=True)  16.5 us
    pallas_call x2, Pallas kernels, down_hop(): pl.pallas_call(down_kernel, out_shape=jax.ShapeDtypeStruct((rows, own_col...  11.5 us
    unnamed x26, local copies, waits for them, and re-layouts  3.53 us
  transfers between devices with their start and end apart: 2, of which 0 were waited for; matrix products, arithmetic and copies ran while one was open for 6% of the time, Pallas kernels for 8%

profile of v4, /device:TPU:32, one launch (start us, length us, event | category | flops | bytes accessed | tf_op | source)
XLA Modules:
  0.0 142.2 jit_solution(1288902302253318661)
XLA Ops:
  0.0 1.7 %copy.64 = bf16[128,512]{0,1:T(8,128)(2,1)} copy(f32[128,512]{1,0:T(8,128)} %param.8) | data formatting | bytes 393216 | tf_op args[0]
  1.7 11.5 %all-to-all-start = ((bf16[32,16,128]{2,1,0:T(8,128)(2,1)}), bf16[32,16,128]{2,1,0:T(8,128)(2,1)S(1)}, u32[]{:S(2)}, u32[]{:S(2)}) async-start(bf16[32,16,128]{2,1,0:T(8,128)(2,1)} %bitcast.7), calls=%async_computation | async-start | bytes 262144 | tf_op jit(solution)/shard_map/all_to_all | solution.py:142
  13.2 0.0 copy-done.8
  13.2 0.0 copy-done.9
  13.2 0.1 select_reduce_fusion.1
  13.3 0.1 constant_dynamic-slice_fusion
  13.4 0.1 copy.74
  13.5 0.1 shift_right_arithmetic.7
  13.6 0.1 and.20
  13.6 0.9 fusion.10
  14.5 0.1 copy.65
  14.7 0.1 copy.66
  14.8 13.5 %all_gather.13 = bf16[16,128,128]{2,1,0:T(8,128)(2,1)S(1)} all-gather(bf16[2,128,128]{2,1,0:T(8,128)(2,1)S(1)} %copy.66), channel_id=1, replica_groups=mesh['up'=32,'down'=8] {'down'}, dimensions={0}, use_global_device_ids=true | all-gather | bytes 589824 | tf_op jit(solution)/shard_map/all_gather | solution.py:148
  28.3 13.1 %all_gather.12 = bf16[16,128,128]{2,1,0:T(8,128)(2,1)S(1)} all-gather(bf16[2,128,128]{2,1,0:T(8,128)(2,1)S(1)} %copy.65), channel_id=1, replica_groups=mesh['up'=32,'down'=8] {'down'}, dimensions={0}, use_global_device_ids=true | all-gather | bytes 589824 | tf_op jit(solution)/shard_map/all_gather | solution.py:147
  41.4 0.6 fusion.7.idx_ref
  41.9 1.1 pad_maximum_fusion.g_ref
  43.0 0.0 copy-done.10
  43.0 0.1 select_reduce_fusion
  43.1 0.1 copy.68
  43.2 0.7 reshape.41.idx_ref
  43.9 1.3 broadcast_in_dim.38
  45.2 5.8 %shard_map.82 = f32[128,512]{1,0:T(8,128)} custom-call(s32[256]{0:T(256)} %fusion.7.idx_ref, bf16[32,128,128]{2,1,0:T(8,128)(2,1)} %pad_maximum_fusion.g_ref, bf16[4096,64]{1,0:T(8,128)(2,1)} %bitcast.30), custom_call_target="tpu_custom_call" | custom-call | tf_op jit(solution)/shard_map/pallas_call | solution.py:94
  51.0 1.0 fusion.8
  52.0 0.0 copy-start.6
  52.0 0.1 copy.67
  52.2 0.0 all-to-all-done.x_ref
  52.2 0.9 copy-done.6
  53.1 1.3 broadcast_in_dim.40
  54.4 8.8 %shard_map.83 = f32[32,16,128]{2,1,0:T(8,128)} custom-call(s32[2048]{0:T(1024)} %reshape.41.idx_ref, bf16[32,16,128]{2,1,0:T(8,128)(2,1)} %copy-done.7, bf16[4096,64]{1,0:T(8,128)(2,1)} %bitcast.32), custom_call_target="tpu_custom_call" | custom-call | tf_op jit(solution)/shard_map/pallas_call | solution.py:79
  63.1 1.0 pad_maximum_fusion.2
  64.1 0.0 copy-start.3
  64.2 27.9 %all_to_all.15 = f32[32,32,128]{2,1,0:T(8,128)S(1)} all-to-all(f32[32,32,128]{2,1,0:T(8,128)S(1)} %pad_maximum_fusion.2), channel_id=1, replica_groups=mesh['up'=32,'down'=8] {'up'}, dimensions={0} | all-to-all | bytes 1048576 | tf_op jit(solution)/shard_map/all_to_all | solution.py:142
  92.0 0.7 fusion.1
  92.7 8.8 %shard_map.84 = f32[32,16,128]{2,1,0:T(8,128)} custom-call(s32[2048]{0:T(1024)} %reshape.41.idx_ref, bf16[32,16,128]{2,1,0:T(8,128)(2,1)} %get-tuple-element.5.x_ref, bf16[4096,64]{1,0:T(8,128)(2,1)} %bitcast.33), custom_call_target="tpu_custom_call" | custom-call | tf_op jit(solution)/shard_map/pallas_call | solution.py:79
  101.5 0.1 copy.69
  101.6 5.0 %all-to-all-start.2 = ((f32[32,16,128]{2,1,0:T(8,128)}), f32[32,16,128]{2,1,0:T(8,128)S(1)}, u32[]{:S(2)}, u32[]{:S(2)}) async-start(f32[32,16,128]{2,1,0:T(8,128)} %shard_map.84), calls=%async_computation.2 | async-start | bytes 524288 | tf_op jit(solution)/shard_map/all_to_all | solution.py:142
  106.6 0.1 fusion.5
  106.7 0.1 copy.71
  106.9 0.1 copy.72
  107.0 0.1 copy.73
  107.1 13.1 %all_gather.15 = bf16[16,128,128]{2,1,0:T(8,128)(2,1)S(1)} all-gather(bf16[2,128,128]{2,1,0:T(8,128)(2,1)S(1)} %copy.73), channel_id=1, replica_groups=mesh['up'=32,'down'=8] {'down'}, dimensions={0}, use_global_device_ids=true | all-gather | bytes 589824 | tf_op jit(solution)/shard_map/all_gather | solution.py:148
  120.3 13.3 %all_gather.14 = bf16[16,128,128]{2,1,0:T(8,128)(2,1)S(1)} all-gather(bf16[2,128,128]{2,1,0:T(8,128)(2,1)S(1)} %copy.72), channel_id=1, replica_groups=mesh['up'=32,'down'=8] {'down'}, dimensions={0}, use_global_device_ids=true | all-gather | bytes 589824 | tf_op jit(solution)/shard_map/all_gather | solution.py:147
  133.5 1.1 pad_maximum_fusion.1.g_ref
  134.6 5.7 %shard_map.85 = f32[128,512]{1,0:T(8,128)} custom-call(s32[256]{0:T(256)} %fusion.7.idx_ref, bf16[32,128,128]{2,1,0:T(8,128)(2,1)} %pad_maximum_fusion.1.g_ref, bf16[4096,64]{1,0:T(8,128)(2,1)} %bitcast.31), custom_call_target="tpu_custom_call" | custom-call | tf_op jit(solution)/shard_map/pallas_call | solution.py:94
  140.4 0.0 all-to-all-done.2
  140.4 0.1 copy.70
  140.5 0.8 copy-done.4
  141.3 0.9 fusion.3
  (19 shorter events, 0.0 us)
Async XLA Ops:
  1.7 11.5 %copy-start.8 = (s32[64,32]{0,1:T(8,128)S(1)}, s32[64,32]{0,1:T(8,128)}, u32[]{:S(2)}) copy-start(s32[64,32]{0,1:T(8,128)} %param.13) | copy-start | bytes 24580
  1.7 11.5 %copy-start.9 = (s32[64,32]{0,1:T(8,128)S(1)}, s32[64,32]{0,1:T(8,128)}, u32[]{:S(2)}) copy-start(s32[64,32]{0,1:T(8,128)} %param.14) | copy-start | bytes 24580
  1.7 50.4 %all-to-all-start = ((bf16[32,16,128]{2,1,0:T(8,128)(2,1)}), bf16[32,16,128]{2,1,0:T(8,128)(2,1)S(1)}, u32[]{:S(2)}, u32[]{:S(2)}) async-start(bf16[32,16,128]{2,1,0:T(8,128)(2,1)} %bitcast.7), calls=%async_computation | async-start | bytes 262144 | tf_op jit(solution)/shard_map/all_to_all | solution.py:142
  41.9 1.1 copy-start.10
  41.9 1.1 copy-start.11
  41.9 2.0 %copy-start.5 = (bf16[32,64,64]{2,1,0:T(8,128)(2,1)S(1)}, bf16[32,64,64]{2,1,0:T(8,128)(2,1)}, u32[]{:S(2)}) copy-start(bf16[32,64,64]{2,1,0:T(8,128)(2,1)} %param.15) | copy-start | bytes 786436
  45.2 5.8 %copy-start.1 = (f32[128,512]{1,0:T(8,128)S(1)}, f32[128,512]{1,0:T(8,128)}, u32[]{:S(2)}) copy-start(f32[128,512]{1,0:T(8,128)} %param.8) | copy-start | bytes 786436
  45.2 5.8 %copy-start.2 = (s32[128,512]{1,0:T(8,128)S(1)}, s32[128,512]{1,0:T(8,128)}, u32[]{:S(2)}) copy-start(s32[128,512]{1,0:T(8,128)} %param.9) | copy-start | bytes 786436
  52.0 1.0 copy-start.6
  53.1 1.3 copy-start.7
  64.1 27.9 %copy-start.3 = (f32[32,16,128]{2,1,0:T(8,128)S(1)}, f32[32,16,128]{2,1,0:T(8,128)}, u32[]{:S(2)}) copy-start(f32[32,16,128]{2,1,0:T(8,128)} %shard_map.83) | copy-start | bytes 786436
  101.6 5.0 %copy-start = (f32[128,512]{1,0:T(8,128)S(1)}, f32[128,512]{1,0:T(8,128)}, u32[]{:S(2)}) copy-start(f32[128,512]{1,0:T(8,128)} %shard_map.82) | copy-start | bytes 786436
  101.6 38.7 %all-to-all-start.2 = ((f32[32,16,128]{2,1,0:T(8,128)}), f32[32,16,128]{2,1,0:T(8,128)S(1)}, u32[]{:S(2)}, u32[]{:S(2)}) async-start(f32[32,16,128]{2,1,0:T(8,128)} %shard_map.84), calls=%async_computation.2 | async-start | bytes 524288 | tf_op jit(solution)/shard_map/all_to_all | solution.py:142
  140.4 1.0 copy-start.4

commit v5 on v3

--- a/solution.py
+++ b/solution.py
@@ -17,36 +17,40 @@
     return jnp.sum(jnp.where(matched, block_cols[:, :, None], 0), axis=1)
 
 
-def doubled_table(shared_table):
-    shared_count, block_width, _ = shared_table.shape
-    wide = jnp.broadcast_to(shared_table[:, None], (shared_count, 2, block_width, block_width))
-    return wide.reshape(shared_count * 2 * block_width, block_width)
+def _fill_rolled(src_ref, src2_ref):
+    half = src_ref.shape[-1] // 2
+
+    def one(i, carry):
+        piece = src_ref[i]
+        src2_ref[0, i] = piece
+        src2_ref[1, i] = pltpu.roll(piece, half, 1)
+        return carry
+
+    lax.fori_loop(0, src_ref.shape[0], one, 0)
 
 
-def _stage_row(idx_ref, base, src_ref, stage_ref, row0, rows, shared_count, half_of_lane):
-    for s in range(shared_count):
-        c = idx_ref[base + s]
-        piece = src_ref[lax.shift_right_logical(c, 1)]
-        keep = half_of_lane == (c & 1)
-        stage_ref[row0:row0 + rows, s * LANES:(s + 1) * LANES] = jnp.where(
-            keep, piece, jnp.zeros_like(piece)
-        )
+def _stage_row(idx_ref, base, src2_ref, stage_ref, row0, rows, shared_count, low_lanes):
+    for t in range(shared_count // 2):
+        ce = idx_ref[base + 2 * t]
+        co = idx_ref[base + 2 * t + 1]
+        even = src2_ref[ce & 1, lax.shift_right_logical(ce, 1)]
+        odd = src2_ref[(co & 1) ^ 1, lax.shift_right_logical(co, 1)]
+        stage_ref[row0:row0 + rows, t * LANES:(t + 1) * LANES] = jnp.where(low_lanes, even, odd)
 
 
-def up_kernel(idx_ref, x_ref, w_ref, o_ref, stage_ref):
+def up_kernel(idx_ref, x_ref, w_ref, o_ref, src2_ref, stage_ref):
     pairs, n, _ = x_ref.shape
     block_width = w_ref.shape[1]
-    shared_count = w_ref.shape[0] // LANES
+    shared_count = w_ref.shape[0] // block_width
     rows_per_chunk = stage_ref.shape[0] // n
-    half_of_lane = jnp.where(
-        lax.broadcasted_iota(jnp.int32, (n, LANES), 1) >= block_width, 1, 0
-    )
+    low_lanes = lax.broadcasted_iota(jnp.int32, (n, LANES), 1) < block_width
+    _fill_rolled(x_ref, src2_ref)
 
     def chunk(g, carry):
         for rr in range(rows_per_chunk):
             r = g * rows_per_chunk + rr
-            _stage_row(idx_ref, r * shared_count, x_ref, stage_ref, rr * n, n,
-                       shared_count, half_of_lane)
+            _stage_row(idx_ref, r * shared_count, src2_ref, stage_ref, rr * n, n,
+                       shared_count, low_lanes)
         res = jnp.dot(stage_ref[...], w_ref[...], preferred_element_type=jnp.float32)
         for rr in range(0, rows_per_chunk, 2):
             i = (g * rows_per_chunk + rr) // 2
@@ -57,17 +61,16 @@
     lax.fori_loop(0, 2 * pairs // rows_per_chunk, chunk, 0)
 
 
-def down_kernel(idx_ref, g_ref, w_ref, o_ref, stage_ref):
+def down_kernel(idx_ref, g_ref, w_ref, o_ref, src2_ref, stage_ref):
     _, rows, _ = g_ref.shape
     block_width = w_ref.shape[1]
-    shared_count = w_ref.shape[0] // LANES
+    shared_count = w_ref.shape[0] // block_width
     own_blocks = o_ref.shape[1] // block_width
-    half_of_lane = jnp.where(
-        lax.broadcasted_iota(jnp.int32, (rows, LANES), 1) >= block_width, 1, 0
-    )
+    low_lanes = lax.broadcasted_iota(jnp.int32, (rows, LANES), 1) < block_width
+    _fill_rolled(g_ref, src2_ref)
     for r in range(own_blocks):
-        _stage_row(idx_ref, r * shared_count, g_ref, stage_ref, 0, rows,
-                   shared_count, half_of_lane)
+        _stage_row(idx_ref, r * shared_count, src2_ref, stage_ref, 0, rows,
+                   shared_count, low_lanes)
         o_ref[:, r * block_width:(r + 1) * block_width] = jnp.dot(
             stage_ref[...], w_ref[...], preferred_element_type=jnp.float32
         )
@@ -85,7 +88,10 @@
             pl.BlockSpec(memory_space=pltpu.VMEM),
         ],
         out_specs=pl.BlockSpec(memory_space=pltpu.VMEM),
-        scratch_shapes=[pltpu.VMEM((rows_per_chunk * n, w.shape[0]), jnp.bfloat16)],
+        scratch_shapes=[
+            pltpu.VMEM((2,) + x.shape, jnp.bfloat16),
+            pltpu.VMEM((rows_per_chunk * n, w.shape[0]), jnp.bfloat16),
+        ],
     )(idx, x, w)
 
 
@@ -100,7 +106,10 @@
             pl.BlockSpec(memory_space=pltpu.VMEM),
         ],
         out_specs=pl.BlockSpec(memory_space=pltpu.VMEM),
-        scratch_shapes=[pltpu.VMEM((rows, w.shape[0]), jnp.bfloat16)],
+        scratch_shapes=[
+            pltpu.VMEM((2,) + g.shape, jnp.bfloat16),
+            pltpu.VMEM((rows, w.shape[0]), jnp.bfloat16),
+        ],
     )(idx, g, w)
 
 
@@ -115,8 +124,8 @@
     down_idx = lax.dynamic_slice_in_dim(
         down_order, lax.axis_index("down") * own_blocks, own_blocks, 0
     ).reshape(-1)
-    up_table = doubled_table(up_blocks)
-    down_table = doubled_table(down_blocks)
+    up_table = up_blocks.reshape(shared_count * block_width, block_width)
+    down_table = down_blocks.reshape(shared_count * block_width, block_width)
     onsite = coupling * double_occ.astype(jnp.float32) - center
     col_chunk = local_cols // up_count
 

time: 119 us -> 122 us (1.025)
  Pallas kernels: 29.1 us -> 35.7 us
  local copies, waits for them, and re-layouts: 10.6 us -> 8.48 us
  blocking collectives: 42 us -> 40.5 us
    pallas_call x2, Pallas kernels: 17.6 us -> 22.1 us  [up_hop(): pl.pallas_call(up_kernel, out_shape=jax.ShapeDtypeStruct((pairs, n, LANES...]
    broadcast_in_dim x2 -> x0, local copies, waits for them, and re-layouts: 2.6 us -> none  [doubled_table(): jnp.broadcast_to(shared_table[:, None], (shared_count, 2, block_width, bl...]
    pallas_call x2, Pallas kernels: 11.5 us -> 13.5 us  [down_hop(): pl.pallas_call(down_kernel, out_shape=jax.ShapeDtypeStruct((rows, own_col...]
    all_to_all x2, blocking collectives: 42 us -> 40.5 us  [exchange_up(): return lax.all_to_all(pieces, 'up', 0, 0, tiled=True)]
    unnamed x23 -> x19, local copies, waits for them, and re-layouts: 3.43 us -> 4.02 us
  transfers between devices with their start and end apart: 3 -> 3, of which waited for: 1 -> 1; matrix products, arithmetic and copies ran while one was open for 3% -> 2% of each run, Pallas kernels for 15% -> 18%
where the time goes in v5:
time: 122 us; the launch traced here: 121 us
  blocking collectives  40.5 us (33%)
  Pallas kernels  35.7 us (29%)
  between operations  13.5 us (11%)
  starting transfers between devices  11.4 us (9%)
  local copies, waits for them, and re-layouts  8.48 us (7%)
  waiting for transfers between devices  8 us (7%)
  other arithmetic  3.88 us (3%)
    all_to_all x2, blocking collectives, exchange_up(): return lax.all_to_all(pieces, 'up', 0, 0, tiled=True)  40.5 us
    pallas_call x2, Pallas kernels, up_hop(): pl.pallas_call(up_kernel, out_shape=jax.ShapeDtypeStruct((pairs, n, LANES...  22.1 us
    pallas_call x2, Pallas kernels, down_hop(): pl.pallas_call(down_kernel, out_shape=jax.ShapeDtypeStruct((rows, own_col...  13.5 us
    all_to_all x1, starting transfers between devices, exchange_up(): return lax.all_to_all(pieces, 'up', 0, 0, tiled=True)  11.4 us
    all_to_all x1, waiting for transfers between devices, exchange_up(): return lax.all_to_all(pieces, 'up', 0, 0, tiled=True)  7.95 us
    unnamed x19, local copies, waits for them, and re-layouts  4.02 us
  transfers between devices with their start and end apart: 3, of which 1 were waited for; matrix products, arithmetic and copies ran while one was open for 2% of the time, Pallas kernels for 18%

profile of v5, /device:TPU:32, one launch (start us, length us, event | category | flops | bytes accessed | tf_op | source)
XLA Modules:
  0.0 121.4 jit_solution(5892821757982552574)
XLA Ops:
  6.5 0.0 all-gather.3.cloned.1.call-start
  6.5 1.7 %copy.48 = bf16[128,512]{0,1:T(8,128)(2,1)} copy(f32[128,512]{1,0:T(8,128)} %param.8) | data formatting | bytes 393216 | tf_op args[0]
  8.2 1.7 %copy.49 = bf16[4,128,128]{2,1,0:T(8,128)(2,1)} copy(bf16[4,128,128]{1,2,0:T(8,128)(2,1)} %bitcast.1) | data formatting | bytes 262144 | tf_op jit(solution)/shard_map/transpose | solution.py:142
  9.9 0.0 all-gather.3.cloned.1.call-update
  9.9 0.0 copy-start.5
  9.9 0.0 copy-start.6
  9.9 11.4 %all-to-all-start = ((bf16[32,16,128]{2,1,0:T(8,128)(2,1)}), bf16[32,16,128]{2,1,0:T(8,128)(2,1)S(1)}, u32[]{:S(2)}, u32[]{:S(2)}) async-start(bf16[32,16,128]{2,1,0:T(8,128)(2,1)} %bitcast.6), calls=%async_computation | async-start | bytes 262144 | tf_op jit(solution)/shard_map/all_to_all | solution.py:139
  21.3 0.0 all-gather.5.cloned.1.call-start
  21.4 0.0 copy-done.5
  21.4 0.0 copy-done.6
  21.4 0.1 select_reduce_fusion.1
  21.5 0.0 copy-start.8
  21.5 0.1 constant_dynamic-slice_fusion
  21.6 0.0 copy-start.7
  21.6 0.1 copy.47
  21.7 0.7 reshape.34.idx_ref
  22.3 0.0 copy-done.8
  22.3 0.0 copy-done.7
  22.3 0.1 select_reduce_fusion
  22.4 0.1 copy.51
  22.5 0.7 reshape.38.idx_ref
  23.2 7.9 %all-to-all-done.x_ref = bf16[32,16,128]{2,1,0:T(8,128)(2,1)S(1)} async-done(((bf16[32,16,128]{2,1,0:T(8,128)(2,1)}), bf16[32,16,128]{2,1,0:T(8,128)(2,1)S(1)}, u32[]{:S(2)}, u32[]{:S(2)}) %all-to-all-start) | async-done | bytes 131104 | tf_op jit(solution)/shard_map/all_to_all | solution.py:139
  31.1 0.0 copy-start.4
  31.1 0.7 copy-done.4
  31.8 11.1 %shard_map.83 = f32[32,16,128]{2,1,0:T(8,128)} custom-call(s32[2048]{0:T(1024)} %reshape.38.idx_ref, bf16[32,16,128]{2,1,0:T(8,128)(2,1)} %copy-done.4, bf16[2048,64]{1,0:T(8,128)(2,1)} %bitcast.32), custom_call_target="tpu_custom_call" | custom-call | tf_op jit(solution)/shard_map/pallas_call | solution.py:82
  42.8 0.0 all-gather.3.cloned.1.call-done.g_ref
  42.8 0.0 copy-start.1
  42.8 6.8 %shard_map.82 = f32[128,512]{1,0:T(8,128)} custom-call(s32[256]{0:T(256)} %reshape.34.idx_ref, bf16[32,128,128]{2,1,0:T(8,128)(2,1)} %all-gather.3.cloned.1.call-done.g_ref, bf16[2048,64]{1,0:T(8,128)(2,1)} %bitcast.30), custom_call_target="tpu_custom_call" | custom-call | tf_op jit(solution)/shard_map/pallas_call | solution.py:100
  49.6 0.0 copy-done.1
  49.6 0.0 copy-done.2
  49.7 1.0 fusion.6
  50.7 0.0 copy-start.3
  50.7 0.1 copy.50
  50.8 0.8 copy-done.3
  51.7 23.5 %all_to_all.15 = f32[32,32,128]{2,1,0:T(8,128)S(1)} all-to-all(f32[32,32,128]{2,1,0:T(8,128)S(1)} %pad_maximum_fusion), channel_id=1, replica_groups=mesh['up'=32,'down'=8] {'up'}, dimensions={0} | all-to-all | bytes 1048576 | tf_op jit(solution)/shard_map/all_to_all | solution.py:139
  75.2 0.7 fusion.1
  75.9 0.1 copy.52
  76.1 0.8 copy-done
  76.9 0.1 fusion.5
  77.0 0.1 copy.54
  77.1 0.8 copy.55
  77.9 0.0 all-gather.5.cloned.1.call-update
  77.9 11.1 %shard_map.84 = f32[32,16,128]{2,1,0:T(8,128)} custom-call(s32[2048]{0:T(1024)} %reshape.38.idx_ref, bf16[32,16,128]{2,1,0:T(8,128)(2,1)} %get-tuple-element.5.x_ref, bf16[2048,64]{1,0:T(8,128)(2,1)} %bitcast.33), custom_call_target="tpu_custom_call" | custom-call | tf_op jit(solution)/shard_map/pallas_call | solution.py:82
  89.0 16.9 %all_to_all.16 = f32[32,16,128]{2,1,0:T(8,128)S(1)} all-to-all(f32[32,16,128]{2,1,0:T(8,128)} %shard_map.84), channel_id=1, replica_groups=mesh['up'=32,'down'=8] {'up'}, dimensions={0} | all-to-all | bytes 524288 | tf_op jit(solution)/shard_map/all_to_all | solution.py:139
  105.9 0.1 copy.53
  106.0 0.0 all-gather.5.cloned.1.call-done.g_ref
  106.0 6.7 %shard_map.85 = f32[128,512]{1,0:T(8,128)} custom-call(s32[256]{0:T(256)} %reshape.34.idx_ref, bf16[32,128,128]{2,1,0:T(8,128)(2,1)} %all-gather.5.cloned.1.call-done.g_ref, bf16[2048,64]{1,0:T(8,128)(2,1)} %bitcast.31), custom_call_target="tpu_custom_call" | custom-call | tf_op jit(solution)/shard_map/pallas_call | solution.py:100
  112.8 1.8 %fusion.3 = f32[128,512]{1,0:T(8,128)} fusion(f32[128,512]{1,0:T(8,128)S(1)} %copy-done.1, f32[128,512]{1,0:T(8,128)} %shard_map.85, f32[512,128]{0,1:T(8,128)S(1)} %copy.53, s32[128,512]{1,0:T(8,128)S(1)} %copy-done.2, f32[512,128]{0,1:T(8,128)S(1)} %copy.52, f32[128,512]{1,0:T(8,128)S(1)} %copy-done), kind=kLoop, calls=%fused_computation.10 | loop fusion | flops 720896 | bytes 1835008 | tf_op jit(solution)/shard_map/sub | solution.py:158
  (3 shorter events, 0.1 us)
Async XLA Ops:
  6.5 36.3 %all-gather.3.cloned.1.call-start = ((), (), s32[]{:S(2)}) async-start(), calls=%async_computation.3 | async-start | bytes 1179648 | tf_op jit(solution)/shard_map/all_gather | solution.py:143
  9.9 11.5 %copy-start.5 = (s32[64,32]{0,1:T(8,128)S(1)}, s32[64,32]{0,1:T(8,128)}, u32[]{:S(2)}) copy-start(s32[64,32]{0,1:T(8,128)} %param.13) | copy-start | bytes 24580
  9.9 11.5 %copy-start.6 = (s32[64,32]{0,1:T(8,128)S(1)}, s32[64,32]{0,1:T(8,128)}, u32[]{:S(2)}) copy-start(s32[64,32]{0,1:T(8,128)} %param.14) | copy-start | bytes 24580
  9.9 21.2 %all-to-all-start = ((bf16[32,16,128]{2,1,0:T(8,128)(2,1)}), bf16[32,16,128]{2,1,0:T(8,128)(2,1)S(1)}, u32[]{:S(2)}, u32[]{:S(2)}) async-start(bf16[32,16,128]{2,1,0:T(8,128)(2,1)} %bitcast.6), calls=%async_computation | async-start | bytes 262144 | tf_op jit(solution)/shard_map/all_to_all | solution.py:139
  21.3 84.7 %all-gather.5.cloned.1.call-start = ((), (), s32[]{:S(2)}) async-start(), calls=%async_computation.4 | async-start | bytes 1179648 | tf_op jit(solution)/shard_map/all_gather | solution.py:143
  21.5 0.8 copy-start.8
  21.6 0.7 copy-start.7
  31.1 0.7 copy-start.4
  42.8 6.8 %copy-start.1 = (f32[128,512]{1,0:T(8,128)S(1)}, f32[128,512]{1,0:T(8,128)}, u32[]{:S(2)}) copy-start(f32[128,512]{1,0:T(8,128)} %param.8) | copy-start | bytes 786436
  42.8 6.8 %copy-start.2 = (s32[128,512]{1,0:T(8,128)S(1)}, s32[128,512]{1,0:T(8,128)}, u32[]{:S(2)}) copy-start(s32[128,512]{1,0:T(8,128)} %param.9) | copy-start | bytes 786436
  50.7 1.0 copy-start.3
  75.9 0.9 copy-start
Sparse Core Ops, SparseCore 0:
  10.0 28.3 all-gather.2
  78.0 20.4 all-gather.4

commit v6 on v5

--- a/solution.py
+++ b/solution.py
@@ -18,24 +18,29 @@
 
 
 def _fill_rolled(src_ref, src2_ref):
+    pairs = src_ref.shape[0]
     half = src_ref.shape[-1] // 2
 
     def one(i, carry):
         piece = src_ref[i]
-        src2_ref[0, i] = piece
-        src2_ref[1, i] = pltpu.roll(piece, half, 1)
+        src2_ref[i] = piece
+        src2_ref[pairs + i] = pltpu.roll(piece, half, 1)
         return carry
 
-    lax.fori_loop(0, src_ref.shape[0], one, 0)
+    lax.fori_loop(0, pairs, one, 0)
 
 
-def _stage_row(idx_ref, base, src2_ref, stage_ref, row0, rows, shared_count, low_lanes):
+def _stage_row(idx_ref, base, src2_ref, stage_ref, row0, rows, shared_count, half):
     for t in range(shared_count // 2):
-        ce = idx_ref[base + 2 * t]
-        co = idx_ref[base + 2 * t + 1]
-        even = src2_ref[ce & 1, lax.shift_right_logical(ce, 1)]
-        odd = src2_ref[(co & 1) ^ 1, lax.shift_right_logical(co, 1)]
-        stage_ref[row0:row0 + rows, t * LANES:(t + 1) * LANES] = jnp.where(low_lanes, even, odd)
+        even = idx_ref[base + 2 * t]
+        odd = idx_ref[base + 2 * t + 1]
+        stage_ref[row0:row0 + rows, t * LANES:t * LANES + half] = src2_ref[even, :, 0:half]
+        stage_ref[row0:row0 + rows, t * LANES + half:(t + 1) * LANES] = src2_ref[odd, :, half:LANES]
+
+
+def source_index(order, pairs):
+    parity = jnp.arange(order.shape[-1], dtype=jnp.int32) % 2
+    return ((order & 1) ^ parity) * pairs + (order >> 1)
 
 
 def up_kernel(idx_ref, x_ref, w_ref, o_ref, src2_ref, stage_ref):
@@ -43,14 +48,13 @@
     block_width = w_ref.shape[1]
     shared_count = w_ref.shape[0] // block_width
     rows_per_chunk = stage_ref.shape[0] // n
-    low_lanes = lax.broadcasted_iota(jnp.int32, (n, LANES), 1) < block_width
     _fill_rolled(x_ref, src2_ref)
 
     def chunk(g, carry):
         for rr in range(rows_per_chunk):
             r = g * rows_per_chunk + rr
             _stage_row(idx_ref, r * shared_count, src2_ref, stage_ref, rr * n, n,
-                       shared_count, low_lanes)
+                       shared_count, block_width)
         res = jnp.dot(stage_ref[...], w_ref[...], preferred_element_type=jnp.float32)
         for rr in range(0, rows_per_chunk, 2):
             i = (g * rows_per_chunk + rr) // 2
@@ -66,11 +70,10 @@
     block_width = w_ref.shape[1]
     shared_count = w_ref.shape[0] // block_width
     own_blocks = o_ref.shape[1] // block_width
-    low_lanes = lax.broadcasted_iota(jnp.int32, (rows, LANES), 1) < block_width
     _fill_rolled(g_ref, src2_ref)
     for r in range(own_blocks):
         _stage_row(idx_ref, r * shared_count, src2_ref, stage_ref, 0, rows,
-                   shared_count, low_lanes)
+                   shared_count, block_width)
         o_ref[:, r * block_width:(r + 1) * block_width] = jnp.dot(
             stage_ref[...], w_ref[...], preferred_element_type=jnp.float32
         )
@@ -89,7 +92,7 @@
         ],
         out_specs=pl.BlockSpec(memory_space=pltpu.VMEM),
         scratch_shapes=[
-            pltpu.VMEM((2,) + x.shape, jnp.bfloat16),
+            pltpu.VMEM((2 * pairs, n, LANES), jnp.bfloat16),
             pltpu.VMEM((rows_per_chunk * n, w.shape[0]), jnp.bfloat16),
         ],
     )(idx, x, w)
@@ -107,7 +110,7 @@
         ],
         out_specs=pl.BlockSpec(memory_space=pltpu.VMEM),
         scratch_shapes=[
-            pltpu.VMEM((2,) + g.shape, jnp.bfloat16),
+            pltpu.VMEM((2 * g.shape[0], rows, LANES), jnp.bfloat16),
             pltpu.VMEM((rows, w.shape[0]), jnp.bfloat16),
         ],
     )(idx, g, w)
@@ -119,11 +122,11 @@
     local_rows, local_cols = amplitudes.shape
     up_count = lax.axis_size("up")
     own_blocks = local_cols // block_width
-    up_idx = block_order(up_cols, up_ids, shared_count).reshape(-1)
+    up_idx = source_index(block_order(up_cols, up_ids, shared_count), up_count).reshape(-1)
     down_order = block_order(down_cols, down_ids, shared_count)
-    down_idx = lax.dynamic_slice_in_dim(
+    down_idx = source_index(lax.dynamic_slice_in_dim(
         down_order, lax.axis_index("down") * own_blocks, own_blocks, 0
-    ).reshape(-1)
+    ), lax.axis_size("down") * local_cols // LANES).reshape(-1)
     up_table = up_blocks.reshape(shared_count * block_width, block_width)
     down_table = down_blocks.reshape(shared_count * block_width, block_width)
     onsite = coupling * double_occ.astype(jnp.float32) - center

time: 122 us -> 121 us (level)
  Pallas kernels: 35.7 us -> 32.2 us
  blocking collectives: 40.5 us -> 42.6 us
    pallas_call x2, Pallas kernels: 22.1 us -> 18 us  [up_hop(): pl.pallas_call(up_kernel, out_shape=jax.ShapeDtypeStruct((pairs, n, LANES...]
    all_to_all x2, blocking collectives: 40.5 us -> 42.6 us  [exchange_up(): return lax.all_to_all(pieces, 'up', 0, 0, tiled=True)]
    unnamed x19 -> x20, local copies, waits for them, and re-layouts: 4.02 us -> 4.72 us
  transfers between devices with their start and end apart: 3 -> 3, of which waited for: 1 -> 1; matrix products, arithmetic and copies ran while one was open for 2% -> 2% of each run, Pallas kernels for 18% -> 15%
where the time goes in v6:
time: 121 us; the launch traced here: 120 us
  blocking collectives  42.6 us (35%)
  Pallas kernels  32.2 us (27%)
  between operations  13.5 us (11%)
  starting transfers between devices  11.4 us (9%)
  local copies, waits for them, and re-layouts  9.11 us (8%)
  waiting for transfers between devices  7.29 us (6%)
  other arithmetic  3.97 us (3%)
    all_to_all x2, blocking collectives, exchange_up(): return lax.all_to_all(pieces, 'up', 0, 0, tiled=True)  42.6 us
    pallas_call x2, Pallas kernels, up_hop(): pl.pallas_call(up_kernel, out_shape=jax.ShapeDtypeStruct((pairs, n, LANES...  18 us
    pallas_call x2, Pallas kernels, down_hop(): pl.pallas_call(down_kernel, out_shape=jax.ShapeDtypeStruct((rows, own_col...  14.3 us
    all_to_all x1, starting transfers between devices, exchange_up(): return lax.all_to_all(pieces, 'up', 0, 0, tiled=True)  11.4 us
    all_to_all x1, waiting for transfers between devices, exchange_up(): return lax.all_to_all(pieces, 'up', 0, 0, tiled=True)  7.23 us
    unnamed x20, local copies, waits for them, and re-layouts  4.72 us
    transpose x2, local copies, waits for them, and re-layouts, down_part(): rounded.reshape(local_rows, local_cols // LANES, LANES).transpose(1, 0, 2)  2.42 us
  transfers between devices with their start and end apart: 3, of which 1 were waited for; matrix products, arithmetic and copies ran while one was open for 2% of the time, Pallas kernels for 15%

profile of v6, /device:TPU:32, one launch (start us, length us, event | category | flops | bytes accessed | tf_op | source)
XLA Modules:
  0.0 120.1 jit_solution(12540682729851764984)
XLA Ops:
  6.5 0.0 all-gather.3.cloned.1.call-start
  6.5 1.7 %copy.57 = bf16[128,512]{0,1:T(8,128)(2,1)} copy(f32[128,512]{1,0:T(8,128)} %param.8) | data formatting | bytes 393216 | tf_op args[0]
  8.2 1.7 %copy.58 = bf16[4,128,128]{2,1,0:T(8,128)(2,1)} copy(bf16[4,128,128]{1,2,0:T(8,128)(2,1)} %bitcast.1) | data formatting | bytes 262144 | tf_op jit(solution)/shard_map/transpose | solution.py:145
  9.9 0.0 all-gather.3.cloned.1.call-update
  9.9 0.0 copy-start.5
  9.9 0.0 copy-start.6
  9.9 11.4 %all-to-all-start = ((bf16[32,16,128]{2,1,0:T(8,128)(2,1)}), bf16[32,16,128]{2,1,0:T(8,128)(2,1)S(1)}, u32[]{:S(2)}, u32[]{:S(2)}) async-start(bf16[32,16,128]{2,1,0:T(8,128)(2,1)} %bitcast.6), calls=%async_computation | async-start | bytes 262144 | tf_op jit(solution)/shard_map/all_to_all | solution.py:142
  21.3 0.0 all-gather.5.cloned.1.call-start
  21.4 0.0 copy-done.5
  21.4 0.0 copy-done.6
  21.4 0.1 select_reduce_fusion.1
  21.5 0.0 copy-start.8
  21.5 0.1 constant_dynamic-slice_fusion
  21.6 0.0 copy-start.7
  21.6 0.1 copy.65
  21.7 0.5 copy-done.8
  22.2 0.1 copy-done.7
  22.3 0.1 select_reduce_fusion
  22.4 0.6 reshape.51.idx_ref
  23.1 0.1 shift-right-arithmetic_add_fusion
  23.1 0.1 copy.60
  23.2 0.7 add.48.idx_ref
  23.9 7.2 %all-to-all-done.x_ref = bf16[32,16,128]{2,1,0:T(8,128)(2,1)S(1)} async-done(((bf16[32,16,128]{2,1,0:T(8,128)(2,1)}), bf16[32,16,128]{2,1,0:T(8,128)(2,1)S(1)}, u32[]{:S(2)}, u32[]{:S(2)}) %all-to-all-start) | async-done | bytes 131104 | tf_op jit(solution)/shard_map/all_to_all | solution.py:142
  31.1 0.0 copy-start.4
  31.1 0.7 copy-done.4
  31.8 9.0 %shard_map.83 = f32[32,16,128]{2,1,0:T(8,128)} custom-call(s32[2048]{0:T(1024)} %add.48.idx_ref, bf16[32,16,128]{2,1,0:T(8,128)(2,1)} %copy-done.4, bf16[2048,64]{1,0:T(8,128)(2,1)} %bitcast.32), custom_call_target="tpu_custom_call" | custom-call | tf_op jit(solution)/shard_map/pallas_call | solution.py:85
  40.7 0.0 all-gather.3.cloned.1.call-done.g_ref
  40.8 7.2 %shard_map.82 = f32[128,512]{1,0:T(8,128)} custom-call(s32[256]{0:T(256)} %reshape.51.idx_ref, bf16[32,128,128]{2,1,0:T(8,128)(2,1)} %all-gather.3.cloned.1.call-done.g_ref, bf16[2048,64]{1,0:T(8,128)(2,1)} %bitcast.30), custom_call_target="tpu_custom_call" | custom-call | tf_op jit(solution)/shard_map/pallas_call | solution.py:103
  47.9 0.0 copy-done.1
  47.9 0.0 copy-done.2
  47.9 1.0 fusion.6
  49.0 0.0 copy-start.3
  49.0 0.1 copy.59
  49.1 0.8 copy-done.3
  50.0 25.6 %all_to_all.15 = f32[32,32,128]{2,1,0:T(8,128)S(1)} all-to-all(f32[32,32,128]{2,1,0:T(8,128)S(1)} %pad_maximum_fusion), channel_id=1, replica_groups=mesh['up'=32,'down'=8] {'up'}, dimensions={0} | all-to-all | bytes 1048576 | tf_op jit(solution)/shard_map/all_to_all | solution.py:142
  75.6 0.7 fusion.1
  76.3 0.1 copy.61
  76.4 0.8 copy-done
  77.3 0.1 fusion.5
  77.4 0.1 copy.63
  77.5 0.8 copy.64
  78.3 0.0 all-gather.5.cloned.1.call-update
  78.3 9.0 %shard_map.84 = f32[32,16,128]{2,1,0:T(8,128)} custom-call(s32[2048]{0:T(1024)} %add.48.idx_ref, bf16[32,16,128]{2,1,0:T(8,128)(2,1)} %get-tuple-element.5.x_ref, bf16[2048,64]{1,0:T(8,128)(2,1)} %bitcast.33), custom_call_target="tpu_custom_call" | custom-call | tf_op jit(solution)/shard_map/pallas_call | solution.py:85
  87.3 16.9 %all_to_all.16 = f32[32,16,128]{2,1,0:T(8,128)S(1)} all-to-all(f32[32,16,128]{2,1,0:T(8,128)} %shard_map.84), channel_id=1, replica_groups=mesh['up'=32,'down'=8] {'up'}, dimensions={0} | all-to-all | bytes 524288 | tf_op jit(solution)/shard_map/all_to_all | solution.py:142
  104.2 0.1 copy.62
  104.3 0.0 all-gather.5.cloned.1.call-done.g_ref
  104.3 7.1 %shard_map.85 = f32[128,512]{1,0:T(8,128)} custom-call(s32[256]{0:T(256)} %reshape.51.idx_ref, bf16[32,128,128]{2,1,0:T(8,128)(2,1)} %all-gather.5.cloned.1.call-done.g_ref, bf16[2048,64]{1,0:T(8,128)(2,1)} %bitcast.31), custom_call_target="tpu_custom_call" | custom-call | tf_op jit(solution)/shard_map/pallas_call | solution.py:103
  111.5 1.8 %fusion.3 = f32[128,512]{1,0:T(8,128)} fusion(f32[128,512]{1,0:T(8,128)S(1)} %copy-done.1, f32[128,512]{1,0:T(8,128)} %shard_map.85, f32[512,128]{0,1:T(8,128)S(1)} %copy.62, s32[128,512]{1,0:T(8,128)S(1)} %copy-done.2, f32[512,128]{0,1:T(8,128)S(1)} %copy.61, f32[128,512]{1,0:T(8,128)S(1)} %copy-done), kind=kLoop, calls=%fused_computation.10 | loop fusion | flops 720896 | bytes 1835008 | tf_op jit(solution)/shard_map/sub | solution.py:161
  (6 shorter events, 0.1 us)
Async XLA Ops:
  6.5 34.2 %all-gather.3.cloned.1.call-start = ((), (), s32[]{:S(2)}) async-start(), calls=%async_computation.3 | async-start | bytes 1179648 | tf_op jit(solution)/shard_map/all_gather | solution.py:146
  9.9 11.5 %copy-start.5 = (s32[64,32]{0,1:T(8,128)S(1)}, s32[64,32]{0,1:T(8,128)}, u32[]{:S(2)}) copy-start(s32[64,32]{0,1:T(8,128)} %param.13) | copy-start | bytes 24580
  9.9 11.5 %copy-start.6 = (s32[64,32]{0,1:T(8,128)S(1)}, s32[64,32]{0,1:T(8,128)}, u32[]{:S(2)}) copy-start(s32[64,32]{0,1:T(8,128)} %param.14) | copy-start | bytes 24580
  9.9 21.2 %all-to-all-start = ((bf16[32,16,128]{2,1,0:T(8,128)(2,1)}), bf16[32,16,128]{2,1,0:T(8,128)(2,1)S(1)}, u32[]{:S(2)}, u32[]{:S(2)}) async-start(bf16[32,16,128]{2,1,0:T(8,128)(2,1)} %bitcast.6), calls=%async_computation | async-start | bytes 262144 | tf_op jit(solution)/shard_map/all_to_all | solution.py:142
  21.3 83.0 %all-gather.5.cloned.1.call-start = ((), (), s32[]{:S(2)}) async-start(), calls=%async_computation.4 | async-start | bytes 1179648 | tf_op jit(solution)/shard_map/all_gather | solution.py:146
  21.5 0.7 copy-start.8
  21.6 0.7 copy-start.7
  31.1 0.7 copy-start.4
  40.7 7.2 %copy-start.1 = (f32[128,512]{1,0:T(8,128)S(1)}, f32[128,512]{1,0:T(8,128)}, u32[]{:S(2)}) copy-start(f32[128,512]{1,0:T(8,128)} %param.8) | copy-start | bytes 786436
  40.8 7.2 %copy-start.2 = (s32[128,512]{1,0:T(8,128)S(1)}, s32[128,512]{1,0:T(8,128)}, u32[]{:S(2)}) copy-start(s32[128,512]{1,0:T(8,128)} %param.9) | copy-start | bytes 786436
  49.0 1.0 copy-start.3
  76.3 0.9 copy-start
Sparse Core Ops, SparseCore 0:
  10.0 28.3 all-gather.2
  78.4 20.4 all-gather.4

commit v7 on v6

--- a/solution.py
+++ b/solution.py
@@ -65,17 +65,34 @@
     lax.fori_loop(0, 2 * pairs // rows_per_chunk, chunk, 0)
 
 
-def down_kernel(idx_ref, g_ref, w_ref, o_ref, src2_ref, stage_ref):
-    _, rows, _ = g_ref.shape
+def down_kernel(idx_ref, g_ref, w_ref, o_ref, src_ref, w2_ref, stage_ref):
+    sources, rows, cols = g_ref.shape
     block_width = w_ref.shape[1]
     shared_count = w_ref.shape[0] // block_width
     own_blocks = o_ref.shape[1] // block_width
-    _fill_rolled(g_ref, src2_ref)
+    per_source = cols // LANES
+
+    def relayout(i, carry):
+        for m in range(per_source):
+            src_ref[i * per_source + m] = g_ref[i, :, m * LANES:(m + 1) * LANES]
+        return carry
+
+    lax.fori_loop(0, sources, relayout, 0)
+    for s in range(shared_count):
+        block = w_ref[s * block_width:(s + 1) * block_width, :]
+        w2_ref[s * LANES:s * LANES + block_width, :] = block
+        w2_ref[s * LANES + block_width:(s + 1) * LANES, :] = block
+    half_of_lane = jnp.where(
+        lax.broadcasted_iota(jnp.int32, (rows, LANES), 1) >= block_width, 1, 0
+    )
     for r in range(own_blocks):
-        _stage_row(idx_ref, r * shared_count, src2_ref, stage_ref, 0, rows,
-                   shared_count, block_width)
+        for s in range(shared_count):
+            c = idx_ref[r * shared_count + s]
+            piece = src_ref[lax.shift_right_logical(c, 1)]
+            keep = half_of_lane == (c & 1)
+            stage_ref[:, s * LANES:(s + 1) * LANES] = jnp.where(keep, piece, jnp.zeros_like(piece))
         o_ref[:, r * block_width:(r + 1) * block_width] = jnp.dot(
-            stage_ref[...], w_ref[...], preferred_element_type=jnp.float32
+            stage_ref[...], w2_ref[...], preferred_element_type=jnp.float32
         )
 
 
@@ -110,8 +127,9 @@
         ],
         out_specs=pl.BlockSpec(memory_space=pltpu.VMEM),
         scratch_shapes=[
-            pltpu.VMEM((2 * g.shape[0], rows, LANES), jnp.bfloat16),
-            pltpu.VMEM((rows, w.shape[0]), jnp.bfloat16),
+            pltpu.VMEM((g.shape[0] * g.shape[2] // LANES, rows, LANES), jnp.bfloat16),
+            pltpu.VMEM((2 * w.shape[0], w.shape[1]), jnp.bfloat16),
+            pltpu.VMEM((rows, 2 * w.shape[0]), jnp.bfloat16),
         ],
     )(idx, g, w)
 
@@ -124,9 +142,9 @@
     own_blocks = local_cols // block_width
     up_idx = source_index(block_order(up_cols, up_ids, shared_count), up_count).reshape(-1)
     down_order = block_order(down_cols, down_ids, shared_count)
-    down_idx = source_index(lax.dynamic_slice_in_dim(
+    down_idx = lax.dynamic_slice_in_dim(
         down_order, lax.axis_index("down") * own_blocks, own_blocks, 0
-    ), lax.axis_size("down") * local_cols // LANES).reshape(-1)
+    ).reshape(-1)
     up_table = up_blocks.reshape(shared_count * block_width, block_width)
     down_table = down_blocks.reshape(shared_count * block_width, block_width)
     onsite = coupling * double_occ.astype(jnp.float32) - center
@@ -142,8 +160,7 @@
         return lax.all_to_all(pieces, "up", 0, 0, tiled=True)
 
     def down_part(rounded):
-        paired = rounded.reshape(local_rows, local_cols // LANES, LANES).transpose(1, 0, 2)
-        gathered = lax.all_gather(paired, "down", axis=0, tiled=True)
+        gathered = lax.all_gather(rounded, "down", axis=0)
         return down_hop(down_idx, gathered, down_table, local_cols)
 
     rounded0 = amplitudes.astype(jnp.bfloat16)

time: 121 us -> 117 us (0.967)
  local copies, waits for them, and re-layouts: 9.11 us -> 5.62 us
  Pallas kernels: 32.2 us -> 29.8 us
  other arithmetic: 3.97 us -> 6.31 us
    transpose x2 -> x0, local copies, waits for them, and re-layouts: 2.42 us -> none  [down_part(): rounded.reshape(local_rows, local_cols // LANES, LANES).transpose(1, 0, 2)]
    pallas_call x2, Pallas kernels: 14.3 us -> 11.9 us  [down_hop(): pl.pallas_call(down_kernel, out_shape=jax.ShapeDtypeStruct((rows, own_col...]
    unnamed x20 -> x18, local copies, waits for them, and re-layouts: 4.72 us -> 2.94 us
    convert_element_type x0 -> x1, other arithmetic: none -> 1.68 us  [body(): rounded0 = amplitudes.astype(jnp.bfloat16)]
where the time goes in v7:
time: 117 us
  blocking collectives  42.5 us (36%)
  Pallas kernels  29.8 us (25%)
  between operations  13.5 us (12%)
  starting transfers between devices  11.5 us (10%)
  waiting for transfers between devices  7.28 us (6%)
  other arithmetic  6.31 us (5%)
  local copies, waits for them, and re-layouts  5.62 us (5%)
    all_to_all x2, blocking collectives, exchange_up(): return lax.all_to_all(pieces, 'up', 0, 0, tiled=True)  42.5 us
    pallas_call x2, Pallas kernels, up_hop(): pl.pallas_call(up_kernel, out_shape=jax.ShapeDtypeStruct((pairs, n, LANES...  18 us
    pallas_call x2, Pallas kernels, down_hop(): pl.pallas_call(down_kernel, out_shape=jax.ShapeDtypeStruct((rows, own_col...  11.9 us
    all_to_all x1, starting transfers between devices, exchange_up(): return lax.all_to_all(pieces, 'up', 0, 0, tiled=True)  11.5 us
    all_to_all x1, waiting for transfers between devices, exchange_up(): return lax.all_to_all(pieces, 'up', 0, 0, tiled=True)  7.22 us
    unnamed x18, local copies, waits for them, and re-layouts  2.94 us
  transfers between devices with their start and end apart: 3, of which 1 were waited for; matrix products, arithmetic and copies ran while one was open for 2% of the time, Pallas kernels for 15%

profile of v7, /device:TPU:32, one launch (start us, length us, event | category | flops | bytes accessed | tf_op | source)
XLA Modules:
  0.0 116.6 jit_solution(13024890960618851458)
XLA Ops:
  6.5 0.0 copy-start
  6.5 0.0 all-gather.5.cloned.1.call-start
  6.5 1.7 %convert_element_type.13 = bf16[128,512]{1,0:T(8,128)(2,1)} convert(f32[128,512]{1,0:T(8,128)} %param.8) | non-fusion elementwise | flops 65536 | bytes 393216 | tf_op jit(solution)/shard_map/convert_element_type | solution.py:166
  8.2 0.0 all-gather.5.cloned.1.call-update
  8.2 0.0 copy-done
  8.3 0.8 copy.33
  9.0 0.0 copy-start.5
  9.0 0.0 copy-start.6
  9.0 11.5 %all-to-all-start = ((bf16[32,16,128]{2,1,0:T(8,128)(2,1)}), bf16[32,16,128]{2,1,0:T(8,128)(2,1)S(1)}, u32[]{:S(2)}, u32[]{:S(2)}) async-start(bf16[32,16,128]{2,1,0:T(8,128)(2,1)} %bitcast.5), calls=%async_computation | async-start | bytes 262144 | tf_op jit(solution)/shard_map/all_to_all | solution.py:160
  20.5 0.0 all-gather.7.cloned.1.call-start
  20.6 0.0 copy-done.5
  20.6 0.0 copy-done.6
  20.6 0.1 select_reduce_fusion.1
  20.7 0.0 copy-start.7
  20.7 0.0 copy-start.8
  20.7 0.1 constant_dynamic-slice_fusion
  20.8 0.6 copy-done.7
  21.4 0.0 copy-done.8
  21.5 0.1 select_reduce_fusion
  21.6 0.1 copy.30
  21.6 0.7 reshape.45.idx_ref
  22.3 0.1 shift-right-arithmetic_add_fusion
  22.4 0.1 copy.32
  22.4 0.7 add.40.idx_ref
  23.1 7.2 %all-to-all-done.x_ref = bf16[32,16,128]{2,1,0:T(8,128)(2,1)S(1)} async-done(((bf16[32,16,128]{2,1,0:T(8,128)(2,1)}), bf16[32,16,128]{2,1,0:T(8,128)(2,1)S(1)}, u32[]{:S(2)}, u32[]{:S(2)}) %all-to-all-start) | async-done | bytes 131104 | tf_op jit(solution)/shard_map/all_to_all | solution.py:160
  30.3 0.0 copy-start.4
  30.3 0.7 copy-done.4
  31.0 9.0 %shard_map.83 = f32[32,16,128]{2,1,0:T(8,128)} custom-call(s32[2048]{0:T(1024)} %add.40.idx_ref, bf16[32,16,128]{2,1,0:T(8,128)(2,1)} %copy-done.4, bf16[2048,64]{1,0:T(8,128)(2,1)} %bitcast.28), custom_call_target="tpu_custom_call" | custom-call | tf_op jit(solution)/shard_map/pallas_call | solution.py:102
  40.0 0.0 all-gather.5.cloned.1.call-done
  40.0 0.0 copy-start.2
  40.0 6.0 %shard_map.82 = f32[128,512]{1,0:T(8,128)} custom-call(s32[256]{0:T(256)} %reshape.45.idx_ref, bf16[8,128,512]{2,1,0:T(8,128)(2,1)} %bitcast.30, bf16[2048,64]{1,0:T(8,128)(2,1)} %bitcast.26), custom_call_target="tpu_custom_call" | custom-call | tf_op jit(solution)/shard_map/pallas_call | solution.py:120
  45.9 0.0 copy-done.2
  45.9 1.0 fusion.6
  46.9 0.0 copy-start.3
  47.0 0.1 copy.31
  47.1 0.8 copy-done.3
  48.0 25.6 %all_to_all.15 = f32[32,32,128]{2,1,0:T(8,128)S(1)} all-to-all(f32[32,32,128]{2,1,0:T(8,128)S(1)} %pad_maximum_fusion), channel_id=1, replica_groups=mesh['up'=32,'down'=8] {'up'}, dimensions={0} | all-to-all | bytes 1048576 | tf_op jit(solution)/shard_map/all_to_all | solution.py:160
  73.6 0.7 fusion.1
  74.3 0.1 copy.34
  74.4 0.8 copy-done.1
  75.2 0.8 fusion.5
  76.0 0.0 all-gather.7.cloned.1.call-update
  76.0 9.0 %shard_map.84 = f32[32,16,128]{2,1,0:T(8,128)} custom-call(s32[2048]{0:T(1024)} %add.40.idx_ref, bf16[32,16,128]{2,1,0:T(8,128)(2,1)} %get-tuple-element.5.x_ref, bf16[2048,64]{1,0:T(8,128)(2,1)} %bitcast.29), custom_call_target="tpu_custom_call" | custom-call | tf_op jit(solution)/shard_map/pallas_call | solution.py:102
  85.0 16.9 %all_to_all.16 = f32[32,16,128]{2,1,0:T(8,128)S(1)} all-to-all(f32[32,16,128]{2,1,0:T(8,128)} %shard_map.84), channel_id=1, replica_groups=mesh['up'=32,'down'=8] {'up'}, dimensions={0} | all-to-all | bytes 524288 | tf_op jit(solution)/shard_map/all_to_all | solution.py:160
  101.9 0.1 copy.35
  102.0 0.0 all-gather.7.cloned.1.call-done
  102.0 5.9 %shard_map.85 = f32[128,512]{1,0:T(8,128)} custom-call(s32[256]{0:T(256)} %reshape.45.idx_ref, bf16[8,128,512]{2,1,0:T(8,128)(2,1)} %bitcast.31, bf16[2048,64]{1,0:T(8,128)(2,1)} %bitcast.27), custom_call_target="tpu_custom_call" | custom-call | tf_op jit(solution)/shard_map/pallas_call | solution.py:120
  108.0 1.8 %fusion.3 = f32[128,512]{1,0:T(8,128)} fusion(f32[128,512]{1,0:T(8,128)S(1)} %copy-done, f32[128,512]{1,0:T(8,128)} %shard_map.85, f32[512,128]{0,1:T(8,128)S(1)} %copy.35, s32[128,512]{1,0:T(8,128)S(1)} %copy-done.2, f32[512,128]{0,1:T(8,128)S(1)} %copy.34, f32[128,512]{1,0:T(8,128)S(1)} %copy-done.1), kind=kLoop, calls=%fused_computation.10 | loop fusion | flops 720896 | bytes 1835008 | tf_op jit(solution)/shard_map/sub | solution.py:178
  (4 shorter events, 0.1 us)
Async XLA Ops:
  6.5 1.7 %copy-start = (f32[128,512]{1,0:T(8,128)S(1)}, f32[128,512]{1,0:T(8,128)}, u32[]{:S(2)}) copy-start(f32[128,512]{1,0:T(8,128)} %param.8) | copy-start | bytes 786436
  6.5 33.4 %all-gather.5.cloned.1.call-start = ((), (), s32[]{:S(2)}) async-start(), calls=%async_computation.3 | async-start | bytes 1179648 | tf_op jit(solution)/shard_map/all_gather | solution.py:163
  9.0 11.6 %copy-start.5 = (s32[64,32]{0,1:T(8,128)S(1)}, s32[64,32]{0,1:T(8,128)}, u32[]{:S(2)}) copy-start(s32[64,32]{0,1:T(8,128)} %param.13) | copy-start | bytes 24580
  9.0 11.6 %copy-start.6 = (s32[64,32]{0,1:T(8,128)S(1)}, s32[64,32]{0,1:T(8,128)}, u32[]{:S(2)}) copy-start(s32[64,32]{0,1:T(8,128)} %param.14) | copy-start | bytes 24580
  9.0 21.3 %all-to-all-start = ((bf16[32,16,128]{2,1,0:T(8,128)(2,1)}), bf16[32,16,128]{2,1,0:T(8,128)(2,1)S(1)}, u32[]{:S(2)}, u32[]{:S(2)}) async-start(bf16[32,16,128]{2,1,0:T(8,128)(2,1)} %bitcast.5), calls=%async_computation | async-start | bytes 262144 | tf_op jit(solution)/shard_map/all_to_all | solution.py:160
  20.5 81.5 %all-gather.7.cloned.1.call-start = ((), (), s32[]{:S(2)}) async-start(), calls=%async_computation.4 | async-start | bytes 1179648 | tf_op jit(solution)/shard_map/all_gather | solution.py:163
  20.7 0.7 copy-start.7
  20.7 0.7 copy-start.8
  30.3 0.7 copy-start.4
  40.0 6.0 %copy-start.2 = (s32[128,512]{1,0:T(8,128)S(1)}, s32[128,512]{1,0:T(8,128)}, u32[]{:S(2)}) copy-start(s32[128,512]{1,0:T(8,128)} %param.9) | copy-start | bytes 786436
  46.9 1.0 copy-start.3
  74.3 0.9 copy-start.1
Sparse Core Ops, SparseCore 0:
  9.2 28.3 all-gather.4
  76.1 20.4 all-gather.6

commit v8 on v7

--- a/solution.py
+++ b/solution.py
@@ -4,6 +4,7 @@
 from jax.experimental import pallas as pl
 from jax.experimental.pallas import tpu as pltpu
 from jax.sharding import PartitionSpec as P
+
 
 coupling = 0.5
 center = 2.0
@@ -160,11 +161,13 @@
         return lax.all_to_all(pieces, "up", 0, 0, tiled=True)
 
     def down_part(rounded):
-        gathered = lax.all_gather(rounded, "down", axis=0)
+        copies = jnp.broadcast_to(rounded[None], (lax.axis_size("down"),) + rounded.shape)
+        gathered = lax.all_to_all(copies, "down", 0, 0, tiled=True)
         return down_hop(down_idx, gathered, down_table, local_cols)
 
     rounded0 = amplitudes.astype(jnp.bfloat16)
-    up0_cols = up_hop(up_idx, exchange_up(to_columns(rounded0)), up_table)
+    sent0 = exchange_up(to_columns(rounded0))
+    up0_cols = up_hop(up_idx, sent0, up_table)
     partial_rows = onsite * amplitudes + down_part(rounded0)
     both = exchange_up(jnp.concatenate([to_columns(partial_rows), up0_cols], axis=1))
     partial_cols = both[:, :col_chunk]

time: 117 us -> 132 us (1.13); the launches traced: 117 us -> 130 us
  waiting for transfers between devices: 7.28 us -> 41.2 us
  blocking collectives: 42.5 us -> 21.4 us
  between operations: 13.5 us -> 0.14 us
  starting transfers between devices: 11.5 us -> 24.2 us
  local copies, waits for them, and re-layouts: 5.62 us -> 8.46 us
  other arithmetic: 6.31 us -> 4.95 us
    all_to_all x2 -> x1, blocking collectives: 42.5 us -> 21.4 us  [exchange_up(): return lax.all_to_all(pieces, 'up', 0, 0, tiled=True)]
    all_to_all x0 -> x2, waiting for transfers between devices: none -> 20.8 us  [down_part(): gathered = lax.all_to_all(copies, 'down', 0, 0, tiled=True)]
    all_to_all x1 -> x2, waiting for transfers between devices: 7.22 us -> 20.4 us  [exchange_up(): return lax.all_to_all(pieces, 'up', 0, 0, tiled=True)]
    all_to_all x0 -> x2, starting transfers between devices: none -> 7.99 us  [down_part(): gathered = lax.all_to_all(copies, 'down', 0, 0, tiled=True)]
    all_to_all x1 -> x2, starting transfers between devices: 11.5 us -> 16.2 us  [exchange_up(): return lax.all_to_all(pieces, 'up', 0, 0, tiled=True)]
    broadcast_in_dim x0 -> x2, local copies, waits for them, and re-layouts: none -> 2.14 us  [down_part(): jnp.broadcast_to(rounded[None], (lax.axis_size('down'),) + rounded.shape)]
    convert_element_type x1, other arithmetic: 1.68 us -> 0.02 us  [body(): rounded0 = amplitudes.astype(jnp.bfloat16)]
    unnamed x18 -> x22, local copies, waits for them, and re-layouts: 2.94 us -> 3.62 us
  transfers between devices with their start and end apart: 3 -> 4, of which waited for: 1 -> 4; matrix products, arithmetic and copies ran while one was open for 2% -> 2% of each run, Pallas kernels for 15% -> 7%
where the time goes in v8:
time: 132 us; the launch traced here: 130 us
  waiting for transfers between devices  41.2 us (31%)
  Pallas kernels  29.8 us (23%)
  starting transfers between devices  24.2 us (18%)
  blocking collectives  21.4 us (16%)
  local copies, waits for them, and re-layouts  8.46 us (6%)
  other arithmetic  4.95 us (4%)
    all_to_all x1, blocking collectives, exchange_up(): return lax.all_to_all(pieces, 'up', 0, 0, tiled=True)  21.4 us
    all_to_all x2, waiting for transfers between devices, down_part(): gathered = lax.all_to_all(copies, 'down', 0, 0, tiled=True)  20.8 us
    all_to_all x2, waiting for transfers between devices, exchange_up(): return lax.all_to_all(pieces, 'up', 0, 0, tiled=True)  20.4 us
    pallas_call x2, Pallas kernels, up_hop(): pl.pallas_call(up_kernel, out_shape=jax.ShapeDtypeStruct((pairs, n, LANES...  17.9 us
    all_to_all x2, starting transfers between devices, exchange_up(): return lax.all_to_all(pieces, 'up', 0, 0, tiled=True)  16.2 us
    pallas_call x2, Pallas kernels, down_hop(): pl.pallas_call(down_kernel, out_shape=jax.ShapeDtypeStruct((rows, own_col...  11.9 us
    all_to_all x2, starting transfers between devices, down_part(): gathered = lax.all_to_all(copies, 'down', 0, 0, tiled=True)  7.99 us
    unnamed x22, local copies, waits for them, and re-layouts  3.62 us
  transfers between devices with their start and end apart: 4, of which 4 were waited for; matrix products, arithmetic and copies ran while one was open for 2% of the time, Pallas kernels for 7%

profile of v8, /device:TPU:32, one launch (start us, length us, event | category | flops | bytes accessed | tf_op | source)
XLA Modules:
  0.0 130.2 jit_solution(18289684263130014189)
XLA Ops:
  0.0 1.0 convert_bitcast_fusion
  1.0 0.0 copy-start
  1.0 0.8 copy.33
  1.7 11.4 %all-to-all-start.1 = ((bf16[32,16,128]{2,1,0:T(8,128)(2,1)}), bf16[32,16,128]{2,1,0:T(8,128)(2,1)S(1)}, u32[]{:S(2)}, u32[]{:S(2)}) async-start(bf16[32,16,128]{2,1,0:T(8,128)(2,1)} %bitcast.4), calls=%async_computation.1 | async-start | bytes 262144 | tf_op jit(solution)/shard_map/all_to_all | solution.py:161
  13.1 0.0 copy-done
  13.1 9.8 %all-to-all-done.1.x_ref = bf16[32,16,128]{2,1,0:T(8,128)(2,1)S(1)} async-done(((bf16[32,16,128]{2,1,0:T(8,128)(2,1)}), bf16[32,16,128]{2,1,0:T(8,128)(2,1)S(1)}, u32[]{:S(2)}, u32[]{:S(2)}) %all-to-all-start.1) | async-done | bytes 131104 | tf_op jit(solution)/shard_map/all_to_all | solution.py:161
  22.9 0.0 copy-start.6
  22.9 1.1 broadcast_in_dim.39
  24.0 0.0 copy-done.6
  24.0 4.4 %all-to-all-start = ((bf16[8,128,512]{2,1,0:T(8,128)(2,1)}), bf16[8,128,512]{2,1,0:T(8,128)(2,1)S(1)}, u32[]{:S(2)}, u32[]{:S(2)}) async-start(bf16[8,128,512]{2,1,0:T(8,128)(2,1)} %broadcast_in_dim.39), calls=%async_computation | async-start | bytes 2097152 | tf_op jit(solution)/shard_map/all_to_all | solution.py:165
  28.4 0.0 copy-done.7
  28.4 0.0 copy-done.8
  28.4 0.1 select_reduce_fusion.1
  28.5 0.0 copy-start.10
  28.5 0.1 constant_dynamic-slice_fusion
  28.6 0.1 copy.30
  28.7 0.7 reshape.47.idx_ref
  29.3 0.0 copy-done.10
  29.4 0.0 copy-done.9
  29.4 0.1 select_reduce_fusion
  29.5 0.1 shift-right-arithmetic_add_fusion
  29.5 0.1 copy.32
  29.6 0.7 add.40.idx_ref
  30.3 9.0 %shard_map.83 = f32[32,16,128]{2,1,0:T(8,128)} custom-call(s32[2048]{0:T(1024)} %add.40.idx_ref, bf16[32,16,128]{2,1,0:T(8,128)(2,1)} %copy-done.6, bf16[2048,64]{1,0:T(8,128)(2,1)} %bitcast.26), custom_call_target="tpu_custom_call" | custom-call | tf_op jit(solution)/shard_map/pallas_call | solution.py:103
  39.3 5.1 %all-to-all-done.g_ref = bf16[8,128,512]{2,1,0:T(8,128)(2,1)S(1)} async-done(((bf16[8,128,512]{2,1,0:T(8,128)(2,1)}), bf16[8,128,512]{2,1,0:T(8,128)(2,1)S(1)}, u32[]{:S(2)}, u32[]{:S(2)}) %all-to-all-start) | async-done | bytes 1048608 | tf_op jit(solution)/shard_map/all_to_all | solution.py:165
  44.3 1.0 copy-done.1
  45.3 6.0 %shard_map.82 = f32[128,512]{1,0:T(8,128)} custom-call(s32[256]{0:T(256)} %reshape.47.idx_ref, bf16[8,128,512]{2,1,0:T(8,128)(2,1)} %copy-done.1, bf16[2048,64]{1,0:T(8,128)(2,1)} %bitcast.24), custom_call_target="tpu_custom_call" | custom-call | tf_op jit(solution)/shard_map/pallas_call | solution.py:121
  51.3 0.0 copy-done.4
  51.3 1.0 fusion.6
  52.3 0.0 copy-start.5
  52.3 0.1 copy.31
  52.5 0.8 copy-done.5
  53.3 21.4 %all_to_all.25 = f32[32,32,128]{2,1,0:T(8,128)S(1)} all-to-all(f32[32,32,128]{2,1,0:T(8,128)S(1)} %pad_maximum_fusion), channel_id=1, replica_groups=mesh['up'=32,'down'=8] {'up'}, dimensions={0} | all-to-all | bytes 1048576 | tf_op jit(solution)/shard_map/all_to_all | solution.py:161
  74.7 0.7 fusion.1
  75.4 9.0 %shard_map.84 = f32[32,16,128]{2,1,0:T(8,128)} custom-call(s32[2048]{0:T(1024)} %add.40.idx_ref, bf16[32,16,128]{2,1,0:T(8,128)(2,1)} %get-tuple-element.5.x_ref, bf16[2048,64]{1,0:T(8,128)(2,1)} %bitcast.27), custom_call_target="tpu_custom_call" | custom-call | tf_op jit(solution)/shard_map/pallas_call | solution.py:103
  84.4 4.8 %all-to-all-start.3 = ((f32[32,16,128]{2,1,0:T(8,128)}), f32[32,16,128]{2,1,0:T(8,128)S(1)}, u32[]{:S(2)}, u32[]{:S(2)}) async-start(f32[32,16,128]{2,1,0:T(8,128)} %shard_map.84), calls=%async_computation.3 | async-start | bytes 524288 | tf_op jit(solution)/shard_map/all_to_all | solution.py:161
  89.3 0.0 copy-start.3
  89.3 0.1 copy.34
  89.4 0.8 copy-done.3
  90.2 0.1 fusion.5
  90.3 10.7 %all-to-all-done.3 = f32[32,16,128]{2,1,0:T(8,128)S(1)} async-done(((f32[32,16,128]{2,1,0:T(8,128)}), f32[32,16,128]{2,1,0:T(8,128)S(1)}, u32[]{:S(2)}, u32[]{:S(2)}) %all-to-all-start.3) | async-done | bytes 262176 | tf_op jit(solution)/shard_map/all_to_all | solution.py:161
  101.0 1.1 broadcast_in_dim.41
  102.1 3.6 %all-to-all-start.4 = ((bf16[8,128,512]{2,1,0:T(8,128)(2,1)}), bf16[8,128,512]{2,1,0:T(8,128)(2,1)S(1)}, u32[]{:S(2)}, u32[]{:S(2)}) async-start(bf16[8,128,512]{2,1,0:T(8,128)(2,1)} %broadcast_in_dim.41), calls=%async_computation.4 | async-start | bytes 2097152 | tf_op jit(solution)/shard_map/all_to_all | solution.py:165
  105.6 0.1 copy.35
  105.8 15.7 %all-to-all-done.4.g_ref = bf16[8,128,512]{2,1,0:T(8,128)(2,1)S(1)} async-done(((bf16[8,128,512]{2,1,0:T(8,128)(2,1)}), bf16[8,128,512]{2,1,0:T(8,128)(2,1)S(1)}, u32[]{:S(2)}, u32[]{:S(2)}) %all-to-all-start.4) | async-done | bytes 1048608 | tf_op jit(solution)/shard_map/all_to_all | solution.py:165
  121.5 1.0 copy-done.2
  122.5 5.9 %shard_map.85 = f32[128,512]{1,0:T(8,128)} custom-call(s32[256]{0:T(256)} %reshape.47.idx_ref, bf16[8,128,512]{2,1,0:T(8,128)(2,1)} %copy-done.2, bf16[2048,64]{1,0:T(8,128)(2,1)} %bitcast.25), custom_call_target="tpu_custom_call" | custom-call | tf_op jit(solution)/shard_map/pallas_call | solution.py:121
  128.4 1.8 %fusion.3 = f32[128,512]{1,0:T(8,128)} fusion(f32[128,512]{1,0:T(8,128)S(1)} %copy-done, f32[128,512]{1,0:T(8,128)} %shard_map.85, f32[512,128]{0,1:T(8,128)S(1)} %copy.35, s32[128,512]{1,0:T(8,128)S(1)} %copy-done.4, f32[512,128]{0,1:T(8,128)S(1)} %copy.34, f32[128,512]{1,0:T(8,128)S(1)} %copy-done.3), kind=kLoop, calls=%fused_computation.10 | loop fusion | flops 720896 | bytes 1835008 | tf_op jit(solution)/shard_map/sub | solution.py:181
  (9 shorter events, 0.1 us)
Async XLA Ops:
  1.0 12.1 %copy-start = (f32[128,512]{1,0:T(8,128)S(1)}, f32[128,512]{1,0:T(8,128)}, u32[]{:S(2)}) copy-start(f32[128,512]{1,0:T(8,128)} %param.8) | copy-start | bytes 786436
  1.7 21.2 %all-to-all-start.1 = ((bf16[32,16,128]{2,1,0:T(8,128)(2,1)}), bf16[32,16,128]{2,1,0:T(8,128)(2,1)S(1)}, u32[]{:S(2)}, u32[]{:S(2)}) async-start(bf16[32,16,128]{2,1,0:T(8,128)(2,1)} %bitcast.4), calls=%async_computation.1 | async-start | bytes 262144 | tf_op jit(solution)/shard_map/all_to_all | solution.py:161
  22.9 1.1 copy-start.6
  24.0 4.4 %copy-start.7 = (s32[64,32]{0,1:T(8,128)S(1)}, s32[64,32]{0,1:T(8,128)}, u32[]{:S(2)}) copy-start(s32[64,32]{0,1:T(8,128)} %param.13) | copy-start | bytes 24580
  24.0 4.4 %copy-start.8 = (s32[64,32]{0,1:T(8,128)S(1)}, s32[64,32]{0,1:T(8,128)}, u32[]{:S(2)}) copy-start(s32[64,32]{0,1:T(8,128)} %param.14) | copy-start | bytes 24580
  24.0 20.4 %all-to-all-start = ((bf16[8,128,512]{2,1,0:T(8,128)(2,1)}), bf16[8,128,512]{2,1,0:T(8,128)(2,1)S(1)}, u32[]{:S(2)}, u32[]{:S(2)}) async-start(bf16[8,128,512]{2,1,0:T(8,128)(2,1)} %broadcast_in_dim.39), calls=%async_computation | async-start | bytes 2097152 | tf_op jit(solution)/shard_map/all_to_all | solution.py:165
  28.5 0.8 copy-start.10
  28.6 0.7 copy-start.9
  44.3 1.0 copy-start.1
  45.3 6.0 %copy-start.4 = (s32[128,512]{1,0:T(8,128)S(1)}, s32[128,512]{1,0:T(8,128)}, u32[]{:S(2)}) copy-start(s32[128,512]{1,0:T(8,128)} %param.9) | copy-start | bytes 786436
  52.3 1.0 copy-start.5
  84.4 16.6 %all-to-all-start.3 = ((f32[32,16,128]{2,1,0:T(8,128)}), f32[32,16,128]{2,1,0:T(8,128)S(1)}, u32[]{:S(2)}, u32[]{:S(2)}) async-start(f32[32,16,128]{2,1,0:T(8,128)} %shard_map.84), calls=%async_computation.3 | async-start | bytes 524288 | tf_op jit(solution)/shard_map/all_to_all | solution.py:161
  89.3 1.0 copy-start.3
  102.1 19.4 %all-to-all-start.4 = ((bf16[8,128,512]{2,1,0:T(8,128)(2,1)}), bf16[8,128,512]{2,1,0:T(8,128)(2,1)S(1)}, u32[]{:S(2)}, u32[]{:S(2)}) async-start(bf16[8,128,512]{2,1,0:T(8,128)(2,1)} %broadcast_in_dim.41), calls=%async_computation.4 | async-start | bytes 2097152 | tf_op jit(solution)/shard_map/all_to_all | solution.py:165
  121.5 1.0 copy-start.2

commit v9 on v8

--- a/solution.py
+++ b/solution.py
@@ -97,6 +97,22 @@
         )
 
 
+def transpose_round_kernel(x_ref, o_ref):
+    for m in range(x_ref.shape[1] // LANES):
+        tile = x_ref[:, m * LANES:(m + 1) * LANES]
+        o_ref[m * LANES:(m + 1) * LANES, :] = tile.T.astype(o_ref.dtype)
+
+
+def transpose_round(x):
+    rows, cols = x.shape
+    return pl.pallas_call(
+        transpose_round_kernel,
+        out_shape=jax.ShapeDtypeStruct((cols, rows), jnp.bfloat16),
+        in_specs=[pl.BlockSpec(memory_space=pltpu.VMEM)],
+        out_specs=pl.BlockSpec(memory_space=pltpu.VMEM),
+    )(x)
+
+
 def up_hop(idx, x, w):
     pairs, n, _ = x.shape
     rows_per_chunk = 8
@@ -166,7 +182,9 @@
         return down_hop(down_idx, gathered, down_table, local_cols)
 
     rounded0 = amplitudes.astype(jnp.bfloat16)
-    sent0 = exchange_up(to_columns(rounded0))
+    sent0 = exchange_up(
+        transpose_round(amplitudes).reshape(up_count, col_chunk, local_rows)
+    )
     up0_cols = up_hop(up_idx, sent0, up_table)
     partial_rows = onsite * amplitudes + down_part(rounded0)
     both = exchange_up(jnp.concatenate([to_columns(partial_rows), up0_cols], axis=1))

time: 132 us -> 132 us (level)
  Pallas kernels: 29.8 us -> 31.6 us
    pallas_call x0 -> x1, Pallas kernels: none -> 1.78 us  [transpose_round(): pl.pallas_call(transpose_round_kernel, out_shape=jax.ShapeDtypeStruct((co...]
where the time goes in v9:
time: 132 us; the launch traced here: 130 us
  waiting for transfers between devices  41.1 us (31%)
  Pallas kernels  31.6 us (24%)
  starting transfers between devices  24.2 us (18%)
  blocking collectives  21.4 us (16%)
  local copies, waits for them, and re-layouts  7.7 us (6%)
  other arithmetic  3.98 us (3%)
    all_to_all x1, blocking collectives, exchange_up(): return lax.all_to_all(pieces, 'up', 0, 0, tiled=True)  21.4 us
    all_to_all x2, waiting for transfers between devices, down_part(): gathered = lax.all_to_all(copies, 'down', 0, 0, tiled=True)  20.8 us
    all_to_all x2, waiting for transfers between devices, exchange_up(): return lax.all_to_all(pieces, 'up', 0, 0, tiled=True)  20.3 us
    pallas_call x2, Pallas kernels, up_hop(): pl.pallas_call(up_kernel, out_shape=jax.ShapeDtypeStruct((pairs, n, LANES...  17.9 us
    all_to_all x2, starting transfers between devices, exchange_up(): return lax.all_to_all(pieces, 'up', 0, 0, tiled=True)  16.2 us
    pallas_call x2, Pallas kernels, down_hop(): pl.pallas_call(down_kernel, out_shape=jax.ShapeDtypeStruct((rows, own_col...  11.9 us
    all_to_all x2, starting transfers between devices, down_part(): gathered = lax.all_to_all(copies, 'down', 0, 0, tiled=True)  7.99 us
    unnamed x22, local copies, waits for them, and re-layouts  3.61 us
  transfers between devices with their start and end apart: 4, of which 4 were waited for; matrix products, arithmetic and copies ran while one was open for 2% of the time, Pallas kernels for 7%

profile of v9, /device:TPU:32, one launch (start us, length us, event | category | flops | bytes accessed | tf_op | source)
XLA Modules:
  0.0 130.2 jit_solution(13353297082006007034)
XLA Ops:
  0.0 0.0 copy-start
  0.0 1.8 %shard_map.83 = bf16[512,128]{1,0:T(8,128)(2,1)} custom-call(f32[128,512]{1,0:T(8,128)} %x_ref.1), custom_call_target="tpu_custom_call" | custom-call | tf_op jit(solution)/shard_map/pallas_call | solution.py:108
  1.8 11.4 %all-to-all-start.1 = ((bf16[32,16,128]{2,1,0:T(8,128)(2,1)}), bf16[32,16,128]{2,1,0:T(8,128)(2,1)S(1)}, u32[]{:S(2)}, u32[]{:S(2)}) async-start(bf16[32,16,128]{2,1,0:T(8,128)(2,1)} %bitcast.29), calls=%async_computation.1 | async-start | bytes 262144 | tf_op jit(solution)/shard_map/all_to_all | solution.py:177
  13.1 0.0 copy-done
  13.2 9.8 %all-to-all-done.1.x_ref = bf16[32,16,128]{2,1,0:T(8,128)(2,1)S(1)} async-done(((bf16[32,16,128]{2,1,0:T(8,128)(2,1)}), bf16[32,16,128]{2,1,0:T(8,128)(2,1)S(1)}, u32[]{:S(2)}, u32[]{:S(2)}) %all-to-all-start.1) | async-done | bytes 131104 | tf_op jit(solution)/shard_map/all_to_all | solution.py:177
  22.9 0.0 copy-start.6
  22.9 1.1 broadcast_in_dim.39
  24.0 0.0 copy-done.6
  24.0 0.0 copy-start.7
  24.0 4.4 %all-to-all-start = ((bf16[8,128,512]{2,1,0:T(8,128)(2,1)}), bf16[8,128,512]{2,1,0:T(8,128)(2,1)S(1)}, u32[]{:S(2)}, u32[]{:S(2)}) async-start(bf16[8,128,512]{2,1,0:T(8,128)(2,1)} %broadcast_in_dim.39), calls=%async_computation | async-start | bytes 2097152 | tf_op jit(solution)/shard_map/all_to_all | solution.py:181
  28.4 0.0 copy-done.7
  28.5 0.0 copy-done.8
  28.5 0.1 select_reduce_fusion.1
  28.6 0.0 copy-start.10
  28.6 0.1 constant_dynamic-slice_fusion
  28.7 0.1 copy.27
  28.7 0.7 reshape.47.idx_ref
  29.4 0.0 copy-done.10
  29.4 0.0 copy-done.9
  29.4 0.1 select_reduce_fusion
  29.5 0.1 shift-right-arithmetic_add_fusion
  29.6 0.1 copy.29
  29.6 0.7 add.40.idx_ref
  30.3 9.0 %shard_map.84 = f32[32,16,128]{2,1,0:T(8,128)} custom-call(s32[2048]{0:T(1024)} %add.40.idx_ref, bf16[32,16,128]{2,1,0:T(8,128)(2,1)} %copy-done.6, bf16[2048,64]{1,0:T(8,128)(2,1)} %bitcast.24), custom_call_target="tpu_custom_call" | custom-call | tf_op jit(solution)/shard_map/pallas_call | solution.py:119
  39.3 5.1 %all-to-all-done.g_ref = bf16[8,128,512]{2,1,0:T(8,128)(2,1)S(1)} async-done(((bf16[8,128,512]{2,1,0:T(8,128)(2,1)}), bf16[8,128,512]{2,1,0:T(8,128)(2,1)S(1)}, u32[]{:S(2)}, u32[]{:S(2)}) %all-to-all-start) | async-done | bytes 1048608 | tf_op jit(solution)/shard_map/all_to_all | solution.py:181
  44.4 1.0 copy-done.1
  45.4 6.0 %shard_map.82 = f32[128,512]{1,0:T(8,128)} custom-call(s32[256]{0:T(256)} %reshape.47.idx_ref, bf16[8,128,512]{2,1,0:T(8,128)(2,1)} %copy-done.1, bf16[2048,64]{1,0:T(8,128)(2,1)} %bitcast.22), custom_call_target="tpu_custom_call" | custom-call | tf_op jit(solution)/shard_map/pallas_call | solution.py:137
  51.3 0.0 copy-done.4
  51.3 1.0 fusion.6
  52.3 0.0 copy-start.5
  52.4 0.1 copy.28
  52.5 0.8 copy-done.5
  53.4 21.4 %all_to_all.25 = f32[32,32,128]{2,1,0:T(8,128)S(1)} all-to-all(f32[32,32,128]{2,1,0:T(8,128)S(1)} %pad_maximum_fusion), channel_id=1, replica_groups=mesh['up'=32,'down'=8] {'up'}, dimensions={0} | all-to-all | bytes 1048576 | tf_op jit(solution)/shard_map/all_to_all | solution.py:177
  74.8 0.7 fusion.1
  75.5 9.0 %shard_map.85 = f32[32,16,128]{2,1,0:T(8,128)} custom-call(s32[2048]{0:T(1024)} %add.40.idx_ref, bf16[32,16,128]{2,1,0:T(8,128)(2,1)} %get-tuple-element.5.x_ref, bf16[2048,64]{1,0:T(8,128)(2,1)} %bitcast.25), custom_call_target="tpu_custom_call" | custom-call | tf_op jit(solution)/shard_map/pallas_call | solution.py:119
  84.4 4.8 %all-to-all-start.3 = ((f32[32,16,128]{2,1,0:T(8,128)}), f32[32,16,128]{2,1,0:T(8,128)S(1)}, u32[]{:S(2)}, u32[]{:S(2)}) async-start(f32[32,16,128]{2,1,0:T(8,128)} %shard_map.85), calls=%async_computation.3 | async-start | bytes 524288 | tf_op jit(solution)/shard_map/all_to_all | solution.py:177
  89.3 0.0 copy-start.3
  89.3 0.1 copy.30
  89.4 0.8 copy-done.3
  90.3 0.1 fusion.5
  90.4 10.6 %all-to-all-done.3 = f32[32,16,128]{2,1,0:T(8,128)S(1)} async-done(((f32[32,16,128]{2,1,0:T(8,128)}), f32[32,16,128]{2,1,0:T(8,128)S(1)}, u32[]{:S(2)}, u32[]{:S(2)}) %all-to-all-start.3) | async-done | bytes 262176 | tf_op jit(solution)/shard_map/all_to_all | solution.py:177
  100.9 1.1 broadcast_in_dim.41
  102.0 3.6 %all-to-all-start.4 = ((bf16[8,128,512]{2,1,0:T(8,128)(2,1)}), bf16[8,128,512]{2,1,0:T(8,128)(2,1)S(1)}, u32[]{:S(2)}, u32[]{:S(2)}) async-start(bf16[8,128,512]{2,1,0:T(8,128)(2,1)} %broadcast_in_dim.41), calls=%async_computation.4 | async-start | bytes 2097152 | tf_op jit(solution)/shard_map/all_to_all | solution.py:181
  105.6 0.1 copy.31
  105.7 15.7 %all-to-all-done.4.g_ref = bf16[8,128,512]{2,1,0:T(8,128)(2,1)S(1)} async-done(((bf16[8,128,512]{2,1,0:T(8,128)(2,1)}), bf16[8,128,512]{2,1,0:T(8,128)(2,1)S(1)}, u32[]{:S(2)}, u32[]{:S(2)}) %all-to-all-start.4) | async-done | bytes 1048608 | tf_op jit(solution)/shard_map/all_to_all | solution.py:181
  121.4 1.0 copy-done.2
  122.4 5.9 %shard_map.86 = f32[128,512]{1,0:T(8,128)} custom-call(s32[256]{0:T(256)} %reshape.47.idx_ref, bf16[8,128,512]{2,1,0:T(8,128)(2,1)} %copy-done.2, bf16[2048,64]{1,0:T(8,128)(2,1)} %bitcast.23), custom_call_target="tpu_custom_call" | custom-call | tf_op jit(solution)/shard_map/pallas_call | solution.py:137
  128.3 1.8 %fusion.3 = f32[128,512]{1,0:T(8,128)} fusion(f32[128,512]{1,0:T(8,128)S(1)} %copy-done, f32[128,512]{1,0:T(8,128)} %shard_map.86, f32[512,128]{0,1:T(8,128)S(1)} %copy.31, s32[128,512]{1,0:T(8,128)S(1)} %copy-done.4, f32[512,128]{0,1:T(8,128)S(1)} %copy.30, f32[128,512]{1,0:T(8,128)S(1)} %copy-done.3), kind=kLoop, calls=%fused_computation.10 | loop fusion | flops 720896 | bytes 1835008 | tf_op jit(solution)/shard_map/sub | solution.py:199
  (8 shorter events, 0.1 us)
Async XLA Ops:
  0.0 13.1 %copy-start = (f32[128,512]{1,0:T(8,128)S(1)}, f32[128,512]{1,0:T(8,128)}, u32[]{:S(2)}) copy-start(f32[128,512]{1,0:T(8,128)} %x_ref.1) | copy-start | bytes 786436
  1.8 21.2 %all-to-all-start.1 = ((bf16[32,16,128]{2,1,0:T(8,128)(2,1)}), bf16[32,16,128]{2,1,0:T(8,128)(2,1)S(1)}, u32[]{:S(2)}, u32[]{:S(2)}) async-start(bf16[32,16,128]{2,1,0:T(8,128)(2,1)} %bitcast.29), calls=%async_computation.1 | async-start | bytes 262144 | tf_op jit(solution)/shard_map/all_to_all | solution.py:177
  22.9 1.1 copy-start.6
  24.0 4.4 %copy-start.7 = (s32[64,32]{0,1:T(8,128)S(1)}, s32[64,32]{0,1:T(8,128)}, u32[]{:S(2)}) copy-start(s32[64,32]{0,1:T(8,128)} %param.13) | copy-start | bytes 24580
  24.0 4.4 %copy-start.8 = (s32[64,32]{0,1:T(8,128)S(1)}, s32[64,32]{0,1:T(8,128)}, u32[]{:S(2)}) copy-start(s32[64,32]{0,1:T(8,128)} %param.14) | copy-start | bytes 24580
  24.0 20.4 %all-to-all-start = ((bf16[8,128,512]{2,1,0:T(8,128)(2,1)}), bf16[8,128,512]{2,1,0:T(8,128)(2,1)S(1)}, u32[]{:S(2)}, u32[]{:S(2)}) async-start(bf16[8,128,512]{2,1,0:T(8,128)(2,1)} %broadcast_in_dim.39), calls=%async_computation | async-start | bytes 2097152 | tf_op jit(solution)/shard_map/all_to_all | solution.py:181
  28.6 0.8 copy-start.10
  28.7 0.7 copy-start.9
  44.4 1.0 copy-start.1
  45.4 6.0 %copy-start.4 = (s32[128,512]{1,0:T(8,128)S(1)}, s32[128,512]{1,0:T(8,128)}, u32[]{:S(2)}) copy-start(s32[128,512]{1,0:T(8,128)} %param.9) | copy-start | bytes 786436
  52.3 1.0 copy-start.5
  84.4 16.5 %all-to-all-start.3 = ((f32[32,16,128]{2,1,0:T(8,128)}), f32[32,16,128]{2,1,0:T(8,128)S(1)}, u32[]{:S(2)}, u32[]{:S(2)}) async-start(f32[32,16,128]{2,1,0:T(8,128)} %shard_map.85), calls=%async_computation.3 | async-start | bytes 524288 | tf_op jit(solution)/shard_map/all_to_all | solution.py:177
  89.3 1.0 copy-start.3
  102.0 19.4 %all-to-all-start.4 = ((bf16[8,128,512]{2,1,0:T(8,128)(2,1)}), bf16[8,128,512]{2,1,0:T(8,128)(2,1)S(1)}, u32[]{:S(2)}, u32[]{:S(2)}) async-start(bf16[8,128,512]{2,1,0:T(8,128)(2,1)} %broadcast_in_dim.41), calls=%async_computation.4 | async-start | bytes 2097152 | tf_op jit(solution)/shard_map/all_to_all | solution.py:181
  121.4 1.0 copy-start.2

commit v10 on v9

--- a/solution.py
+++ b/solution.py
@@ -66,35 +66,56 @@
     lax.fori_loop(0, 2 * pairs // rows_per_chunk, chunk, 0)
 
 
-def down_kernel(idx_ref, g_ref, w_ref, o_ref, src_ref, w2_ref, stage_ref):
-    sources, rows, cols = g_ref.shape
-    block_width = w_ref.shape[1]
-    shared_count = w_ref.shape[0] // block_width
-    own_blocks = o_ref.shape[1] // block_width
-    per_source = cols // LANES
-
-    def relayout(i, carry):
-        for m in range(per_source):
-            src_ref[i * per_source + m] = g_ref[i, :, m * LANES:(m + 1) * LANES]
+def dense_kernel(sid_ref, t_ref, m_ref):
+    width = t_ref.shape[1]
+    pairs = m_ref.shape[1] // LANES
+    low_lanes = lax.broadcasted_iota(jnp.int32, (width, LANES), 1) < width
+
+    def one(c, carry):
+        for q in range(pairs):
+            even = t_ref[sid_ref[c * 2 * pairs + 2 * q]]
+            odd = t_ref[sid_ref[c * 2 * pairs + 2 * q + 1]]
+            m_ref[pl.ds(pl.multiple_of(c * width, width), width), q * LANES:(q + 1) * LANES] = (
+                jnp.where(low_lanes, even, odd)
+            )
         return carry
 
-    lax.fori_loop(0, sources, relayout, 0)
-    for s in range(shared_count):
-        block = w_ref[s * block_width:(s + 1) * block_width, :]
-        w2_ref[s * LANES:s * LANES + block_width, :] = block
-        w2_ref[s * LANES + block_width:(s + 1) * LANES, :] = block
-    half_of_lane = jnp.where(
-        lax.broadcasted_iota(jnp.int32, (rows, LANES), 1) >= block_width, 1, 0
-    )
-    for r in range(own_blocks):
-        for s in range(shared_count):
-            c = idx_ref[r * shared_count + s]
-            piece = src_ref[lax.shift_right_logical(c, 1)]
-            keep = half_of_lane == (c & 1)
-            stage_ref[:, s * LANES:(s + 1) * LANES] = jnp.where(keep, piece, jnp.zeros_like(piece))
-        o_ref[:, r * block_width:(r + 1) * block_width] = jnp.dot(
-            stage_ref[...], w2_ref[...], preferred_element_type=jnp.float32
+    lax.fori_loop(0, m_ref.shape[0] // width, one, 0)
+
+
+def dense_hop_kernel(g_ref, m_ref, o_ref):
+    sources, _, cols = g_ref.shape
+    acc = jnp.dot(g_ref[0], m_ref[0:cols, :], preferred_element_type=jnp.float32)
+    for i in range(1, sources):
+        acc = acc + jnp.dot(
+            g_ref[i], m_ref[i * cols:(i + 1) * cols, :], preferred_element_type=jnp.float32
         )
+    o_ref[...] = acc
+
+
+def dense_table(sid, t2, strings, own_cols):
+    return pl.pallas_call(
+        dense_kernel,
+        out_shape=jax.ShapeDtypeStruct((strings, own_cols), jnp.bfloat16),
+        in_specs=[
+            pl.BlockSpec(memory_space=pltpu.SMEM),
+            pl.BlockSpec(memory_space=pltpu.VMEM),
+        ],
+        out_specs=pl.BlockSpec(memory_space=pltpu.VMEM),
+    )(sid, t2)
+
+
+def dense_hop(g, m):
+    _, rows, _ = g.shape
+    return pl.pallas_call(
+        dense_hop_kernel,
+        out_shape=jax.ShapeDtypeStruct((rows, m.shape[1]), jnp.float32),
+        in_specs=[
+            pl.BlockSpec(memory_space=pltpu.VMEM),
+            pl.BlockSpec(memory_space=pltpu.VMEM),
+        ],
+        out_specs=pl.BlockSpec(memory_space=pltpu.VMEM),
+    )(g, m)
 
 
 def transpose_round_kernel(x_ref, o_ref):
@@ -130,25 +151,6 @@
             pltpu.VMEM((rows_per_chunk * n, w.shape[0]), jnp.bfloat16),
         ],
     )(idx, x, w)
-
-
-def down_hop(idx, g, w, own_cols):
-    _, rows, _ = g.shape
-    return pl.pallas_call(
-        down_kernel,
-        out_shape=jax.ShapeDtypeStruct((rows, own_cols), jnp.float32),
-        in_specs=[
-            pl.BlockSpec(memory_space=pltpu.SMEM),
-            pl.BlockSpec(memory_space=pltpu.VMEM),
-            pl.BlockSpec(memory_space=pltpu.VMEM),
-        ],
-        out_specs=pl.BlockSpec(memory_space=pltpu.VMEM),
-        scratch_shapes=[
-            pltpu.VMEM((g.shape[0] * g.shape[2] // LANES, rows, LANES), jnp.bfloat16),
-            pltpu.VMEM((2 * w.shape[0], w.shape[1]), jnp.bfloat16),
-            pltpu.VMEM((rows, 2 * w.shape[0]), jnp.bfloat16),
-        ],
-    )(idx, g, w)
 
 
 def body(amplitudes, double_occ, up_cols, up_ids, up_blocks, down_cols, down_ids, down_blocks):
@@ -163,7 +165,6 @@
         down_order, lax.axis_index("down") * own_blocks, own_blocks, 0
     ).reshape(-1)
     up_table = up_blocks.reshape(shared_count * block_width, block_width)
-    down_table = down_blocks.reshape(shared_count * block_width, block_width)
     onsite = coupling * double_occ.astype(jnp.float32) - center
     col_chunk = local_cols // up_count
 
@@ -179,9 +180,19 @@
     def down_part(rounded):
         copies = jnp.broadcast_to(rounded[None], (lax.axis_size("down"),) + rounded.shape)
         gathered = lax.all_to_all(copies, "down", 0, 0, tiled=True)
-        return down_hop(down_idx, gathered, down_table, local_cols)
+        return dense_hop(gathered, down_dense)
 
     rounded0 = amplitudes.astype(jnp.bfloat16)
+    own_order = down_idx.reshape(own_blocks, shared_count)
+    block_ids = jnp.arange(lax.axis_size("down") * own_blocks, dtype=jnp.int32)
+    hit = own_order[None, :, :] == block_ids[:, None, None]
+    slot = jnp.sum(jnp.where(hit, jnp.arange(shared_count, dtype=jnp.int32) + 1, 0), axis=2)
+    sid = jnp.where(slot == 0, shared_count, slot - 1).reshape(-1)
+    padded = jnp.concatenate([down_blocks, jnp.zeros_like(down_blocks[:1])], axis=0)
+    down_dense = dense_table(
+        sid, jnp.concatenate([padded, padded], axis=2),
+        lax.axis_size("down") * local_cols, local_cols,
+    )
     sent0 = exchange_up(
         transpose_round(amplitudes).reshape(up_count, col_chunk, local_rows)
     )

time: 132 us -> 130 us (0.985)
  waiting for transfers between devices: 41.1 us -> 35.5 us
  other arithmetic: 3.98 us -> 6.97 us
  local copies, waits for them, and re-layouts: 7.7 us -> 6.21 us
    all_to_all x2, waiting for transfers between devices: 20.8 us -> 15.8 us  [down_part(): gathered = lax.all_to_all(copies, 'down', 0, 0, tiled=True)]
    unnamed x22 -> x20, local copies, waits for them, and re-layouts: 3.61 us -> 1.94 us
    pallas_call x2 -> x3, Pallas kernels: 11.9 us -> 12.8 us  [the longest x2 7.87 us: dense_hop(): pl.pallas_call(dense_hop_kernel, out_shape=jax.ShapeDtypeStruct((rows, m....]
  transfers between devices with their start and end apart: 4 -> 4, of which waited for: 4 -> 3; matrix products, arithmetic and copies ran while one was open for 2% -> 4% of each run, Pallas kernels for 7% -> 11%
where the time goes in v10:
time: 130 us; the launch traced here: 129 us
  waiting for transfers between devices  35.5 us (27%)
  Pallas kernels  32.5 us (25%)
  starting transfers between devices  25 us (19%)
  blocking collectives  22.4 us (17%)
  other arithmetic  6.97 us (5%)
  local copies, waits for them, and re-layouts  6.21 us (5%)
    all_to_all x1, blocking collectives, exchange_up(): return lax.all_to_all(pieces, 'up', 0, 0, tiled=True)  22.4 us
    all_to_all x2, waiting for transfers between devices, exchange_up(): return lax.all_to_all(pieces, 'up', 0, 0, tiled=True)  19.7 us
    pallas_call x2, Pallas kernels, up_hop(): pl.pallas_call(up_kernel, out_shape=jax.ShapeDtypeStruct((pairs, n, LANES...  18 us
    all_to_all x2, starting transfers between devices, exchange_up(): return lax.all_to_all(pieces, 'up', 0, 0, tiled=True)  16.2 us
    all_to_all x2, waiting for transfers between devices, down_part(): gathered = lax.all_to_all(copies, 'down', 0, 0, tiled=True)  15.8 us
    all_to_all x2, starting transfers between devices, down_part(): gathered = lax.all_to_all(copies, 'down', 0, 0, tiled=True)  8.85 us
    pallas_call x2, Pallas kernels, dense_hop(): pl.pallas_call(dense_hop_kernel, out_shape=jax.ShapeDtypeStruct((rows, m....  7.87 us
    pallas_call x1, Pallas kernels, dense_table(): pl.pallas_call(dense_kernel, out_shape=jax.ShapeDtypeStruct((strings, own...  4.89 us
  transfers between devices with their start and end apart: 4, of which 3 were waited for; matrix products, arithmetic and copies ran while one was open for 4% of the time, Pallas kernels for 11%

profile of v10, /device:TPU:32, one launch (start us, length us, event | category | flops | bytes accessed | tf_op | source)
XLA Modules:
  0.0 128.7 jit_solution(12844600563788424478)
XLA Ops:
  0.0 1.7 %shard_map.84 = bf16[512,128]{1,0:T(8,128)(2,1)} custom-call(f32[128,512]{1,0:T(8,128)} %x_ref.1), custom_call_target="tpu_custom_call" | custom-call | tf_op jit(solution)/shard_map/pallas_call | solution.py:129
  1.7 11.4 %all-to-all-start.1 = ((bf16[32,16,128]{2,1,0:T(8,128)(2,1)}), bf16[32,16,128]{2,1,0:T(8,128)(2,1)S(1)}, u32[]{:S(2)}, u32[]{:S(2)}) async-start(bf16[32,16,128]{2,1,0:T(8,128)(2,1)} %bitcast.26), calls=%async_computation.1 | async-start | bytes 262144 | tf_op jit(solution)/shard_map/all_to_all | solution.py:178
  13.1 0.8 select_reduce_fusion.1
  13.9 1.0 convert_element_type.13
  14.9 0.1 constant_dynamic-slice_fusion
  15.0 0.1 copy.23
  15.0 7.8 %all-to-all-done.1.x_ref = bf16[32,16,128]{2,1,0:T(8,128)(2,1)S(1)} async-done(((bf16[32,16,128]{2,1,0:T(8,128)(2,1)}), bf16[32,16,128]{2,1,0:T(8,128)(2,1)S(1)}, u32[]{:S(2)}, u32[]{:S(2)}) %all-to-all-start.1) | async-done | bytes 131104 | tf_op jit(solution)/shard_map/all_to_all | solution.py:178
  22.9 1.0 broadcast_in_dim.51
  23.9 0.0 copy-done.6
  23.9 4.4 %all-to-all-start = ((bf16[8,128,512]{2,1,0:T(8,128)(2,1)}), bf16[8,128,512]{2,1,0:T(8,128)(2,1)S(1)}, u32[]{:S(2)}, u32[]{:S(2)}) async-start(bf16[8,128,512]{2,1,0:T(8,128)(2,1)} %broadcast_in_dim.51), calls=%async_computation | async-start | bytes 2097152 | tf_op jit(solution)/shard_map/all_to_all | solution.py:182
  28.4 0.1 select_reduce_fusion.2
  28.5 0.1 copy.24
  28.6 0.7 select_n.37.sid_ref
  29.3 0.0 copy-done.8
  29.3 0.0 copy-done.9
  29.3 0.1 select_reduce_fusion
  29.4 0.1 shift-right-arithmetic_add_fusion
  29.4 0.1 copy.26
  29.5 0.7 add.53.idx_ref
  30.2 0.0 copy-done.7
  30.2 0.1 concatenate.9
  30.4 1.1 pad_maximum_fusion.t_ref
  31.5 4.9 %shard_map.82.m_ref = bf16[4096,512]{1,0:T(8,128)(2,1)} custom-call(s32[512]{0:T(512)} %select_n.37.sid_ref, bf16[33,64,128]{2,1,0:T(8,128)(2,1)} %pad_maximum_fusion.t_ref), custom_call_target="tpu_custom_call" | custom-call | tf_op jit(solution)/shard_map/pallas_call | solution.py:97
  36.4 9.0 %shard_map.85 = f32[32,16,128]{2,1,0:T(8,128)} custom-call(s32[2048]{0:T(1024)} %add.53.idx_ref, bf16[32,16,128]{2,1,0:T(8,128)(2,1)} %copy-done.6, bf16[2048,64]{1,0:T(8,128)(2,1)} %bitcast.21), custom_call_target="tpu_custom_call" | custom-call | tf_op jit(solution)/shard_map/pallas_call | solution.py:140
  45.4 0.0 all-to-all-done.g_ref
  45.4 0.0 copy-start.1
  45.4 0.9 copy-done.1
  46.3 3.9 %shard_map.83 = f32[128,512]{1,0:T(8,128)} custom-call(bf16[8,128,512]{2,1,0:T(8,128)(2,1)} %copy-done.1, bf16[4096,512]{1,0:T(8,128)(2,1)} %shard_map.82.m_ref), custom_call_target="tpu_custom_call" | custom-call | tf_op jit(solution)/shard_map/pallas_call | solution.py:110
  50.3 0.0 copy-done
  50.3 0.0 copy-done.4
  50.3 1.1 fusion.6
  51.3 0.1 copy.25
  51.5 0.0 copy-done.5
  51.5 0.1 pad_maximum_fusion.1
  51.5 22.4 %all_to_all.25 = f32[32,32,128]{2,1,0:T(8,128)S(1)} all-to-all(f32[32,32,128]{2,1,0:T(8,128)S(1)} %pad_maximum_fusion.1), channel_id=1, replica_groups=mesh['up'=32,'down'=8] {'up'}, dimensions={0} | all-to-all | bytes 1048576 | tf_op jit(solution)/shard_map/all_to_all | solution.py:178
  73.9 0.7 fusion.1
  74.6 9.0 %shard_map.86 = f32[32,16,128]{2,1,0:T(8,128)} custom-call(s32[2048]{0:T(1024)} %add.53.idx_ref, bf16[32,16,128]{2,1,0:T(8,128)(2,1)} %get-tuple-element.5.x_ref, bf16[2048,64]{1,0:T(8,128)(2,1)} %bitcast.22), custom_call_target="tpu_custom_call" | custom-call | tf_op jit(solution)/shard_map/pallas_call | solution.py:140
  83.6 4.8 %all-to-all-start.3 = ((f32[32,16,128]{2,1,0:T(8,128)}), f32[32,16,128]{2,1,0:T(8,128)S(1)}, u32[]{:S(2)}, u32[]{:S(2)}) async-start(f32[32,16,128]{2,1,0:T(8,128)} %shard_map.86), calls=%async_computation.3 | async-start | bytes 524288 | tf_op jit(solution)/shard_map/all_to_all | solution.py:178
  88.5 0.1 copy.27
  88.6 0.1 fusion.5
  88.7 11.8 %all-to-all-done.3 = f32[32,16,128]{2,1,0:T(8,128)S(1)} async-done(((f32[32,16,128]{2,1,0:T(8,128)}), f32[32,16,128]{2,1,0:T(8,128)S(1)}, u32[]{:S(2)}, u32[]{:S(2)}) %all-to-all-start.3) | async-done | bytes 262176 | tf_op jit(solution)/shard_map/all_to_all | solution.py:178
  100.6 1.0 broadcast_in_dim.58
  101.6 4.4 %all-to-all-start.4 = ((bf16[8,128,512]{2,1,0:T(8,128)(2,1)}), bf16[8,128,512]{2,1,0:T(8,128)(2,1)S(1)}, u32[]{:S(2)}, u32[]{:S(2)}) async-start(bf16[8,128,512]{2,1,0:T(8,128)(2,1)} %broadcast_in_dim.58), calls=%async_computation.4 | async-start | bytes 2097152 | tf_op jit(solution)/shard_map/all_to_all | solution.py:182
  106.0 0.1 copy.28
  106.1 15.8 %all-to-all-done.4.g_ref = bf16[8,128,512]{2,1,0:T(8,128)(2,1)S(1)} async-done(((bf16[8,128,512]{2,1,0:T(8,128)(2,1)}), bf16[8,128,512]{2,1,0:T(8,128)(2,1)S(1)}, u32[]{:S(2)}, u32[]{:S(2)}) %all-to-all-start.4) | async-done | bytes 1048608 | tf_op jit(solution)/shard_map/all_to_all | solution.py:182
  121.9 1.0 copy-done.2
  122.9 3.9 %shard_map.87 = f32[128,512]{1,0:T(8,128)} custom-call(bf16[8,128,512]{2,1,0:T(8,128)(2,1)} %copy-done.2, bf16[4096,512]{1,0:T(8,128)(2,1)} %shard_map.82.m_ref), custom_call_target="tpu_custom_call" | custom-call | tf_op jit(solution)/shard_map/pallas_call | solution.py:110
  126.8 1.8 %fusion.3 = f32[128,512]{1,0:T(8,128)} fusion(f32[128,512]{1,0:T(8,128)S(1)} %copy-done, f32[128,512]{1,0:T(8,128)} %shard_map.87, f32[512,128]{0,1:T(8,128)S(1)} %copy.28, s32[128,512]{1,0:T(8,128)S(1)} %copy-done.4, f32[512,128]{0,1:T(8,128)S(1)} %copy.27, f32[128,512]{1,0:T(8,128)S(1)} %copy-done.3), kind=kLoop, calls=%fused_computation.11 | loop fusion | flops 720896 | bytes 1835008 | tf_op jit(solution)/shard_map/sub | solution.py:210
  (13 shorter events, 0.0 us)
Async XLA Ops:
  1.7 21.2 %all-to-all-start.1 = ((bf16[32,16,128]{2,1,0:T(8,128)(2,1)}), bf16[32,16,128]{2,1,0:T(8,128)(2,1)S(1)}, u32[]{:S(2)}, u32[]{:S(2)}) async-start(bf16[32,16,128]{2,1,0:T(8,128)(2,1)} %bitcast.26), calls=%async_computation.1 | async-start | bytes 262144 | tf_op jit(solution)/shard_map/all_to_all | solution.py:178
  22.9 1.1 copy-start.6
  23.9 5.4 %copy-start.8 = (s32[64,32]{0,1:T(8,128)S(1)}, s32[64,32]{0,1:T(8,128)}, u32[]{:S(2)}) copy-start(s32[64,32]{0,1:T(8,128)} %param.10) | copy-start | bytes 24580
  23.9 5.4 %copy-start.9 = (s32[64,32]{0,1:T(8,128)S(1)}, s32[64,32]{0,1:T(8,128)}, u32[]{:S(2)}) copy-start(s32[64,32]{0,1:T(8,128)} %param.11) | copy-start | bytes 24580
  23.9 6.3 %copy-start.7 = (bf16[32,64,64]{2,1,0:T(8,128)(2,1)S(1)}, bf16[32,64,64]{2,1,0:T(8,128)(2,1)}, u32[]{:S(2)}) copy-start(bf16[32,64,64]{2,1,0:T(8,128)(2,1)} %param.15) | copy-start | bytes 786436
  23.9 21.4 %all-to-all-start = ((bf16[8,128,512]{2,1,0:T(8,128)(2,1)}), bf16[8,128,512]{2,1,0:T(8,128)(2,1)S(1)}, u32[]{:S(2)}, u32[]{:S(2)}) async-start(bf16[8,128,512]{2,1,0:T(8,128)(2,1)} %broadcast_in_dim.51), calls=%async_computation | async-start | bytes 2097152 | tf_op jit(solution)/shard_map/all_to_all | solution.py:182
  45.4 4.9 %copy-start = (f32[128,512]{1,0:T(8,128)S(1)}, f32[128,512]{1,0:T(8,128)}, u32[]{:S(2)}) copy-start(f32[128,512]{1,0:T(8,128)} %x_ref.1) | copy-start | bytes 786436
  45.4 4.9 %copy-start.4 = (s32[128,512]{1,0:T(8,128)S(1)}, s32[128,512]{1,0:T(8,128)}, u32[]{:S(2)}) copy-start(s32[128,512]{1,0:T(8,128)} %param.9) | copy-start | bytes 786436
  45.4 1.0 copy-start.1
  50.3 1.2 copy-start.5
  74.6 14.0 %copy-start.3 = (f32[128,512]{1,0:T(8,128)S(1)}, f32[128,512]{1,0:T(8,128)}, u32[]{:S(2)}) copy-start(f32[128,512]{1,0:T(8,128)} %shard_map.83) | copy-start | bytes 786436
  83.6 16.9 %all-to-all-start.3 = ((f32[32,16,128]{2,1,0:T(8,128)}), f32[32,16,128]{2,1,0:T(8,128)S(1)}, u32[]{:S(2)}, u32[]{:S(2)}) async-start(f32[32,16,128]{2,1,0:T(8,128)} %shard_map.86), calls=%async_computation.3 | async-start | bytes 524288 | tf_op jit(solution)/shard_map/all_to_all | solution.py:178
  101.6 20.3 %all-to-all-start.4 = ((bf16[8,128,512]{2,1,0:T(8,128)(2,1)}), bf16[8,128,512]{2,1,0:T(8,128)(2,1)S(1)}, u32[]{:S(2)}, u32[]{:S(2)}) async-start(bf16[8,128,512]{2,1,0:T(8,128)(2,1)} %broadcast_in_dim.58), calls=%async_computation.4 | async-start | bytes 2097152 | tf_op jit(solution)/shard_map/all_to_all | solution.py:182
  121.9 1.0 copy-start.2

commit v11 on v10

--- a/solution.py
+++ b/solution.py
@@ -66,15 +66,34 @@
     lax.fori_loop(0, 2 * pairs // rows_per_chunk, chunk, 0)
 
 
-def dense_kernel(sid_ref, t_ref, m_ref):
-    width = t_ref.shape[1]
-    pairs = m_ref.shape[1] // LANES
+def dense_kernel(own_ref, blocks_ref, m_ref, sid_ref, t_ref):
+    shared_count, width, _ = blocks_ref.shape
+    own_blocks = m_ref.shape[1] // width
+    pairs = own_blocks // 2
+
+    def clear(i, carry):
+        sid_ref[i] = shared_count
+        return carry
+
+    lax.fori_loop(0, sid_ref.shape[0], clear, 0)
+
+    def scatter(k, carry):
+        r = k // shared_count
+        sid_ref[own_ref[k] * own_blocks + r] = k % shared_count
+        return carry
+
+    lax.fori_loop(0, own_blocks * shared_count, scatter, 0)
+    for s in range(shared_count):
+        block = blocks_ref[s]
+        t_ref[s, :, 0:width] = block
+        t_ref[s, :, width:2 * width] = block
+    t_ref[shared_count] = jnp.zeros(t_ref.shape[1:], t_ref.dtype)
     low_lanes = lax.broadcasted_iota(jnp.int32, (width, LANES), 1) < width
 
     def one(c, carry):
         for q in range(pairs):
-            even = t_ref[sid_ref[c * 2 * pairs + 2 * q]]
-            odd = t_ref[sid_ref[c * 2 * pairs + 2 * q + 1]]
+            even = t_ref[sid_ref[c * own_blocks + 2 * q]]
+            odd = t_ref[sid_ref[c * own_blocks + 2 * q + 1]]
             m_ref[pl.ds(pl.multiple_of(c * width, width), width), q * LANES:(q + 1) * LANES] = (
                 jnp.where(low_lanes, even, odd)
             )
@@ -93,7 +112,8 @@
     o_ref[...] = acc
 
 
-def dense_table(sid, t2, strings, own_cols):
+def dense_table(own_order, blocks, strings, own_cols):
+    shared_count, width, _ = blocks.shape
     return pl.pallas_call(
         dense_kernel,
         out_shape=jax.ShapeDtypeStruct((strings, own_cols), jnp.bfloat16),
@@ -102,7 +122,11 @@
             pl.BlockSpec(memory_space=pltpu.VMEM),
         ],
         out_specs=pl.BlockSpec(memory_space=pltpu.VMEM),
-    )(sid, t2)
+        scratch_shapes=[
+            pltpu.SMEM(((strings // width) * (own_cols // width),), jnp.int32),
+            pltpu.VMEM((shared_count + 1, width, 2 * width), blocks.dtype),
+        ],
+    )(own_order, blocks)
 
 
 def dense_hop(g, m):
@@ -183,16 +207,7 @@
         return dense_hop(gathered, down_dense)
 
     rounded0 = amplitudes.astype(jnp.bfloat16)
-    own_order = down_idx.reshape(own_blocks, shared_count)
-    block_ids = jnp.arange(lax.axis_size("down") * own_blocks, dtype=jnp.int32)
-    hit = own_order[None, :, :] == block_ids[:, None, None]
-    slot = jnp.sum(jnp.where(hit, jnp.arange(shared_count, dtype=jnp.int32) + 1, 0), axis=2)
-    sid = jnp.where(slot == 0, shared_count, slot - 1).reshape(-1)
-    padded = jnp.concatenate([down_blocks, jnp.zeros_like(down_blocks[:1])], axis=0)
-    down_dense = dense_table(
-        sid, jnp.concatenate([padded, padded], axis=2),
-        lax.axis_size("down") * local_cols, local_cols,
-    )
+    down_dense = dense_table(down_idx, down_blocks, lax.axis_size("down") * local_cols, local_cols)
     sent0 = exchange_up(
         transpose_round(amplitudes).reshape(up_count, col_chunk, local_rows)
     )

time: 130 us -> 135 us (1.038)
  Pallas kernels: 32.5 us -> 38.6 us
  other arithmetic: 6.97 us -> 5.02 us
    pallas_call x1, Pallas kernels: 4.89 us -> 11 us  [dense_table(): pl.pallas_call(dense_kernel, out_shape=jax.ShapeDtypeStruct((strings, own...]
  transfers between devices with their start and end apart: 4 -> 4, of which waited for: 3 -> 3; matrix products, arithmetic and copies ran while one was open for 4% -> 2% of each run, Pallas kernels for 11% -> 15%
where the time goes in v11:
time: 135 us; the launch traced here: 133 us
  Pallas kernels  38.6 us (29%)
  waiting for transfers between devices  36.5 us (27%)
  starting transfers between devices  24.9 us (18%)
  blocking collectives  22.4 us (17%)
  local copies, waits for them, and re-layouts  6.03 us (4%)
  other arithmetic  5.02 us (4%)
    all_to_all x1, blocking collectives, exchange_up(): return lax.all_to_all(pieces, 'up', 0, 0, tiled=True)  22.4 us
    all_to_all x2, waiting for transfers between devices, exchange_up(): return lax.all_to_all(pieces, 'up', 0, 0, tiled=True)  20.7 us
    pallas_call x2, Pallas kernels, up_hop(): pl.pallas_call(up_kernel, out_shape=jax.ShapeDtypeStruct((pairs, n, LANES...  18 us
    all_to_all x2, starting transfers between devices, exchange_up(): return lax.all_to_all(pieces, 'up', 0, 0, tiled=True)  16.2 us
    all_to_all x2, waiting for transfers between devices, down_part(): gathered = lax.all_to_all(copies, 'down', 0, 0, tiled=True)  15.8 us
    pallas_call x1, Pallas kernels, dense_table(): pl.pallas_call(dense_kernel, out_shape=jax.ShapeDtypeStruct((strings, own...  11 us
    all_to_all x2, starting transfers between devices, down_part(): gathered = lax.all_to_all(copies, 'down', 0, 0, tiled=True)  8.69 us
    pallas_call x2, Pallas kernels, dense_hop(): pl.pallas_call(dense_hop_kernel, out_shape=jax.ShapeDtypeStruct((rows, m....  7.87 us
  transfers between devices with their start and end apart: 4, of which 3 were waited for; matrix products, arithmetic and copies ran while one was open for 2% of the time, Pallas kernels for 15%

profile of v11, /device:TPU:32, one launch (start us, length us, event | category | flops | bytes accessed | tf_op | source)
XLA Modules:
  0.0 133.5 jit_solution(15498694068359166035)
XLA Ops:
  0.0 0.0 copy-start.7
  0.0 0.0 copy-start.8
  0.0 0.0 copy-start.10
  0.0 1.8 %shard_map.84 = bf16[512,128]{1,0:T(8,128)(2,1)} custom-call(f32[128,512]{1,0:T(8,128)} %x_ref.1), custom_call_target="tpu_custom_call" | custom-call | tf_op jit(solution)/shard_map/pallas_call | solution.py:153
  1.8 11.4 %all-to-all-start.1 = ((bf16[32,16,128]{2,1,0:T(8,128)(2,1)}), bf16[32,16,128]{2,1,0:T(8,128)(2,1)S(1)}, u32[]{:S(2)}, u32[]{:S(2)}) async-start(bf16[32,16,128]{2,1,0:T(8,128)(2,1)} %bitcast.26), calls=%async_computation.1 | async-start | bytes 262144 | tf_op jit(solution)/shard_map/all_to_all | solution.py:202
  13.1 1.0 convert_element_type.13
  14.1 8.8 %all-to-all-done.1.x_ref = bf16[32,16,128]{2,1,0:T(8,128)(2,1)S(1)} async-done(((bf16[32,16,128]{2,1,0:T(8,128)(2,1)}), bf16[32,16,128]{2,1,0:T(8,128)(2,1)S(1)}, u32[]{:S(2)}, u32[]{:S(2)}) %all-to-all-start.1) | async-done | bytes 131104 | tf_op jit(solution)/shard_map/all_to_all | solution.py:202
  22.9 1.1 broadcast_in_dim.22
  24.0 4.3 %all-to-all-start = ((bf16[8,128,512]{2,1,0:T(8,128)(2,1)}), bf16[8,128,512]{2,1,0:T(8,128)(2,1)S(1)}, u32[]{:S(2)}, u32[]{:S(2)}) async-start(bf16[8,128,512]{2,1,0:T(8,128)(2,1)} %broadcast_in_dim.22), calls=%async_computation | async-start | bytes 2097152 | tf_op jit(solution)/shard_map/all_to_all | solution.py:206
  28.3 0.0 copy-done.7
  28.3 0.0 copy-done.8
  28.3 0.1 select_reduce_fusion.1
  28.4 0.1 constant_dynamic-slice_fusion
  28.5 0.1 copy.27
  28.6 0.6 reshape.44.own_ref
  29.2 0.0 copy-done.9
  29.2 0.0 copy-done.10
  29.2 0.1 select_reduce_fusion
  29.3 0.1 shift-right-arithmetic_add_fusion
  29.4 0.1 copy.29
  29.5 0.7 add.40.idx_ref
  30.1 11.0 %shard_map.82.m_ref = bf16[4096,512]{1,0:T(8,128)(2,1)} custom-call(s32[256]{0:T(256)} %reshape.44.own_ref, bf16[32,64,64]{2,1,0:T(8,128)(2,1)} %blocks_ref.1), custom_call_target="tpu_custom_call" | custom-call | tf_op jit(solution)/shard_map/pallas_call | solution.py:117
  41.1 0.0 copy-done.6
  41.2 9.0 %shard_map.85 = f32[32,16,128]{2,1,0:T(8,128)} custom-call(s32[2048]{0:T(1024)} %add.40.idx_ref, bf16[32,16,128]{2,1,0:T(8,128)(2,1)} %copy-done.6, bf16[2048,64]{1,0:T(8,128)(2,1)} %bitcast.21), custom_call_target="tpu_custom_call" | custom-call | tf_op jit(solution)/shard_map/pallas_call | solution.py:164
  50.2 0.0 all-to-all-done.g_ref
  50.2 1.0 copy-done.1
  51.2 3.9 %shard_map.83 = f32[128,512]{1,0:T(8,128)} custom-call(bf16[8,128,512]{2,1,0:T(8,128)(2,1)} %copy-done.1, bf16[4096,512]{1,0:T(8,128)(2,1)} %shard_map.82.m_ref), custom_call_target="tpu_custom_call" | custom-call | tf_op jit(solution)/shard_map/pallas_call | solution.py:134
  55.1 0.0 copy-done
  55.1 0.0 copy-done.4
  55.1 1.1 fusion.6
  56.2 0.1 copy.28
  56.3 0.0 copy-done.5
  56.3 0.1 pad_maximum_fusion
  56.4 22.4 %all_to_all.25 = f32[32,32,128]{2,1,0:T(8,128)S(1)} all-to-all(f32[32,32,128]{2,1,0:T(8,128)S(1)} %pad_maximum_fusion), channel_id=1, replica_groups=mesh['up'=32,'down'=8] {'up'}, dimensions={0} | all-to-all | bytes 1048576 | tf_op jit(solution)/shard_map/all_to_all | solution.py:202
  78.7 0.7 fusion.1
  79.5 9.0 %shard_map.86 = f32[32,16,128]{2,1,0:T(8,128)} custom-call(s32[2048]{0:T(1024)} %add.40.idx_ref, bf16[32,16,128]{2,1,0:T(8,128)(2,1)} %get-tuple-element.5.x_ref, bf16[2048,64]{1,0:T(8,128)(2,1)} %bitcast.22), custom_call_target="tpu_custom_call" | custom-call | tf_op jit(solution)/shard_map/pallas_call | solution.py:164
  88.4 4.8 %all-to-all-start.3 = ((f32[32,16,128]{2,1,0:T(8,128)}), f32[32,16,128]{2,1,0:T(8,128)S(1)}, u32[]{:S(2)}, u32[]{:S(2)}) async-start(f32[32,16,128]{2,1,0:T(8,128)} %shard_map.86), calls=%async_computation.3 | async-start | bytes 524288 | tf_op jit(solution)/shard_map/all_to_all | solution.py:202
  93.3 0.1 copy.30
  93.4 0.0 copy-done.3
  93.4 0.1 fusion.5
  93.5 11.8 %all-to-all-done.3 = f32[32,16,128]{2,1,0:T(8,128)S(1)} async-done(((f32[32,16,128]{2,1,0:T(8,128)}), f32[32,16,128]{2,1,0:T(8,128)S(1)}, u32[]{:S(2)}, u32[]{:S(2)}) %all-to-all-start.3) | async-done | bytes 262176 | tf_op jit(solution)/shard_map/all_to_all | solution.py:202
  105.4 1.1 broadcast_in_dim.41
  106.5 4.4 %all-to-all-start.4 = ((bf16[8,128,512]{2,1,0:T(8,128)(2,1)}), bf16[8,128,512]{2,1,0:T(8,128)(2,1)S(1)}, u32[]{:S(2)}, u32[]{:S(2)}) async-start(bf16[8,128,512]{2,1,0:T(8,128)(2,1)} %broadcast_in_dim.41), calls=%async_computation.4 | async-start | bytes 2097152 | tf_op jit(solution)/shard_map/all_to_all | solution.py:206
  110.8 0.1 copy.31
  111.0 15.8 %all-to-all-done.4.g_ref = bf16[8,128,512]{2,1,0:T(8,128)(2,1)S(1)} async-done(((bf16[8,128,512]{2,1,0:T(8,128)(2,1)}), bf16[8,128,512]{2,1,0:T(8,128)(2,1)S(1)}, u32[]{:S(2)}, u32[]{:S(2)}) %all-to-all-start.4) | async-done | bytes 1048608 | tf_op jit(solution)/shard_map/all_to_all | solution.py:206
  126.8 1.0 copy-done.2
  127.8 3.9 %shard_map.87 = f32[128,512]{1,0:T(8,128)} custom-call(bf16[8,128,512]{2,1,0:T(8,128)(2,1)} %copy-done.2, bf16[4096,512]{1,0:T(8,128)(2,1)} %shard_map.82.m_ref), custom_call_target="tpu_custom_call" | custom-call | tf_op jit(solution)/shard_map/pallas_call | solution.py:134
  131.7 1.8 %fusion.3 = f32[128,512]{1,0:T(8,128)} fusion(f32[128,512]{1,0:T(8,128)S(1)} %copy-done, f32[128,512]{1,0:T(8,128)} %shard_map.87, f32[512,128]{0,1:T(8,128)S(1)} %copy.31, s32[128,512]{1,0:T(8,128)S(1)} %copy-done.4, f32[512,128]{0,1:T(8,128)S(1)} %copy.30, f32[128,512]{1,0:T(8,128)S(1)} %copy-done.3), kind=kLoop, calls=%fused_computation.10 | loop fusion | flops 720896 | bytes 1835008 | tf_op jit(solution)/shard_map/sub | solution.py:225
  (9 shorter events, 0.0 us)
Async XLA Ops:
  0.0 28.3 %copy-start.7 = (s32[64,32]{0,1:T(8,128)S(1)}, s32[64,32]{0,1:T(8,128)}, u32[]{:S(2)}) copy-start(s32[64,32]{0,1:T(8,128)} %param.13) | copy-start | bytes 24580
  0.0 28.3 %copy-start.8 = (s32[64,32]{0,1:T(8,128)S(1)}, s32[64,32]{0,1:T(8,128)}, u32[]{:S(2)}) copy-start(s32[64,32]{0,1:T(8,128)} %param.14) | copy-start | bytes 24580
  0.0 29.2 %copy-start.9 = (s32[64,32]{0,1:T(8,128)S(1)}, s32[64,32]{0,1:T(8,128)}, u32[]{:S(2)}) copy-start(s32[64,32]{0,1:T(8,128)} %param.10) | copy-start | bytes 24580
  0.0 29.2 %copy-start.10 = (s32[64,32]{0,1:T(8,128)S(1)}, s32[64,32]{0,1:T(8,128)}, u32[]{:S(2)}) copy-start(s32[64,32]{0,1:T(8,128)} %param.11) | copy-start | bytes 24580
  1.8 21.2 %all-to-all-start.1 = ((bf16[32,16,128]{2,1,0:T(8,128)(2,1)}), bf16[32,16,128]{2,1,0:T(8,128)(2,1)S(1)}, u32[]{:S(2)}, u32[]{:S(2)}) async-start(bf16[32,16,128]{2,1,0:T(8,128)(2,1)} %bitcast.26), calls=%async_computation.1 | async-start | bytes 262144 | tf_op jit(solution)/shard_map/all_to_all | solution.py:202
  22.9 18.2 %copy-start.6 = (bf16[32,16,128]{2,1,0:T(8,128)(2,1)}, bf16[32,16,128]{2,1,0:T(8,128)(2,1)S(1)}, u32[]{:S(2)}) copy-start(bf16[32,16,128]{2,1,0:T(8,128)(2,1)S(1)} %all-to-all-done.1.x_ref) | copy-start | bytes 393220
  24.0 26.2 %all-to-all-start = ((bf16[8,128,512]{2,1,0:T(8,128)(2,1)}), bf16[8,128,512]{2,1,0:T(8,128)(2,1)S(1)}, u32[]{:S(2)}, u32[]{:S(2)}) async-start(bf16[8,128,512]{2,1,0:T(8,128)(2,1)} %broadcast_in_dim.22), calls=%async_computation | async-start | bytes 2097152 | tf_op jit(solution)/shard_map/all_to_all | solution.py:206
  41.1 14.0 %copy-start = (f32[128,512]{1,0:T(8,128)S(1)}, f32[128,512]{1,0:T(8,128)}, u32[]{:S(2)}) copy-start(f32[128,512]{1,0:T(8,128)} %x_ref.1) | copy-start | bytes 786436
  41.1 14.0 %copy-start.4 = (s32[128,512]{1,0:T(8,128)S(1)}, s32[128,512]{1,0:T(8,128)}, u32[]{:S(2)}) copy-start(s32[128,512]{1,0:T(8,128)} %param.9) | copy-start | bytes 786436
  50.2 6.2 %copy-start.5 = (f32[32,16,128]{2,1,0:T(8,128)S(1)}, f32[32,16,128]{2,1,0:T(8,128)}, u32[]{:S(2)}) copy-start(f32[32,16,128]{2,1,0:T(8,128)} %shard_map.85) | copy-start | bytes 786436
  50.2 1.0 copy-start.1
  55.1 38.3 %copy-start.3 = (f32[128,512]{1,0:T(8,128)S(1)}, f32[128,512]{1,0:T(8,128)}, u32[]{:S(2)}) copy-start(f32[128,512]{1,0:T(8,128)} %shard_map.83) | copy-start | bytes 786436
  88.4 17.0 %all-to-all-start.3 = ((f32[32,16,128]{2,1,0:T(8,128)}), f32[32,16,128]{2,1,0:T(8,128)S(1)}, u32[]{:S(2)}, u32[]{:S(2)}) async-start(f32[32,16,128]{2,1,0:T(8,128)} %shard_map.86), calls=%async_computation.3 | async-start | bytes 524288 | tf_op jit(solution)/shard_map/all_to_all | solution.py:202
  106.5 20.3 %all-to-all-start.4 = ((bf16[8,128,512]{2,1,0:T(8,128)(2,1)}), bf16[8,128,512]{2,1,0:T(8,128)(2,1)S(1)}, u32[]{:S(2)}, u32[]{:S(2)}) async-start(bf16[8,128,512]{2,1,0:T(8,128)(2,1)} %broadcast_in_dim.41), calls=%async_computation.4 | async-start | bytes 2097152 | tf_op jit(solution)/shard_map/all_to_all | solution.py:206
  126.8 1.0 copy-start.2

commit v12 on v9

--- a/solution.py
+++ b/solution.py
@@ -66,7 +66,7 @@
     lax.fori_loop(0, 2 * pairs // rows_per_chunk, chunk, 0)
 
 
-def down_kernel(idx_ref, g_ref, w_ref, o_ref, src_ref, w2_ref, stage_ref):
+def down_kernel(idx_ref, g_ref, w_ref, a_ref, b_ref, o_ref, src_ref, w2_ref, stage_ref):
     sources, rows, cols = g_ref.shape
     block_width = w_ref.shape[1]
     shared_count = w_ref.shape[0] // block_width
@@ -92,7 +92,8 @@
             piece = src_ref[lax.shift_right_logical(c, 1)]
             keep = half_of_lane == (c & 1)
             stage_ref[:, s * LANES:(s + 1) * LANES] = jnp.where(keep, piece, jnp.zeros_like(piece))
-        o_ref[:, r * block_width:(r + 1) * block_width] = jnp.dot(
+        cols_r = slice(r * block_width, (r + 1) * block_width)
+        o_ref[:, cols_r] = a_ref[:, cols_r] * b_ref[:, cols_r] + jnp.dot(
             stage_ref[...], w2_ref[...], preferred_element_type=jnp.float32
         )
 
@@ -132,13 +133,15 @@
     )(idx, x, w)
 
 
-def down_hop(idx, g, w, own_cols):
+def down_hop(idx, g, w, a, b):
     _, rows, _ = g.shape
     return pl.pallas_call(
         down_kernel,
-        out_shape=jax.ShapeDtypeStruct((rows, own_cols), jnp.float32),
+        out_shape=jax.ShapeDtypeStruct(a.shape, jnp.float32),
         in_specs=[
             pl.BlockSpec(memory_space=pltpu.SMEM),
+            pl.BlockSpec(memory_space=pltpu.VMEM),
+            pl.BlockSpec(memory_space=pltpu.VMEM),
             pl.BlockSpec(memory_space=pltpu.VMEM),
             pl.BlockSpec(memory_space=pltpu.VMEM),
         ],
@@ -148,7 +151,7 @@
             pltpu.VMEM((2 * w.shape[0], w.shape[1]), jnp.bfloat16),
             pltpu.VMEM((rows, 2 * w.shape[0]), jnp.bfloat16),
         ],
-    )(idx, g, w)
+    )(idx, g, w, a, b)
 
 
 def body(amplitudes, double_occ, up_cols, up_ids, up_blocks, down_cols, down_ids, down_blocks):
@@ -176,17 +179,17 @@
     def exchange_up(pieces):
         return lax.all_to_all(pieces, "up", 0, 0, tiled=True)
 
-    def down_part(rounded):
+    def down_part(current, rounded):
         copies = jnp.broadcast_to(rounded[None], (lax.axis_size("down"),) + rounded.shape)
         gathered = lax.all_to_all(copies, "down", 0, 0, tiled=True)
-        return down_hop(down_idx, gathered, down_table, local_cols)
+        return down_hop(down_idx, gathered, down_table, onsite, current)
 
     rounded0 = amplitudes.astype(jnp.bfloat16)
     sent0 = exchange_up(
         transpose_round(amplitudes).reshape(up_count, col_chunk, local_rows)
     )
     up0_cols = up_hop(up_idx, sent0, up_table)
-    partial_rows = onsite * amplitudes + down_part(rounded0)
+    partial_rows = down_part(amplitudes, rounded0)
     both = exchange_up(jnp.concatenate([to_columns(partial_rows), up0_cols], axis=1))
     partial_cols = both[:, :col_chunk]
     up0_rows = to_rows(both[:, col_chunk:])
@@ -194,9 +197,9 @@
     first_rows = (partial_rows + up0_rows) / half_span
 
     up1_cols = up_hop(up_idx, first_cols.astype(jnp.bfloat16), up_table)
-    down1_rows = down_part(first_rows.astype(jnp.bfloat16))
+    known_rows = down_part(first_rows, first_rows.astype(jnp.bfloat16))
     up1_rows = to_rows(exchange_up(up1_cols))
-    return 2.0 * ((onsite * first_rows + up1_rows + down1_rows) / half_span) - amplitudes
+    return 2.0 * ((known_rows + up1_rows) / half_span) - amplitudes
 
 
 def solution(mesh):

time: 132 us -> 131 us (level)
  waiting for transfers between devices: 41.1 us -> 39.7 us
    unnamed x22 -> x24, local copies, waits for them, and re-layouts: 3.61 us -> 2.79 us
  transfers between devices with their start and end apart: 4 -> 4, of which waited for: 4 -> 4; matrix products, arithmetic and copies ran while one was open for 2% -> 3% of each run, Pallas kernels for 7% -> 7%
where the time goes in v12:
time: 131 us; the launch traced here: 130 us
  waiting for transfers between devices  39.7 us (30%)
  Pallas kernels  31.9 us (24%)
  starting transfers between devices  24.2 us (18%)
  blocking collectives  21.4 us (16%)
  local copies, waits for them, and re-layouts  7.87 us (6%)
  other arithmetic  4.26 us (3%)
    all_to_all x1, blocking collectives, exchange_up(): return lax.all_to_all(pieces, 'up', 0, 0, tiled=True)  21.4 us
    all_to_all x2, waiting for transfers between devices, down_part(): gathered = lax.all_to_all(copies, 'down', 0, 0, tiled=True)  20 us
    all_to_all x2, waiting for transfers between devices, exchange_up(): return lax.all_to_all(pieces, 'up', 0, 0, tiled=True)  19.7 us
    pallas_call x2, Pallas kernels, up_hop(): pl.pallas_call(up_kernel, out_shape=jax.ShapeDtypeStruct((pairs, n, LANES...  17.9 us
    all_to_all x2, starting transfers between devices, exchange_up(): return lax.all_to_all(pieces, 'up', 0, 0, tiled=True)  16.2 us
    pallas_call x2, Pallas kernels, down_hop(): pl.pallas_call(down_kernel, out_shape=jax.ShapeDtypeStruct(a.shape, jnp.f...  12.2 us
    all_to_all x2, starting transfers between devices, down_part(): gathered = lax.all_to_all(copies, 'down', 0, 0, tiled=True)  8 us
    unnamed x24, local copies, waits for them, and re-layouts  2.79 us
  transfers between devices with their start and end apart: 4, of which 4 were waited for; matrix products, arithmetic and copies ran while one was open for 3% of the time, Pallas kernels for 7%

profile of v12, /device:TPU:32, one launch (start us, length us, event | category | flops | bytes accessed | tf_op | source)
XLA Modules:
  0.0 129.5 jit_solution(14407778708189609242)
XLA Ops:
  0.0 0.0 copy-start.2
  0.0 1.8 %shard_map.83 = bf16[512,128]{1,0:T(8,128)(2,1)} custom-call(f32[128,512]{1,0:T(8,128)} %x_ref.1), custom_call_target="tpu_custom_call" | custom-call | tf_op jit(solution)/shard_map/pallas_call | solution.py:109
  1.8 11.4 %all-to-all-start.1 = ((bf16[32,16,128]{2,1,0:T(8,128)(2,1)}), bf16[32,16,128]{2,1,0:T(8,128)(2,1)S(1)}, u32[]{:S(2)}, u32[]{:S(2)}) async-start(bf16[32,16,128]{2,1,0:T(8,128)(2,1)} %bitcast.24), calls=%async_computation.1 | async-start | bytes 262144 | tf_op jit(solution)/shard_map/all_to_all | solution.py:180
  13.1 0.0 copy-done.2
  13.2 9.7 %all-to-all-done.1.x_ref = bf16[32,16,128]{2,1,0:T(8,128)(2,1)S(1)} async-done(((bf16[32,16,128]{2,1,0:T(8,128)(2,1)}), bf16[32,16,128]{2,1,0:T(8,128)(2,1)S(1)}, u32[]{:S(2)}, u32[]{:S(2)}) %all-to-all-start.1) | async-done | bytes 131104 | tf_op jit(solution)/shard_map/all_to_all | solution.py:180
  22.9 1.1 broadcast_in_dim.39
  24.0 0.0 copy-done.6
  24.0 0.0 copy-start.11
  24.0 4.4 %all-to-all-start = ((bf16[8,128,512]{2,1,0:T(8,128)(2,1)}), bf16[8,128,512]{2,1,0:T(8,128)(2,1)S(1)}, u32[]{:S(2)}, u32[]{:S(2)}) async-start(bf16[8,128,512]{2,1,0:T(8,128)(2,1)} %broadcast_in_dim.39), calls=%async_computation | async-start | bytes 2097152 | tf_op jit(solution)/shard_map/all_to_all | solution.py:184
  28.5 0.0 copy-done.8
  28.5 0.0 copy-done.9
  28.5 0.0 copy-start.7
  28.5 0.1 select_reduce_fusion.1
  28.6 0.1 constant_dynamic-slice_fusion
  28.7 0.1 copy.27
  28.7 0.7 reshape.47.idx_ref
  29.4 0.0 copy-done.10
  29.4 0.0 copy-done.11
  29.4 0.1 select_reduce_fusion
  29.5 0.1 shift-right-arithmetic_add_fusion
  29.6 0.1 copy.29
  29.7 0.7 add.33.idx_ref
  30.4 0.0 copy-done.7
  30.4 0.7 multiply_add_fusion.a_ref
  31.1 9.0 %shard_map.84 = f32[32,16,128]{2,1,0:T(8,128)} custom-call(s32[2048]{0:T(1024)} %add.33.idx_ref, bf16[32,16,128]{2,1,0:T(8,128)(2,1)} %copy-done.6, bf16[2048,64]{1,0:T(8,128)(2,1)} %bitcast.17), custom_call_target="tpu_custom_call" | custom-call | tf_op jit(solution)/shard_map/pallas_call | solution.py:120
  40.1 4.3 %all-to-all-done.g_ref = bf16[8,128,512]{2,1,0:T(8,128)(2,1)S(1)} async-done(((bf16[8,128,512]{2,1,0:T(8,128)(2,1)}), bf16[8,128,512]{2,1,0:T(8,128)(2,1)S(1)}, u32[]{:S(2)}, u32[]{:S(2)}) %all-to-all-start) | async-done | bytes 1048608 | tf_op jit(solution)/shard_map/all_to_all | solution.py:184
  44.4 1.0 copy-done
  45.4 6.1 %shard_map.82 = f32[128,512]{1,0:T(8,128)} custom-call(s32[256]{0:T(256)} %reshape.47.idx_ref, bf16[8,128,512]{2,1,0:T(8,128)(2,1)} %copy-done, bf16[2048,64]{1,0:T(8,128)(2,1)} %bitcast.19, f32[128,512]{1,0:T(8,128)} %multiply_add_fusion.a_ref, f32[128,512]{1,0:T(8,128)} %x_ref.1), custom_call_target="tpu_custom_call" | custom-call | tf_op jit(solution)/shard_map/pallas_call | solution.py:138
  51.5 1.1 copy.28
  52.6 0.0 copy-done.5
  52.6 0.1 pad_maximum_fusion
  52.7 21.4 %all_to_all.25 = f32[32,32,128]{2,1,0:T(8,128)S(1)} all-to-all(f32[32,32,128]{2,1,0:T(8,128)S(1)} %pad_maximum_fusion), channel_id=1, replica_groups=mesh['up'=32,'down'=8] {'up'}, dimensions={0} | all-to-all | bytes 1048576 | tf_op jit(solution)/shard_map/all_to_all | solution.py:180
  74.1 0.7 fusion.1
  74.8 9.0 %shard_map.86 = f32[32,16,128]{2,1,0:T(8,128)} custom-call(s32[2048]{0:T(1024)} %add.33.idx_ref, bf16[32,16,128]{2,1,0:T(8,128)(2,1)} %get-tuple-element.7.x_ref, bf16[2048,64]{1,0:T(8,128)(2,1)} %bitcast.18), custom_call_target="tpu_custom_call" | custom-call | tf_op jit(solution)/shard_map/pallas_call | solution.py:120
  83.7 4.8 %all-to-all-start.4 = ((f32[32,16,128]{2,1,0:T(8,128)}), f32[32,16,128]{2,1,0:T(8,128)S(1)}, u32[]{:S(2)}, u32[]{:S(2)}) async-start(f32[32,16,128]{2,1,0:T(8,128)} %shard_map.86), calls=%async_computation.4 | async-start | bytes 524288 | tf_op jit(solution)/shard_map/all_to_all | solution.py:180
  88.6 0.0 copy-start.4
  88.6 0.1 copy.30
  88.7 0.8 copy-done.4
  89.5 0.8 fusion.4
  90.3 9.9 %all-to-all-done.4 = f32[32,16,128]{2,1,0:T(8,128)S(1)} async-done(((f32[32,16,128]{2,1,0:T(8,128)}), f32[32,16,128]{2,1,0:T(8,128)S(1)}, u32[]{:S(2)}, u32[]{:S(2)}) %all-to-all-start.4) | async-done | bytes 262176 | tf_op jit(solution)/shard_map/all_to_all | solution.py:180
  100.3 1.1 broadcast_in_dim.41
  101.3 3.6 %all-to-all-start.3 = ((bf16[8,128,512]{2,1,0:T(8,128)(2,1)}), bf16[8,128,512]{2,1,0:T(8,128)(2,1)S(1)}, u32[]{:S(2)}, u32[]{:S(2)}) async-start(bf16[8,128,512]{2,1,0:T(8,128)(2,1)} %broadcast_in_dim.41), calls=%async_computation.3 | async-start | bytes 2097152 | tf_op jit(solution)/shard_map/all_to_all | solution.py:184
  104.9 0.1 copy.31
  105.0 15.7 %all-to-all-done.3.g_ref = bf16[8,128,512]{2,1,0:T(8,128)(2,1)S(1)} async-done(((bf16[8,128,512]{2,1,0:T(8,128)(2,1)}), bf16[8,128,512]{2,1,0:T(8,128)(2,1)S(1)}, u32[]{:S(2)}, u32[]{:S(2)}) %all-to-all-start.3) | async-done | bytes 1048608 | tf_op jit(solution)/shard_map/all_to_all | solution.py:184
  120.7 1.0 copy-done.1
  121.7 6.1 %shard_map.85 = f32[128,512]{1,0:T(8,128)} custom-call(s32[256]{0:T(256)} %reshape.47.idx_ref, bf16[8,128,512]{2,1,0:T(8,128)(2,1)} %copy-done.1, bf16[2048,64]{1,0:T(8,128)(2,1)} %bitcast.20, f32[128,512]{1,0:T(8,128)} %multiply_add_fusion.a_ref, f32[128,512]{1,0:T(8,128)} %get-tuple-element.6.b_ref), custom_call_target="tpu_custom_call" | custom-call | tf_op jit(solution)/shard_map/pallas_call | solution.py:138
  127.8 0.0 copy-done.3
  127.8 1.7 %fusion.2 = f32[128,512]{1,0:T(8,128)} fusion(f32[128,512]{1,0:T(8,128)S(1)} %copy-done.3, f32[128,512]{1,0:T(8,128)} %shard_map.85, f32[512,128]{0,1:T(8,128)S(1)} %copy.31), kind=kLoop, calls=%fused_computation.9 | loop fusion | flops 131072 | bytes 1048576 | tf_op jit(solution)/shard_map/sub | solution.py:202
  (10 shorter events, 0.0 us)
Async XLA Ops:
  0.0 13.2 %copy-start.2 = (f32[128,512]{1,0:T(8,128)S(1)}, f32[128,512]{1,0:T(8,128)}, u32[]{:S(2)}) copy-start(f32[128,512]{1,0:T(8,128)} %x_ref.1) | copy-start | bytes 786436
  1.8 21.2 %all-to-all-start.1 = ((bf16[32,16,128]{2,1,0:T(8,128)(2,1)}), bf16[32,16,128]{2,1,0:T(8,128)(2,1)S(1)}, u32[]{:S(2)}, u32[]{:S(2)}) async-start(bf16[32,16,128]{2,1,0:T(8,128)(2,1)} %bitcast.24), calls=%async_computation.1 | async-start | bytes 262144 | tf_op jit(solution)/shard_map/all_to_all | solution.py:180
  22.9 1.1 copy-start.6
  24.0 4.5 %copy-start.8 = (s32[64,32]{0,1:T(8,128)S(1)}, s32[64,32]{0,1:T(8,128)}, u32[]{:S(2)}) copy-start(s32[64,32]{0,1:T(8,128)} %param.13) | copy-start | bytes 24580
  24.0 4.5 %copy-start.9 = (s32[64,32]{0,1:T(8,128)S(1)}, s32[64,32]{0,1:T(8,128)}, u32[]{:S(2)}) copy-start(s32[64,32]{0,1:T(8,128)} %param.14) | copy-start | bytes 24580
  24.0 5.4 %copy-start.10 = (s32[64,32]{0,1:T(8,128)S(1)}, s32[64,32]{0,1:T(8,128)}, u32[]{:S(2)}) copy-start(s32[64,32]{0,1:T(8,128)} %param.10) | copy-start | bytes 24580
  24.0 5.4 %copy-start.11 = (s32[64,32]{0,1:T(8,128)S(1)}, s32[64,32]{0,1:T(8,128)}, u32[]{:S(2)}) copy-start(s32[64,32]{0,1:T(8,128)} %param.11) | copy-start | bytes 24580
  24.0 20.4 %all-to-all-start = ((bf16[8,128,512]{2,1,0:T(8,128)(2,1)}), bf16[8,128,512]{2,1,0:T(8,128)(2,1)S(1)}, u32[]{:S(2)}, u32[]{:S(2)}) async-start(bf16[8,128,512]{2,1,0:T(8,128)(2,1)} %broadcast_in_dim.39), calls=%async_computation | async-start | bytes 2097152 | tf_op jit(solution)/shard_map/all_to_all | solution.py:184
  28.5 1.9 %copy-start.7 = (s32[128,512]{1,0:T(8,128)S(1)}, s32[128,512]{1,0:T(8,128)}, u32[]{:S(2)}) copy-start(s32[128,512]{1,0:T(8,128)} %param.9) | copy-start | bytes 786436
  44.4 1.0 copy-start
  51.5 1.1 copy-start.5
  83.7 16.5 %all-to-all-start.4 = ((f32[32,16,128]{2,1,0:T(8,128)}), f32[32,16,128]{2,1,0:T(8,128)S(1)}, u32[]{:S(2)}, u32[]{:S(2)}) async-start(f32[32,16,128]{2,1,0:T(8,128)} %shard_map.86), calls=%async_computation.4 | async-start | bytes 524288 | tf_op jit(solution)/shard_map/all_to_all | solution.py:180
  88.6 1.0 copy-start.4
  101.3 19.4 %all-to-all-start.3 = ((bf16[8,128,512]{2,1,0:T(8,128)(2,1)}), bf16[8,128,512]{2,1,0:T(8,128)(2,1)S(1)}, u32[]{:S(2)}, u32[]{:S(2)}) async-start(bf16[8,128,512]{2,1,0:T(8,128)(2,1)} %broadcast_in_dim.41), calls=%async_computation.3 | async-start | bytes 2097152 | tf_op jit(solution)/shard_map/all_to_all | solution.py:184
  120.7 1.0 copy-start.1
  121.7 6.1 %copy-start.3 = (f32[128,512]{1,0:T(8,128)S(1)}, f32[128,512]{1,0:T(8,128)}, u32[]{:S(2)}) copy-start(f32[128,512]{1,0:T(8,128)} %x_ref.1) | copy-start | bytes 786436

commit v13 on v9

--- a/solution.py
+++ b/solution.py
@@ -18,12 +18,11 @@
     return jnp.sum(jnp.where(matched, block_cols[:, :, None], 0), axis=1)
 
 
-def _fill_rolled(src_ref, src2_ref):
-    pairs = src_ref.shape[0]
-    half = src_ref.shape[-1] // 2
+def _fill_rolled(load, pairs, src2_ref):
+    half = src2_ref.shape[-1] // 2
 
     def one(i, carry):
-        piece = src_ref[i]
+        piece = load(i)
         src2_ref[i] = piece
         src2_ref[pairs + i] = pltpu.roll(piece, half, 1)
         return carry
@@ -45,11 +44,23 @@
 
 
 def up_kernel(idx_ref, x_ref, w_ref, o_ref, src2_ref, stage_ref):
-    pairs, n, _ = x_ref.shape
+    _fill_rolled(lambda i: x_ref[i], x_ref.shape[0], src2_ref)
+    _up_body(idx_ref, w_ref, o_ref, src2_ref, stage_ref)
+
+
+def up_kernel_halved(idx_ref, p_ref, u_ref, w_ref, o_ref, src2_ref, stage_ref):
+    _fill_rolled(
+        lambda i: ((p_ref[i] + u_ref[i]) / half_span).astype(jnp.bfloat16),
+        p_ref.shape[0], src2_ref,
+    )
+    _up_body(idx_ref, w_ref, o_ref, src2_ref, stage_ref)
+
+
+def _up_body(idx_ref, w_ref, o_ref, src2_ref, stage_ref):
+    pairs, n, _ = o_ref.shape
     block_width = w_ref.shape[1]
     shared_count = w_ref.shape[0] // block_width
     rows_per_chunk = stage_ref.shape[0] // n
-    _fill_rolled(x_ref, src2_ref)
 
     def chunk(g, carry):
         for rr in range(rows_per_chunk):
@@ -113,23 +124,20 @@
     )(x)
 
 
-def up_hop(idx, x, w):
-    pairs, n, _ = x.shape
+def up_hop(idx, w, *parts):
+    pairs, n, _ = parts[0].shape
     rows_per_chunk = 8
     return pl.pallas_call(
-        up_kernel,
+        up_kernel if len(parts) == 1 else up_kernel_halved,
         out_shape=jax.ShapeDtypeStruct((pairs, n, LANES), jnp.float32),
-        in_specs=[
-            pl.BlockSpec(memory_space=pltpu.SMEM),
-            pl.BlockSpec(memory_space=pltpu.VMEM),
-            pl.BlockSpec(memory_space=pltpu.VMEM),
-        ],
+        in_specs=[pl.BlockSpec(memory_space=pltpu.SMEM)]
+        + [pl.BlockSpec(memory_space=pltpu.VMEM)] * (len(parts) + 1),
         out_specs=pl.BlockSpec(memory_space=pltpu.VMEM),
         scratch_shapes=[
             pltpu.VMEM((2 * pairs, n, LANES), jnp.bfloat16),
             pltpu.VMEM((rows_per_chunk * n, w.shape[0]), jnp.bfloat16),
         ],
-    )(idx, x, w)
+    )(idx, *parts, w)
 
 
 def down_hop(idx, g, w, own_cols):
@@ -185,15 +193,14 @@
     sent0 = exchange_up(
         transpose_round(amplitudes).reshape(up_count, col_chunk, local_rows)
     )
-    up0_cols = up_hop(up_idx, sent0, up_table)
+    up0_cols = up_hop(up_idx, up_table, sent0)
     partial_rows = onsite * amplitudes + down_part(rounded0)
     both = exchange_up(jnp.concatenate([to_columns(partial_rows), up0_cols], axis=1))
     partial_cols = both[:, :col_chunk]
     up0_rows = to_rows(both[:, col_chunk:])
-    first_cols = (partial_cols + up0_cols) / half_span
     first_rows = (partial_rows + up0_rows) / half_span
 
-    up1_cols = up_hop(up_idx, first_cols.astype(jnp.bfloat16), up_table)
+    up1_cols = up_hop(up_idx, up_table, partial_cols, up0_cols)
     down1_rows = down_part(first_rows.astype(jnp.bfloat16))
     up1_rows = to_rows(exchange_up(up1_cols))
     return 2.0 * ((onsite * first_rows + up1_rows + down1_rows) / half_span) - amplitudes

time: 132 us -> 132 us (level)
  no operation moved by 1% of the time
where the time goes in v13:
time: 132 us; the launch traced here: 130 us
  waiting for transfers between devices  41.1 us (31%)
  Pallas kernels  31.8 us (24%)
  starting transfers between devices  24.2 us (18%)
  blocking collectives  21.4 us (16%)
  local copies, waits for them, and re-layouts  8.48 us (6%)
  other arithmetic  3.28 us (2%)
    all_to_all x1, blocking collectives, exchange_up(): return lax.all_to_all(pieces, 'up', 0, 0, tiled=True)  21.4 us
    all_to_all x2, waiting for transfers between devices, down_part(): gathered = lax.all_to_all(copies, 'down', 0, 0, tiled=True)  20.8 us
    all_to_all x2, waiting for transfers between devices, exchange_up(): return lax.all_to_all(pieces, 'up', 0, 0, tiled=True)  20.3 us
    pallas_call x2, Pallas kernels, up_hop(): pl.pallas_call(up_kernel if len(parts) == 1 else up_kernel_halved, out_sh...  18.1 us
    all_to_all x2, starting transfers between devices, exchange_up(): return lax.all_to_all(pieces, 'up', 0, 0, tiled=True)  16.2 us
    pallas_call x2, Pallas kernels, down_hop(): pl.pallas_call(down_kernel, out_shape=jax.ShapeDtypeStruct((rows, own_col...  11.9 us
    all_to_all x2, starting transfers between devices, down_part(): gathered = lax.all_to_all(copies, 'down', 0, 0, tiled=True)  7.99 us
    unnamed x22, local copies, waits for them, and re-layouts  3.67 us
  transfers between devices with their start and end apart: 4, of which 4 were waited for; matrix products, arithmetic and copies ran while one was open for 2% of the time, Pallas kernels for 7%

profile of v13, /device:TPU:32, one launch (start us, length us, event | category | flops | bytes accessed | tf_op | source)
XLA Modules:
  0.0 130.4 jit_solution(1854357108784278774)
XLA Ops:
  0.0 0.0 copy-start
  0.0 1.8 %shard_map.83 = bf16[512,128]{1,0:T(8,128)(2,1)} custom-call(f32[128,512]{1,0:T(8,128)} %x_ref.1), custom_call_target="tpu_custom_call" | custom-call | tf_op jit(solution)/shard_map/pallas_call | solution.py:119
  1.8 11.4 %all-to-all-start.1 = ((bf16[32,16,128]{2,1,0:T(8,128)(2,1)}), bf16[32,16,128]{2,1,0:T(8,128)(2,1)S(1)}, u32[]{:S(2)}, u32[]{:S(2)}) async-start(bf16[32,16,128]{2,1,0:T(8,128)(2,1)} %bitcast.29), calls=%async_computation.1 | async-start | bytes 262144 | tf_op jit(solution)/shard_map/all_to_all | solution.py:185
  13.1 0.0 copy-done
  13.2 9.8 %all-to-all-done.1.x_ref = bf16[32,16,128]{2,1,0:T(8,128)(2,1)S(1)} async-done(((bf16[32,16,128]{2,1,0:T(8,128)(2,1)}), bf16[32,16,128]{2,1,0:T(8,128)(2,1)S(1)}, u32[]{:S(2)}, u32[]{:S(2)}) %all-to-all-start.1) | async-done | bytes 131104 | tf_op jit(solution)/shard_map/all_to_all | solution.py:185
  22.9 0.0 copy-start.6
  22.9 1.1 broadcast_in_dim.39
  24.0 0.0 copy-done.6
  24.0 0.0 copy-start.7
  24.0 4.4 %all-to-all-start = ((bf16[8,128,512]{2,1,0:T(8,128)(2,1)}), bf16[8,128,512]{2,1,0:T(8,128)(2,1)S(1)}, u32[]{:S(2)}, u32[]{:S(2)}) async-start(bf16[8,128,512]{2,1,0:T(8,128)(2,1)} %broadcast_in_dim.39), calls=%async_computation | async-start | bytes 2097152 | tf_op jit(solution)/shard_map/all_to_all | solution.py:189
  28.5 0.0 copy-done.7
  28.5 0.0 copy-done.8
  28.5 0.1 select_reduce_fusion
  28.6 0.1 shift-right-arithmetic_add_fusion
  28.7 0.1 copy.29
  28.7 0.0 copy-start.10
  28.7 0.7 add.37.idx_ref
  29.4 0.0 copy-done.9
  29.5 0.0 copy-done.10
  29.5 0.1 select_reduce_fusion.1
  29.6 0.1 constant_dynamic-slice_fusion
  29.6 0.1 copy.27
  29.7 0.7 reshape.47.idx_ref
  30.4 9.0 %shard_map.84.u_ref = f32[32,16,128]{2,1,0:T(8,128)} custom-call(s32[2048]{0:T(1024)} %add.37.idx_ref, bf16[32,16,128]{2,1,0:T(8,128)(2,1)} %copy-done.6, bf16[2048,64]{1,0:T(8,128)(2,1)} %bitcast.24), custom_call_target="tpu_custom_call" | custom-call | tf_op jit(solution)/shard_map/pallas_call | solution.py:130
  39.4 5.0 %all-to-all-done.g_ref = bf16[8,128,512]{2,1,0:T(8,128)(2,1)S(1)} async-done(((bf16[8,128,512]{2,1,0:T(8,128)(2,1)}), bf16[8,128,512]{2,1,0:T(8,128)(2,1)S(1)}, u32[]{:S(2)}, u32[]{:S(2)}) %all-to-all-start) | async-done | bytes 1048608 | tf_op jit(solution)/shard_map/all_to_all | solution.py:189
  44.4 1.0 copy-done.1
  45.4 6.0 %shard_map.82 = f32[128,512]{1,0:T(8,128)} custom-call(s32[256]{0:T(256)} %reshape.47.idx_ref, bf16[8,128,512]{2,1,0:T(8,128)(2,1)} %copy-done.1, bf16[2048,64]{1,0:T(8,128)(2,1)} %bitcast.22), custom_call_target="tpu_custom_call" | custom-call | tf_op jit(solution)/shard_map/pallas_call | solution.py:145
  51.3 0.0 copy-done.5
  51.3 1.0 fusion.4
  52.3 0.0 copy-start.4
  52.4 0.1 copy.28
  52.5 0.8 copy-done.4
  53.4 21.4 %all_to_all.25 = f32[32,32,128]{2,1,0:T(8,128)S(1)} all-to-all(f32[32,32,128]{2,1,0:T(8,128)S(1)} %pad_maximum_fusion), channel_id=1, replica_groups=mesh['up'=32,'down'=8] {'up'}, dimensions={0} | all-to-all | bytes 1048576 | tf_op jit(solution)/shard_map/all_to_all | solution.py:185
  74.8 0.7 fusion.5
  75.5 9.1 %shard_map.85 = f32[32,16,128]{2,1,0:T(8,128)} custom-call(s32[2048]{0:T(1024)} %add.37.idx_ref, f32[32,16,128]{2,1,0:T(8,128)} %get-tuple-element.5.p_ref, f32[32,16,128]{2,1,0:T(8,128)} %shard_map.84.u_ref, bf16[2048,64]{1,0:T(8,128)(2,1)} %bitcast.25), custom_call_target="tpu_custom_call" | custom-call | tf_op jit(solution)/shard_map/pallas_call | solution.py:130
  84.7 4.8 %all-to-all-start.3 = ((f32[32,16,128]{2,1,0:T(8,128)}), f32[32,16,128]{2,1,0:T(8,128)S(1)}, u32[]{:S(2)}, u32[]{:S(2)}) async-start(f32[32,16,128]{2,1,0:T(8,128)} %shard_map.85), calls=%async_computation.3 | async-start | bytes 524288 | tf_op jit(solution)/shard_map/all_to_all | solution.py:185
  89.5 0.0 copy-start.3
  89.5 0.1 copy.30
  89.7 0.8 copy-done.3
  90.5 0.1 fusion.3
  90.6 10.6 %all-to-all-done.3 = f32[32,16,128]{2,1,0:T(8,128)S(1)} async-done(((f32[32,16,128]{2,1,0:T(8,128)}), f32[32,16,128]{2,1,0:T(8,128)S(1)}, u32[]{:S(2)}, u32[]{:S(2)}) %all-to-all-start.3) | async-done | bytes 262176 | tf_op jit(solution)/shard_map/all_to_all | solution.py:185
  101.2 1.1 broadcast_in_dim.41
  102.2 3.6 %all-to-all-start.4 = ((bf16[8,128,512]{2,1,0:T(8,128)(2,1)}), bf16[8,128,512]{2,1,0:T(8,128)(2,1)S(1)}, u32[]{:S(2)}, u32[]{:S(2)}) async-start(bf16[8,128,512]{2,1,0:T(8,128)(2,1)} %broadcast_in_dim.41), calls=%async_computation.4 | async-start | bytes 2097152 | tf_op jit(solution)/shard_map/all_to_all | solution.py:189
  105.8 0.1 copy.31
  105.9 15.7 %all-to-all-done.4.g_ref = bf16[8,128,512]{2,1,0:T(8,128)(2,1)S(1)} async-done(((bf16[8,128,512]{2,1,0:T(8,128)(2,1)}), bf16[8,128,512]{2,1,0:T(8,128)(2,1)S(1)}, u32[]{:S(2)}, u32[]{:S(2)}) %all-to-all-start.4) | async-done | bytes 1048608 | tf_op jit(solution)/shard_map/all_to_all | solution.py:189
  121.7 1.0 copy-done.2
  122.6 5.9 %shard_map.86 = f32[128,512]{1,0:T(8,128)} custom-call(s32[256]{0:T(256)} %reshape.47.idx_ref, bf16[8,128,512]{2,1,0:T(8,128)(2,1)} %copy-done.2, bf16[2048,64]{1,0:T(8,128)(2,1)} %bitcast.23), custom_call_target="tpu_custom_call" | custom-call | tf_op jit(solution)/shard_map/pallas_call | solution.py:145
  128.5 1.8 %fusion.1 = f32[128,512]{1,0:T(8,128)} fusion(f32[128,512]{1,0:T(8,128)S(1)} %copy-done, f32[128,512]{1,0:T(8,128)} %shard_map.86, f32[512,128]{0,1:T(8,128)S(1)} %copy.31, s32[128,512]{1,0:T(8,128)S(1)} %copy-done.5, f32[512,128]{0,1:T(8,128)S(1)} %copy.30, f32[128,512]{1,0:T(8,128)S(1)} %copy-done.3), kind=kLoop, calls=%fused_computation.7 | loop fusion | flops 720896 | bytes 1835008 | tf_op jit(solution)/shard_map/sub | solution.py:206
  (8 shorter events, 0.1 us)
Async XLA Ops:
  0.0 13.1 %copy-start = (f32[128,512]{1,0:T(8,128)S(1)}, f32[128,512]{1,0:T(8,128)}, u32[]{:S(2)}) copy-start(f32[128,512]{1,0:T(8,128)} %x_ref.1) | copy-start | bytes 786436
  1.8 21.2 %all-to-all-start.1 = ((bf16[32,16,128]{2,1,0:T(8,128)(2,1)}), bf16[32,16,128]{2,1,0:T(8,128)(2,1)S(1)}, u32[]{:S(2)}, u32[]{:S(2)}) async-start(bf16[32,16,128]{2,1,0:T(8,128)(2,1)} %bitcast.29), calls=%async_computation.1 | async-start | bytes 262144 | tf_op jit(solution)/shard_map/all_to_all | solution.py:185
  22.9 1.1 copy-start.6
  24.0 4.4 %copy-start.7 = (s32[64,32]{0,1:T(8,128)S(1)}, s32[64,32]{0,1:T(8,128)}, u32[]{:S(2)}) copy-start(s32[64,32]{0,1:T(8,128)} %param.10) | copy-start | bytes 24580
  24.0 4.5 %copy-start.8 = (s32[64,32]{0,1:T(8,128)S(1)}, s32[64,32]{0,1:T(8,128)}, u32[]{:S(2)}) copy-start(s32[64,32]{0,1:T(8,128)} %param.11) | copy-start | bytes 24580
  24.0 20.4 %all-to-all-start = ((bf16[8,128,512]{2,1,0:T(8,128)(2,1)}), bf16[8,128,512]{2,1,0:T(8,128)(2,1)S(1)}, u32[]{:S(2)}, u32[]{:S(2)}) async-start(bf16[8,128,512]{2,1,0:T(8,128)(2,1)} %broadcast_in_dim.39), calls=%async_computation | async-start | bytes 2097152 | tf_op jit(solution)/shard_map/all_to_all | solution.py:189
  28.7 0.7 copy-start.9
  28.7 0.7 copy-start.10
  44.4 1.0 copy-start.1
  45.4 6.0 %copy-start.5 = (s32[128,512]{1,0:T(8,128)S(1)}, s32[128,512]{1,0:T(8,128)}, u32[]{:S(2)}) copy-start(s32[128,512]{1,0:T(8,128)} %param.9) | copy-start | bytes 786436
  52.3 1.0 copy-start.4
  84.7 16.5 %all-to-all-start.3 = ((f32[32,16,128]{2,1,0:T(8,128)}), f32[32,16,128]{2,1,0:T(8,128)S(1)}, u32[]{:S(2)}, u32[]{:S(2)}) async-start(f32[32,16,128]{2,1,0:T(8,128)} %shard_map.85), calls=%async_computation.3 | async-start | bytes 524288 | tf_op jit(solution)/shard_map/all_to_all | solution.py:185
  89.5 1.0 copy-start.3
  102.2 19.4 %all-to-all-start.4 = ((bf16[8,128,512]{2,1,0:T(8,128)(2,1)}), bf16[8,128,512]{2,1,0:T(8,128)(2,1)S(1)}, u32[]{:S(2)}, u32[]{:S(2)}) async-start(bf16[8,128,512]{2,1,0:T(8,128)(2,1)} %broadcast_in_dim.41), calls=%async_computation.4 | async-start | bytes 2097152 | tf_op jit(solution)/shard_map/all_to_all | solution.py:189
  121.7 1.0 copy-start.2

commit v14 on v9

--- a/solution.py
+++ b/solution.py
@@ -66,7 +66,7 @@
     lax.fori_loop(0, 2 * pairs // rows_per_chunk, chunk, 0)
 
 
-def down_kernel(idx_ref, g_ref, w_ref, o_ref, src_ref, w2_ref, stage_ref):
+def down_kernel(idx_ref, g_ref, w_ref, o_ref, src_ref, w2_ref, stage_ref, mask_ref):
     sources, rows, cols = g_ref.shape
     block_width = w_ref.shape[1]
     shared_count = w_ref.shape[0] // block_width
@@ -83,15 +83,16 @@
         block = w_ref[s * block_width:(s + 1) * block_width, :]
         w2_ref[s * LANES:s * LANES + block_width, :] = block
         w2_ref[s * LANES + block_width:(s + 1) * LANES, :] = block
-    half_of_lane = jnp.where(
-        lax.broadcasted_iota(jnp.int32, (rows, LANES), 1) >= block_width, 1, 0
-    )
+    upper = lax.broadcasted_iota(jnp.int32, (rows, LANES), 1) >= block_width
+    ones = jnp.ones((rows, LANES), mask_ref.dtype)
+    zeros = jnp.zeros((rows, LANES), mask_ref.dtype)
+    mask_ref[0] = jnp.where(upper, zeros, ones)
+    mask_ref[1] = jnp.where(upper, ones, zeros)
     for r in range(own_blocks):
         for s in range(shared_count):
             c = idx_ref[r * shared_count + s]
             piece = src_ref[lax.shift_right_logical(c, 1)]
-            keep = half_of_lane == (c & 1)
-            stage_ref[:, s * LANES:(s + 1) * LANES] = jnp.where(keep, piece, jnp.zeros_like(piece))
+            stage_ref[:, s * LANES:(s + 1) * LANES] = piece * mask_ref[c & 1]
         o_ref[:, r * block_width:(r + 1) * block_width] = jnp.dot(
             stage_ref[...], w2_ref[...], preferred_element_type=jnp.float32
         )
@@ -147,6 +148,7 @@
             pltpu.VMEM((g.shape[0] * g.shape[2] // LANES, rows, LANES), jnp.bfloat16),
             pltpu.VMEM((2 * w.shape[0], w.shape[1]), jnp.bfloat16),
             pltpu.VMEM((rows, 2 * w.shape[0]), jnp.bfloat16),
+            pltpu.VMEM((2, rows, LANES), jnp.bfloat16),
         ],
     )(idx, g, w)
 

time: 132 us -> 133 us (level)
  no operation moved by 1% of the time
where the time goes in v14:
time: 133 us; the launch traced here: 131 us
  waiting for transfers between devices  41.2 us (31%)
  Pallas kernels  32.6 us (25%)
  starting transfers between devices  24.2 us (18%)
  blocking collectives  21.4 us (16%)
  local copies, waits for them, and re-layouts  7.7 us (6%)
  other arithmetic  3.98 us (3%)
    all_to_all x1, blocking collectives, exchange_up(): return lax.all_to_all(pieces, 'up', 0, 0, tiled=True)  21.4 us
    all_to_all x2, waiting for transfers between devices, down_part(): gathered = lax.all_to_all(copies, 'down', 0, 0, tiled=True)  20.8 us
    all_to_all x2, waiting for transfers between devices, exchange_up(): return lax.all_to_all(pieces, 'up', 0, 0, tiled=True)  20.4 us
    pallas_call x2, Pallas kernels, up_hop(): pl.pallas_call(up_kernel, out_shape=jax.ShapeDtypeStruct((pairs, n, LANES...  17.9 us
    all_to_all x2, starting transfers between devices, exchange_up(): return lax.all_to_all(pieces, 'up', 0, 0, tiled=True)  16.2 us
    pallas_call x2, Pallas kernels, down_hop(): pl.pallas_call(down_kernel, out_shape=jax.ShapeDtypeStruct((rows, own_col...  12.9 us
    all_to_all x2, starting transfers between devices, down_part(): gathered = lax.all_to_all(copies, 'down', 0, 0, tiled=True)  7.99 us
    unnamed x22, local copies, waits for them, and re-layouts  3.61 us
  transfers between devices with their start and end apart: 4, of which 4 were waited for; matrix products, arithmetic and copies ran while one was open for 2% of the time, Pallas kernels for 7%

profile of v14, /device:TPU:32, one launch (start us, length us, event | category | flops | bytes accessed | tf_op | source)
XLA Modules:
  0.0 131.1 jit_solution(8426386799411668846)
XLA Ops:
  0.0 0.0 copy-start
  0.0 1.8 %shard_map.83 = bf16[512,128]{1,0:T(8,128)(2,1)} custom-call(f32[128,512]{1,0:T(8,128)} %x_ref.1), custom_call_target="tpu_custom_call" | custom-call | tf_op jit(solution)/shard_map/pallas_call | solution.py:109
  1.8 11.4 %all-to-all-start.1 = ((bf16[32,16,128]{2,1,0:T(8,128)(2,1)}), bf16[32,16,128]{2,1,0:T(8,128)(2,1)S(1)}, u32[]{:S(2)}, u32[]{:S(2)}) async-start(bf16[32,16,128]{2,1,0:T(8,128)(2,1)} %bitcast.29), calls=%async_computation.1 | async-start | bytes 262144 | tf_op jit(solution)/shard_map/all_to_all | solution.py:179
  13.1 0.0 copy-done
  13.2 9.8 %all-to-all-done.1.x_ref = bf16[32,16,128]{2,1,0:T(8,128)(2,1)S(1)} async-done(((bf16[32,16,128]{2,1,0:T(8,128)(2,1)}), bf16[32,16,128]{2,1,0:T(8,128)(2,1)S(1)}, u32[]{:S(2)}, u32[]{:S(2)}) %all-to-all-start.1) | async-done | bytes 131104 | tf_op jit(solution)/shard_map/all_to_all | solution.py:179
  22.9 0.0 copy-start.6
  22.9 1.1 broadcast_in_dim.39
  24.0 0.0 copy-done.6
  24.0 0.0 copy-start.7
  24.0 4.4 %all-to-all-start = ((bf16[8,128,512]{2,1,0:T(8,128)(2,1)}), bf16[8,128,512]{2,1,0:T(8,128)(2,1)S(1)}, u32[]{:S(2)}, u32[]{:S(2)}) async-start(bf16[8,128,512]{2,1,0:T(8,128)(2,1)} %broadcast_in_dim.39), calls=%async_computation | async-start | bytes 2097152 | tf_op jit(solution)/shard_map/all_to_all | solution.py:183
  28.4 0.0 copy-done.7
  28.5 0.0 copy-done.8
  28.5 0.1 select_reduce_fusion.1
  28.6 0.0 copy-start.10
  28.6 0.1 constant_dynamic-slice_fusion
  28.7 0.1 copy.27
  28.7 0.7 reshape.47.idx_ref
  29.4 0.0 copy-done.10
  29.4 0.0 copy-done.9
  29.4 0.1 select_reduce_fusion
  29.5 0.1 shift-right-arithmetic_add_fusion
  29.6 0.1 copy.29
  29.6 0.7 add.40.idx_ref
  30.3 9.0 %shard_map.84 = f32[32,16,128]{2,1,0:T(8,128)} custom-call(s32[2048]{0:T(1024)} %add.40.idx_ref, bf16[32,16,128]{2,1,0:T(8,128)(2,1)} %copy-done.6, bf16[2048,64]{1,0:T(8,128)(2,1)} %bitcast.24), custom_call_target="tpu_custom_call" | custom-call | tf_op jit(solution)/shard_map/pallas_call | solution.py:120
  39.3 5.1 %all-to-all-done.g_ref = bf16[8,128,512]{2,1,0:T(8,128)(2,1)S(1)} async-done(((bf16[8,128,512]{2,1,0:T(8,128)(2,1)}), bf16[8,128,512]{2,1,0:T(8,128)(2,1)S(1)}, u32[]{:S(2)}, u32[]{:S(2)}) %all-to-all-start) | async-done | bytes 1048608 | tf_op jit(solution)/shard_map/all_to_all | solution.py:183
  44.4 1.0 copy-done.1
  45.4 6.5 %shard_map.82 = f32[128,512]{1,0:T(8,128)} custom-call(s32[256]{0:T(256)} %reshape.47.idx_ref, bf16[8,128,512]{2,1,0:T(8,128)(2,1)} %copy-done.1, bf16[2048,64]{1,0:T(8,128)(2,1)} %bitcast.22), custom_call_target="tpu_custom_call" | custom-call | tf_op jit(solution)/shard_map/pallas_call | solution.py:138
  51.8 0.0 copy-done.4
  51.8 1.0 fusion.6
  52.8 0.0 copy-start.5
  52.9 0.1 copy.28
  53.0 0.8 copy-done.5
  53.9 21.4 %all_to_all.25 = f32[32,32,128]{2,1,0:T(8,128)S(1)} all-to-all(f32[32,32,128]{2,1,0:T(8,128)S(1)} %pad_maximum_fusion), channel_id=1, replica_groups=mesh['up'=32,'down'=8] {'up'}, dimensions={0} | all-to-all | bytes 1048576 | tf_op jit(solution)/shard_map/all_to_all | solution.py:179
  75.3 0.7 fusion.1
  76.0 9.0 %shard_map.85 = f32[32,16,128]{2,1,0:T(8,128)} custom-call(s32[2048]{0:T(1024)} %add.40.idx_ref, bf16[32,16,128]{2,1,0:T(8,128)(2,1)} %get-tuple-element.5.x_ref, bf16[2048,64]{1,0:T(8,128)(2,1)} %bitcast.25), custom_call_target="tpu_custom_call" | custom-call | tf_op jit(solution)/shard_map/pallas_call | solution.py:120
  84.9 4.8 %all-to-all-start.3 = ((f32[32,16,128]{2,1,0:T(8,128)}), f32[32,16,128]{2,1,0:T(8,128)S(1)}, u32[]{:S(2)}, u32[]{:S(2)}) async-start(f32[32,16,128]{2,1,0:T(8,128)} %shard_map.85), calls=%async_computation.3 | async-start | bytes 524288 | tf_op jit(solution)/shard_map/all_to_all | solution.py:179
  89.8 0.0 copy-start.3
  89.8 0.1 copy.30
  89.9 0.8 copy-done.3
  90.7 0.1 fusion.5
  90.8 10.6 %all-to-all-done.3 = f32[32,16,128]{2,1,0:T(8,128)S(1)} async-done(((f32[32,16,128]{2,1,0:T(8,128)}), f32[32,16,128]{2,1,0:T(8,128)S(1)}, u32[]{:S(2)}, u32[]{:S(2)}) %all-to-all-start.3) | async-done | bytes 262176 | tf_op jit(solution)/shard_map/all_to_all | solution.py:179
  101.4 1.1 broadcast_in_dim.41
  102.5 3.6 %all-to-all-start.4 = ((bf16[8,128,512]{2,1,0:T(8,128)(2,1)}), bf16[8,128,512]{2,1,0:T(8,128)(2,1)S(1)}, u32[]{:S(2)}, u32[]{:S(2)}) async-start(bf16[8,128,512]{2,1,0:T(8,128)(2,1)} %broadcast_in_dim.41), calls=%async_computation.4 | async-start | bytes 2097152 | tf_op jit(solution)/shard_map/all_to_all | solution.py:183
  106.1 0.1 copy.31
  106.2 15.7 %all-to-all-done.4.g_ref = bf16[8,128,512]{2,1,0:T(8,128)(2,1)S(1)} async-done(((bf16[8,128,512]{2,1,0:T(8,128)(2,1)}), bf16[8,128,512]{2,1,0:T(8,128)(2,1)S(1)}, u32[]{:S(2)}, u32[]{:S(2)}) %all-to-all-start.4) | async-done | bytes 1048608 | tf_op jit(solution)/shard_map/all_to_all | solution.py:183
  121.9 1.0 copy-done.2
  122.9 6.4 %shard_map.86 = f32[128,512]{1,0:T(8,128)} custom-call(s32[256]{0:T(256)} %reshape.47.idx_ref, bf16[8,128,512]{2,1,0:T(8,128)(2,1)} %copy-done.2, bf16[2048,64]{1,0:T(8,128)(2,1)} %bitcast.23), custom_call_target="tpu_custom_call" | custom-call | tf_op jit(solution)/shard_map/pallas_call | solution.py:138
  129.3 1.8 %fusion.3 = f32[128,512]{1,0:T(8,128)} fusion(f32[128,512]{1,0:T(8,128)S(1)} %copy-done, f32[128,512]{1,0:T(8,128)} %shard_map.86, f32[512,128]{0,1:T(8,128)S(1)} %copy.31, s32[128,512]{1,0:T(8,128)S(1)} %copy-done.4, f32[512,128]{0,1:T(8,128)S(1)} %copy.30, f32[128,512]{1,0:T(8,128)S(1)} %copy-done.3), kind=kLoop, calls=%fused_computation.10 | loop fusion | flops 720896 | bytes 1835008 | tf_op jit(solution)/shard_map/sub | solution.py:201
  (8 shorter events, 0.1 us)
Async XLA Ops:
  0.0 13.1 %copy-start = (f32[128,512]{1,0:T(8,128)S(1)}, f32[128,512]{1,0:T(8,128)}, u32[]{:S(2)}) copy-start(f32[128,512]{1,0:T(8,128)} %x_ref.1) | copy-start | bytes 786436
  1.8 21.2 %all-to-all-start.1 = ((bf16[32,16,128]{2,1,0:T(8,128)(2,1)}), bf16[32,16,128]{2,1,0:T(8,128)(2,1)S(1)}, u32[]{:S(2)}, u32[]{:S(2)}) async-start(bf16[32,16,128]{2,1,0:T(8,128)(2,1)} %bitcast.29), calls=%async_computation.1 | async-start | bytes 262144 | tf_op jit(solution)/shard_map/all_to_all | solution.py:179
  22.9 1.1 copy-start.6
  24.0 4.4 %copy-start.7 = (s32[64,32]{0,1:T(8,128)S(1)}, s32[64,32]{0,1:T(8,128)}, u32[]{:S(2)}) copy-start(s32[64,32]{0,1:T(8,128)} %param.13) | copy-start | bytes 24580
  24.0 4.4 %copy-start.8 = (s32[64,32]{0,1:T(8,128)S(1)}, s32[64,32]{0,1:T(8,128)}, u32[]{:S(2)}) copy-start(s32[64,32]{0,1:T(8,128)} %param.14) | copy-start | bytes 24580
  24.0 20.4 %all-to-all-start = ((bf16[8,128,512]{2,1,0:T(8,128)(2,1)}), bf16[8,128,512]{2,1,0:T(8,128)(2,1)S(1)}, u32[]{:S(2)}, u32[]{:S(2)}) async-start(bf16[8,128,512]{2,1,0:T(8,128)(2,1)} %broadcast_in_dim.39), calls=%async_computation | async-start | bytes 2097152 | tf_op jit(solution)/shard_map/all_to_all | solution.py:183
  28.6 0.8 copy-start.10
  28.7 0.7 copy-start.9
  44.4 1.0 copy-start.1
  45.4 6.5 %copy-start.4 = (s32[128,512]{1,0:T(8,128)S(1)}, s32[128,512]{1,0:T(8,128)}, u32[]{:S(2)}) copy-start(s32[128,512]{1,0:T(8,128)} %param.9) | copy-start | bytes 786436
  52.8 1.0 copy-start.5
  84.9 16.5 %all-to-all-start.3 = ((f32[32,16,128]{2,1,0:T(8,128)}), f32[32,16,128]{2,1,0:T(8,128)S(1)}, u32[]{:S(2)}, u32[]{:S(2)}) async-start(f32[32,16,128]{2,1,0:T(8,128)} %shard_map.85), calls=%async_computation.3 | async-start | bytes 524288 | tf_op jit(solution)/shard_map/all_to_all | solution.py:179
  89.8 1.0 copy-start.3
  102.5 19.4 %all-to-all-start.4 = ((bf16[8,128,512]{2,1,0:T(8,128)(2,1)}), bf16[8,128,512]{2,1,0:T(8,128)(2,1)S(1)}, u32[]{:S(2)}, u32[]{:S(2)}) async-start(bf16[8,128,512]{2,1,0:T(8,128)(2,1)} %broadcast_in_dim.41), calls=%async_computation.4 | async-start | bytes 2097152 | tf_op jit(solution)/shard_map/all_to_all | solution.py:183
  121.9 1.0 copy-start.2
